TPU v7x, 32 devices: a whole 2x2x4 slice. The times are simulated.
32 devices in a mesh: blk: 4 (over y, x), group: 8 (over z, core).
Axes of the slice: x: 2, y: 2, z: 4, core: 2. Of those that a mesh axis runs over, the one named last changes fastest.
Arguments:
- picture_vector_list: bfloat16 [8, 1024, 768], P('group', 'blk'), may hold values from -0.25 to 0.25
- caption_latent_matrix: bfloat16 [8, 1024, 3072], P('group', 'blk'), may hold values from -6 to 6
- linear_map_matrix: bfloat16 [3072, 768], P('group'), may hold values from -0.109375 to 0.109375
- target_match_index: int32 [8, 1024], P('group', 'blk'), may hold values from 0 to 1023, each once within a row
- sharpness_factor: float32 [1], replicated, may hold values from 24 to 40
- offset_term: float32 [1], replicated, may hold values from -6 to -5
Outputs:
- row_loss: float32 [8, 1024], P('group', 'blk')
- image_grad: bfloat16 [8, 1024, 768], P('group', 'blk')
- projection_grad: float32 [3072, 768], P(('blk', 'group'))
Inputs may be any that keep to these rules, and one draw needn't show every extreme that they name: `target_match_index`: each data group's row of positives is a permutation of 0 to 1023.
All inputs are finite; a program needn't handle non-finite values.
Results may differ from a plain program's by a relative error of at most 0.015.
Values may be sent and summed in bfloat16 or wider, within the bound.
No kernel may reach another device: no remote copies, remote signals or barrier semaphores. Data moves between devices by JAX's collectives and lax.ppermute only.
A program may use at most 64 MiB of HBM per device.

v0:
```python
import jax
import jax.numpy as jnp
from jax import lax
from jax.sharding import PartitionSpec as P

epsilon = 1e-06


def passed_along(value, axis, steps):
    count = lax.axis_size(axis)
    pairs = [(source, (source + steps) % count) for source in range(count)]
    return lax.ppermute(value, axis, pairs)


def body(
    picture_vector_list,
    caption_latent_matrix,
    linear_map_matrix,
    target_match_index,
    sharpness_factor,
    offset_term,
):
    image_rows = picture_vector_list[0]
    hidden_rows = caption_latent_matrix[0]
    label_rows = target_match_index[0]
    row_count = image_rows.shape[0]
    feature_dim = image_rows.shape[1]
    blocks = lax.axis_size("blk")
    my_index = lax.axis_index("blk")
    multiplier_amount = sharpness_factor[0]
    offset_value = offset_term[0]
    columns = hidden_rows
    projected = jnp.dot(
        columns,
        lax.all_gather(linear_map_matrix, "group", axis=0, tiled=True),
        preferred_element_type=jnp.float32,
    )
    text_scale = lax.rsqrt(jnp.sum(projected * projected, axis=1, keepdims=True) + epsilon)
    text_dir = projected * text_scale
    text_unit = text_dir.astype(jnp.bfloat16)
    image_float = image_rows.astype(jnp.float32)
    image_scale = lax.rsqrt(jnp.sum(image_float * image_float, axis=1, keepdims=True) + epsilon)
    image_dir = image_float * image_scale
    image_unit = image_dir.astype(jnp.bfloat16)

    def signed_logits(image_tile_rows, label_block, text_block, column_start):
        columns = column_start + jnp.arange(text_block.shape[0], dtype=jnp.int32)
        pair_sign = jnp.where(label_block[:, None] == columns[None, :], 1.0, -1.0).astype(
            jnp.float32
        )
        pair_scores = lax.dot_general(
            image_tile_rows,
            text_block,
            (((1,), (1,)), ((), ())),
            preferred_element_type=jnp.float32,
        )
        return (multiplier_amount * pair_scores + offset_value, pair_sign)

    def weights_of(logits, pair_sign):
        return (-pair_sign * jax.nn.sigmoid(-pair_sign * logits) * multiplier_amount).astype(
            jnp.bfloat16
        )

    image_unit_grad = jnp.zeros((row_count, feature_dim), jnp.float32)
    loss_local = jnp.zeros((row_count,), jnp.float32)
    text_block = text_unit
    for step_index in range(blocks):
        source = (my_index - step_index) % blocks
        logits, pair_sign = signed_logits(image_unit, label_rows, text_block, source * row_count)
        loss_local = loss_local + -jnp.sum(jax.nn.log_sigmoid(pair_sign * logits), axis=1)
        pair_weight = weights_of(logits, pair_sign)
        image_unit_grad = image_unit_grad + jnp.dot(
            pair_weight, text_block, preferred_element_type=jnp.float32
        )
        if step_index + 1 < blocks:
            text_block = passed_along(text_block, "blk", 1)
    own_start = my_index * row_count
    image_piece = lax.all_gather(image_unit, "blk", axis=0, tiled=True)
    label_piece = lax.all_gather(label_rows, "blk", axis=0, tiled=True)
    logits, pair_sign = signed_logits(image_piece, label_piece, text_unit, own_start)
    pair_weight = weights_of(logits, pair_sign)
    text_unit_grad = lax.dot_general(
        pair_weight, image_piece, (((0,), (0,)), ((), ())), preferred_element_type=jnp.float32
    )
    image_grad = (
        image_scale
        * (
            image_unit_grad
            - image_dir * jnp.sum(image_dir * image_unit_grad, axis=1, keepdims=True)
        )
    ).astype(jnp.bfloat16)
    projection_output_gradient = (
        text_scale
        * (text_unit_grad - text_dir * jnp.sum(text_dir * text_unit_grad, axis=1, keepdims=True))
    ).astype(jnp.bfloat16)
    columns = hidden_rows
    projection_grad = lax.psum_scatter(
        lax.dot_general(
            columns,
            projection_output_gradient,
            (((0,), (0,)), ((), ())),
            preferred_element_type=jnp.float32,
        ),
        ("blk", "group"),
        scatter_dimension=0,
        tiled=True,
    )
    return (loss_local[None], image_grad[None], projection_grad)


def solution(mesh):
    return jax.shard_map(
        body,
        mesh=mesh,
        in_specs=(
            P("group", "blk", None),
            P("group", "blk", None),
            P("group", None),
            P("group", "blk"),
            P(),
            P(),
        ),
        out_specs=(P("group", "blk"), P("group", "blk", None), P(("blk", "group"), None)),
        check_vma=False,
    )
```

profile of v0, /device:TPU:0, one launch (start us, length us, event | category | flops | bytes accessed | tf_op | source)
XLA Modules:
  0.0 257.5 jit_solution(9647050227928517033)
XLA Ops:
  7.2 0.0 copy-start
  7.2 0.0 copy-start.3
  7.2 0.0 all-gather.4.cloned.1.call-start
  7.2 0.7 all-gather.4.cloned.1.call-update
  7.9 0.0 all-gather.6.cloned.1.call-start
  8.0 1.2 fusion.27
  9.1 1.9 fusion.22
  11.0 0.0 all-gather.6.cloned.1.call-update
  11.0 0.0 reduce-scatter.4.cloned.1.call-start
  12.4 0.0 copy-done.3
  12.4 10.1 %all-gather = s32[1,1024]{1,0:T(1,128)} all-gather(s32[1,256]{1,0:T(1,128)S(1)} %copy-done.3), channel_id=2, replica_groups=mesh['blk'=4,'group'=8] {'blk'}, dimensions={1}, use_global_device_ids=true | all-gather | bytes 5120 | tf_op jit(solution)/shard_map/all_gather | solution.py:79
  22.5 0.6 iota_add_fusion
  23.0 41.1 %all-gather.4.cloned.1.call-done = bf16[3072,768]{1,0:T(8,128)(2,1)} async-done(((bf16[384,768]{1,0:T(8,128)(2,1)}), bf16[3072,768]{1,0:T(8,128)(2,1)}) %all-gather.4.cloned.1.call-update) | async-done | bytes 4718608 | tf_op jit(solution)/shard_map/all_gather | solution.py:35
  64.1 0.0 copy-done
  64.1 3.8 %multiply_reduce_fusion.1 = (f32[256]{0:T(256)S(1)}, f32[256,768]{1,0:T(8,128)S(1)}) fusion(bf16[3072,768]{1,0:T(8,128)(2,1)} %all-gather.4.cloned.1.call-done, bf16[1,256,3072]{2,1,0:T(8,128)(2,1)S(1)} %copy-done), kind=kOutput, calls=%fused_computation.41 | convolution fusion | flops 1208352512 | bytes 7078912 | tf_op jit(solution)/shard_map/dot_general | solution.py:33
  67.9 0.1 multiply_convert_fusion.1
  68.0 28.3 %all-gather.6.cloned.1.call-done = bf16[1024,768]{1,0:T(8,128)(2,1)} async-done(((bf16[256,768]{1,0:T(8,128)(2,1)}), bf16[1024,768]{1,0:T(8,128)(2,1)}) %all-gather.6.cloned.1.call-update) | async-done | bytes 1572880 | tf_op jit(solution)/shard_map/all_gather | solution.py:78
  96.3 3.9 %multiply_reduce_fusion = (f32[256]{0:T(256)S(1)}, f32[256,768]{1,0:T(8,128)S(1)}) fusion(f32[256,768]{1,0:T(8,128)S(1)} %get-tuple-element.14, f32[256]{0:T(256)S(1)} %add_rsqrt_fusion, bf16[1024,768]{1,0:T(8,128)(2,1)} %all-gather.6.cloned.1.call-done, bf16[256,768]{1,0:T(8,128)(2,1)S(1)} %multiply_convert_fusion.1, f32[]{:T(128)} %bitcast.49, ...), kind=kOutput, calls=%fused_computation.40 | convolution fusion | flops 809041664 | bytes 3546120 | tf_op jit(solution)/shard_map/dot_general | solution.py:82
  100.2 5.3 %convolution_bitcast_fusion = f32[3072,768]{0,1:T(8,128)} fusion(bf16[1,256,3072]{2,1,0:T(8,128)(2,1)S(1)} %copy-done, f32[256,768]{1,0:T(8,128)S(1)} %get-tuple-element.19, f32[256,768]{1,0:T(8,128)S(1)} %get-tuple-element.14, f32[256]{0:T(256)S(1)} %get-tuple-element.18, f32[256]{0:T(256)S(1)} %add_rsqrt_fusion), kind=kOutput, calls=%fused_computation | convolution fusion | flops 1208942592 | bytes 12584960 | tf_op jit(solution)/shard_map/dot_general | solution.py:98
  105.5 9.6 %copy.11 = f32[3072,768]{1,0:T(8,128)} copy(f32[3072,768]{0,1:T(8,128)} %convolution_bitcast_fusion) | data formatting | bytes 18874368
  115.1 0.0 copy-start.1
  115.1 0.0 reduce-scatter.4.cloned.1.call-update
  115.2 1.5 collective-permute-start
  116.7 10.3 %collective-permute-done = bf16[256,768]{1,0:T(8,128)(2,1)S(1)} collective-permute-done((bf16[256,768]{1,0:T(8,128)(2,1)S(1)}, bf16[256,768]{1,0:T(8,128)(2,1)S(1)}, u32[]{:S(2)}, u32[]{:S(2)}) %collective-permute-start) | collective-permute-done | bytes 393248 | tf_op jit(solution)/shard_map/ppermute | solution.py:12
  127.0 0.6 collective-permute-start.1
  127.5 0.0 copy-done.1
  127.5 0.3 fusion.12
  127.8 10.0 %collective-permute-done.1 = bf16[256,768]{1,0:T(8,128)(2,1)S(1)} collective-permute-done((bf16[256,768]{1,0:T(8,128)(2,1)S(1)}, bf16[256,768]{1,0:T(8,128)(2,1)S(1)}, u32[]{:S(2)}, u32[]{:S(2)}) %collective-permute-start.1) | collective-permute-done | bytes 393248 | tf_op jit(solution)/shard_map/ppermute | solution.py:12
  137.8 0.0 collective-permute-start.2
  137.8 0.4 fusion.77
  138.3 0.3 fusion.14
  138.6 9.2 %collective-permute-done.2 = bf16[256,768]{1,0:T(8,128)(2,1)S(1)} collective-permute-done((bf16[256,768]{1,0:T(8,128)(2,1)S(1)}, bf16[256,768]{1,0:T(8,128)(2,1)S(1)}, u32[]{:S(2)}, u32[]{:S(2)}) %collective-permute-start.2) | collective-permute-done | bytes 393248 | tf_op jit(solution)/shard_map/ppermute | solution.py:12
  147.8 0.3 fusion.15
  148.1 0.9 fusion.70
  149.0 0.6 add_add_fusion
  149.6 0.4 convolution_add_fusion.2
  150.0 0.0 copy-start.2
  150.0 0.4 convolution_add_fusion.1
  150.5 0.5 copy-done.2
  151.0 0.5 fusion.23
  151.6 1.0 fusion.34
  152.5 98.5 %reduce-scatter.4.cloned.1.call-done = f32[96,768]{1,0:T(8,128)} async-done(((f32[3072,768]{1,0:T(8,128)}), f32[96,768]{1,0:T(8,128)}) %reduce-scatter.4.cloned.1.call-update) | async-done | bytes 294928
  (4 shorter events, 0.0 us)
Async XLA Ops:
  7.2 56.9 %copy-start = (bf16[1,256,3072]{2,1,0:T(8,128)(2,1)S(1)}, bf16[1,256,3072]{2,1,0:T(8,128)(2,1)}, u32[]{:S(2)}) copy-start(bf16[1,256,3072]{2,1,0:T(8,128)(2,1)} %param.7) | copy-start | bytes 4718596
  7.2 5.2 %copy-start.3 = (s32[1,256]{1,0:T(1,128)S(1)}, s32[1,256]{1,0:T(1,128)}, u32[]{:S(2)}) copy-start(s32[1,256]{1,0:T(1,128)} %param.9) | copy-start | bytes 3076
  7.2 56.9 %all-gather.4.cloned.1.call-start = ((), (), s32[]{:S(2)}) async-start(), calls=%async_computation.1 | async-start | bytes 5308416 | tf_op jit(solution)/shard_map/all_gather | solution.py:35
  7.9 88.4 %all-gather.6.cloned.1.call-start = ((), (), s32[]{:S(2)}) async-start(), calls=%async_computation.2 | async-start | bytes 1966080 | tf_op jit(solution)/shard_map/all_gather | solution.py:78
  11.0 240.0 %reduce-scatter.4.cloned.1.call-start = ((), (), s32[]{:S(2)}) async-start(), calls=%async_computation.3 | async-start | bytes 9732096
  115.1 12.4 %copy-start.1 = (bf16[256,768]{1,0:T(8,128)(2,1)S(1)}, bf16[256,768]{1,0:T(8,128)(2,1)}, u32[]{:S(2)}) copy-start(bf16[256,768]{1,0:T(8,128)(2,1)} %fusion.22) | copy-start | bytes 1179652
  115.2 11.8 %collective-permute-start = (bf16[256,768]{1,0:T(8,128)(2,1)S(1)}, bf16[256,768]{1,0:T(8,128)(2,1)S(1)}, u32[]{:S(2)}, u32[]{:S(2)}) collective-permute-start(bf16[256,768]{1,0:T(8,128)(2,1)S(1)} %multiply_convert_fusion.1), channel_id=1, source_target_pairs={{0,8},{8,16},{16,24},{24,0},{1,9},{9,17},{17,25},{25,1},{2,10},{10... | collective-permute-start | bytes 1179656 | tf_op jit(solution)/shard_map/ppermute | solution.py:12
  127.0 10.9 %collective-permute-start.1 = (bf16[256,768]{1,0:T(8,128)(2,1)S(1)}, bf16[256,768]{1,0:T(8,128)(2,1)S(1)}, u32[]{:S(2)}, u32[]{:S(2)}) collective-permute-start(bf16[256,768]{1,0:T(8,128)(2,1)S(1)} %collective-permute-done), channel_id=1, source_target_pairs={{0,8},{8,16},{16,24},{24,0},{1,9},{9,17},{17,25},{25,1},{2,10},{10... | collective-permute-start | bytes 1179656 | tf_op jit(solution)/shard_map/ppermute | solution.py:12
  137.8 10.0 %collective-permute-start.2 = (bf16[256,768]{1,0:T(8,128)(2,1)S(1)}, bf16[256,768]{1,0:T(8,128)(2,1)S(1)}, u32[]{:S(2)}, u32[]{:S(2)}) collective-permute-start(bf16[256,768]{1,0:T(8,128)(2,1)S(1)} %collective-permute-done.1), channel_id=1, source_target_pairs={{0,8},{8,16},{16,24},{24,0},{1,9},{9,17},{17,25},{25,1},{2,10},{10... | collective-permute-start | bytes 1179656 | tf_op jit(solution)/shard_map/ppermute | solution.py:12
  150.0 1.0 copy-start.2
Sparse Core Ops, SparseCore 0:
  9.7 54.3 all-gather.3
  66.5 29.7 all-gather.5
  115.3 135.6 reduce-scatter.3
where the time goes:
time: 258 us
  waiting for transfers between devices  198 us (77%)
  matrix products  16.6 us (6%)
  between operations  15.1 us (6%)
  local copies, waits for them, and re-layouts  10.2 us (4%)
  blocking collectives  10.1 us (4%)
  other arithmetic  5.28 us (2%)
    unnamed x4, waiting for transfers between devices  99.2 us
    all_gather x1, waiting for transfers between devices, body(): lax.all_gather(linear_map_matrix, 'group', axis=0, tiled=True)  41.1 us
    ppermute x3, waiting for transfers between devices, passed_along(): return lax.ppermute(value, axis, pairs)  29.5 us
    all_gather x1, waiting for transfers between devices, body(): image_piece = lax.all_gather(image_unit, 'blk', axis=0, tiled=True)  28.3 us
    unnamed x9, local copies, waits for them, and re-layouts  10.2 us
    all_gather x1, blocking collectives, body(): label_piece = lax.all_gather(label_rows, 'blk', axis=0, tiled=True)  10.1 us
    dot_general x1, matrix products, body(): lax.dot_general(columns, projection_output_gradient, (((0,), (0,)), ((),...  5.27 us
  transfers between devices with their start and end apart: 6, of which 6 were waited for; matrix products, arithmetic and copies ran while one was open for 5% of the time, Pallas kernels for 0%

commit v1 on v0

v1 whole, which is shorter than its diff:
```python
import jax
import jax.numpy as jnp
from jax import lax
from jax.sharding import PartitionSpec as P

epsilon = 1e-06


def body(
    picture_vector_list,
    caption_latent_matrix,
    linear_map_matrix,
    target_match_index,
    sharpness_factor,
    offset_term,
):
    image_rows = picture_vector_list[0]
    hidden_rows = caption_latent_matrix[0]
    label_rows = target_match_index[0]
    row_count = image_rows.shape[0]
    blocks = lax.axis_size("blk")
    my_index = lax.axis_index("blk")
    multiplier_amount = sharpness_factor[0]
    offset_value = offset_term[0]

    piece_rows = linear_map_matrix.shape[0] // blocks
    w_piece = lax.dynamic_slice_in_dim(linear_map_matrix, my_index * piece_rows, piece_rows, 0)
    w_full = lax.all_gather(w_piece, ("group", "blk"), axis=0, tiled=True)

    hidden_chunk = lax.all_to_all(hidden_rows, "blk", split_axis=1, concat_axis=0, tiled=True)

    image_float = image_rows.astype(jnp.float32)
    image_scale = lax.rsqrt(jnp.sum(image_float * image_float, axis=1, keepdims=True) + epsilon)
    image_dir = image_float * image_scale
    image_unit = image_dir.astype(jnp.bfloat16)

    projected = jnp.dot(hidden_rows, w_full, preferred_element_type=jnp.float32)
    text_scale = lax.rsqrt(jnp.sum(projected * projected, axis=1, keepdims=True) + epsilon)
    text_dir = projected * text_scale
    text_unit = text_dir.astype(jnp.bfloat16)

    both = lax.all_gather(jnp.stack([image_unit, text_unit]), "blk", axis=1, tiled=True)
    image_all = both[0]
    text_all = both[1]
    label_all = lax.all_gather(label_rows.astype(jnp.float32), "blk", axis=0, tiled=True)

    def weights_of(logits, pair_sign):
        return (-pair_sign * jax.nn.sigmoid(-pair_sign * logits) * multiplier_amount).astype(
            jnp.bfloat16
        )

    scores = lax.dot_general(
        image_unit, text_all, (((1,), (1,)), ((), ())), preferred_element_type=jnp.float32
    )
    logits = multiplier_amount * scores + offset_value
    text_columns = jnp.arange(text_all.shape[0], dtype=jnp.int32)
    pair_sign = jnp.where(label_rows[:, None] == text_columns[None, :], 1.0, -1.0).astype(
        jnp.float32
    )
    loss_local = -jnp.sum(jax.nn.log_sigmoid(pair_sign * logits), axis=1)
    image_unit_grad = jnp.dot(
        weights_of(logits, pair_sign), text_all, preferred_element_type=jnp.float32
    )

    scores_t = lax.dot_general(
        image_all, text_unit, (((1,), (1,)), ((), ())), preferred_element_type=jnp.float32
    )
    logits_t = multiplier_amount * scores_t + offset_value
    own_columns = (my_index * row_count + jnp.arange(row_count, dtype=jnp.int32)).astype(
        jnp.float32
    )
    pair_sign_t = jnp.where(label_all[:, None] == own_columns[None, :], 1.0, -1.0).astype(
        jnp.float32
    )
    text_unit_grad = lax.dot_general(
        weights_of(logits_t, pair_sign_t),
        image_all,
        (((0,), (0,)), ((), ())),
        preferred_element_type=jnp.float32,
    )

    image_grad = (
        image_scale
        * (
            image_unit_grad
            - image_dir * jnp.sum(image_dir * image_unit_grad, axis=1, keepdims=True)
        )
    ).astype(jnp.bfloat16)
    projection_output_gradient = (
        text_scale
        * (text_unit_grad - text_dir * jnp.sum(text_dir * text_unit_grad, axis=1, keepdims=True))
    ).astype(jnp.bfloat16)

    grad_all = lax.all_gather(projection_output_gradient, "blk", axis=0, tiled=True)
    partial = lax.dot_general(
        hidden_chunk, grad_all, (((0,), (0,)), ((), ())), preferred_element_type=jnp.float32
    )
    projection_grad = lax.psum_scatter(partial, "group", scatter_dimension=0, tiled=True)
    return (loss_local[None], image_grad[None], projection_grad)


def solution(mesh):
    return jax.shard_map(
        body,
        mesh=mesh,
        in_specs=(
            P("group", "blk", None),
            P("group", "blk", None),
            P("group", None),
            P("group", "blk"),
            P(),
            P(),
        ),
        out_specs=(P("group", "blk"), P("group", "blk", None), P(("blk", "group"), None)),
        check_vma=False,
    )
```

time: 258 us -> 221 us (0.86)
  waiting for transfers between devices: 198 us -> 139 us
  blocking collectives: 10.1 us -> 35.8 us
    unnamed x4 -> x5, waiting for transfers between devices: 99.2 us -> 30 us
    all_gather x2 -> x3, waiting for transfers between devices: 69.4 us -> 109 us  [the longest x1 66.6 us: body(): w_full = lax.all_gather(w_piece, ('group', 'blk'), axis=0, tiled=True)]
    ppermute x3 -> x0, waiting for transfers between devices: 29.5 us -> none  [passed_along(): return lax.ppermute(value, axis, pairs)]
    all_to_all x0 -> x1, blocking collectives: none -> 27.8 us  [body(): lax.all_to_all(hidden_rows, 'blk', split_axis=1, concat_axis=0, tiled=True)]
    unnamed x9 -> x16, local copies, waits for them, and re-layouts: 10.2 us -> 7.66 us
    dot_general x11 -> x5, matrix products: 16.6 us -> 16.1 us  [the longest x1 4.64 us: body(): lax.dot_general(weights_of(logits_t, pair_sign_t), image_all, (((0,), (0,...]
  transfers between devices with their start and end apart: 6 -> 4, of which waited for: 6 -> 4; matrix products, arithmetic and copies ran while one was open for 5% -> 5% of each run, Pallas kernels for 0% -> 0%
where the time goes in v1:
time: 221 us; the launch traced here: 220 us
  waiting for transfers between devices  139 us (63%)
  blocking collectives  35.8 us (16%)
  matrix products  16.1 us (7%)
  between operations  15.2 us (7%)
  local copies, waits for them, and re-layouts  9.92 us (4%)
  other arithmetic  4.17 us (2%)
    all_gather x1, waiting for transfers between devices, body(): w_full = lax.all_gather(w_piece, ('group', 'blk'), axis=0, tiled=True)  66.6 us
    all_gather x1, waiting for transfers between devices, body(): lax.all_gather(jnp.stack([image_unit, text_unit]), 'blk', axis=1, tiled=T...  33.4 us
    unnamed x5, waiting for transfers between devices  30 us
    all_to_all x1, blocking collectives, body(): lax.all_to_all(hidden_rows, 'blk', split_axis=1, concat_axis=0, tiled=True)  27.8 us
    all_gather x1, waiting for transfers between devices, body(): lax.all_gather(projection_output_gradient, 'blk', axis=0, tiled=True)  9.09 us
    all_gather x1, blocking collectives, body(): lax.all_gather(label_rows.astype(jnp.float32), 'blk', axis=0, tiled=True)  8.03 us
    unnamed x16, local copies, waits for them, and re-layouts  7.66 us
    dot_general x1, matrix products, body(): lax.dot_general(weights_of(logits_t, pair_sign_t), image_all, (((0,), (0,...  4.64 us
  transfers between devices with their start and end apart: 4, of which 4 were waited for; matrix products, arithmetic and copies ran while one was open for 5% of the time, Pallas kernels for 0%

profile of v1, /device:TPU:0, one launch (start us, length us, event | category | flops | bytes accessed | tf_op | source)
XLA Modules:
  0.0 220.5 jit_solution(2753661675826970912)
XLA Ops:
  7.2 0.0 copy-start
  7.2 0.0 copy-start.1
  7.2 0.0 all-gather.5.cloned.1.call-start
  7.2 1.0 copy-done
  8.2 0.7 constant_dynamic-slice_fusion
  8.9 0.0 all-gather.5.cloned.1.call-update
  8.9 0.0 all-gather.7.cloned.1.call-start
  9.0 1.2 copy.32
  10.2 0.1 fusion.37
  10.3 0.8 fusion.38
  11.1 66.6 %all-gather.5.cloned.1.call-done = bf16[3072,768]{1,0:T(8,128)(2,1)} async-done(((bf16[96,768]{1,0:T(8,128)(2,1)}), bf16[3072,768]{1,0:T(8,128)(2,1)}) %all-gather.5.cloned.1.call-update) | async-done | bytes 4718608 | tf_op jit(solution)/shard_map/all_gather | solution.py:28
  77.8 0.0 copy-done.1
  77.8 0.0 copy-start.2
  77.8 3.8 %multiply_reduce_fusion = (f32[256]{0:T(256)S(1)}, f32[768,256]{1,0:T(8,128)S(1)}) fusion(bf16[3072,768]{1,0:T(8,128)(2,1)} %all-gather.5.cloned.1.call-done, bf16[1,256,3072]{2,1,0:T(8,128)(2,1)S(1)} %copy-done.1), kind=kOutput, calls=%fused_computation.57 | convolution fusion | flops 1208352512 | bytes 7078912 | tf_op jit(solution)/shard_map/dot_general | solution.py:37
  81.6 0.0 copy-start.4
  81.6 0.1 fusion.55
  81.7 0.0 copy-done.2
  81.7 0.9 pad_maximum_fusion
  82.7 0.0 all-gather.7.cloned.1.call-update
  82.7 0.0 all-gather.9.cloned.1.call-start
  84.0 0.0 copy-done.4
  84.1 8.0 %all-gather = f32[4,1,256]{2,1,0:T(1,128)S(1)} all-gather(f32[1,1,256]{2,1,0:T(1,128)S(1)} %bitcast.120), channel_id=1, replica_groups=mesh['blk'=4,'group'=8] {'blk'}, dimensions={0}, use_global_device_ids=true | all-gather | bytes 5120 | tf_op jit(solution)/shard_map/all_gather | solution.py:45
  92.1 33.4 %all-gather.7.cloned.1.call-done = bf16[2,1024,768]{1,2,0:T(8,128)(2,1)} async-done(((bf16[2,256,768]{1,2,0:T(8,128)(2,1)}), bf16[2,1024,768]{1,2,0:T(8,128)(2,1)}) %all-gather.7.cloned.1.call-update) | async-done | bytes 3145744 | tf_op jit(solution)/shard_map/all_gather | solution.py:42
  125.5 4.6 %fusion.39 = (f32[256]{0:T(256)S(1)}, f32[256,768]{0,1:T(8,128)}) fusion(f32[768,256]{1,0:T(8,128)S(1)} %get-tuple-element.16, f32[256]{0:T(256)S(1)} %add_rsqrt_fusion, bf16[2,1024,768]{1,2,0:T(8,128)(2,1)} %all-gather.7.cloned.1.call-done, f32[]{:T(128)} %bitcast.115, f32[]{:T(128)} %bitcast.112, f32[256]{0:T(256)S(1)} %add_convert_fusion, ...), kind=kOutput, calls=%fused_computation.53 | convolution fusion | flops 809434880 | bytes 5513224 | tf_op jit(solution)/shard_map/dot_general | solution.py:75
  130.1 2.0 fusion.42
  132.1 0.0 all-gather.9.cloned.1.call-update
  132.2 0.0 reduce-scatter.4.cloned.1.call-start
  132.2 1.6 copy.37
  133.8 27.8 %all_to_all.19 = bf16[256,4,768]{0,2,1:T(8,128)(2,1)S(1)} all-to-all(bf16[256,4,768]{0,2,1:T(8,128)(2,1)} %bitcast.117), channel_id=1, replica_groups=mesh['blk'=4,'group'=8] {'blk'}, dimensions={1} | all-to-all | bytes 3145728 | tf_op jit(solution)/shard_map/all_to_all | solution.py:30
  161.6 1.6 copy.38
  163.2 9.1 %all-gather.9.cloned.1.call-done = bf16[1024,768]{0,1:T(8,128)(2,1)} async-done(((bf16[256,768]{0,1:T(8,128)(2,1)}), bf16[1024,768]{0,1:T(8,128)(2,1)}) %all-gather.9.cloned.1.call-update) | async-done | bytes 1572880 | tf_op jit(solution)/shard_map/all_gather | solution.py:94
  172.3 3.3 %convolution_bitcast_fusion = f32[768,768]{0,1:T(8,128)S(1)} fusion(bf16[1024,768]{0,1:T(8,128)(2,1)} %all-gather.9.cloned.1.call-done, bf16[1024,768]{1,0:T(8,128)(2,1)} %bitcast.118), kind=kOutput, calls=%fused_computation.1 | convolution fusion | flops 1207959552 | bytes 5505024 | tf_op jit(solution)/shard_map/dot_general | solution.py:95
  175.5 2.0 copy.43
  177.5 0.0 copy-start.3
  177.5 0.0 reduce-scatter.4.cloned.1.call-update
  177.6 1.0 copy-done.3
  178.5 0.0 copy-start.5
  178.5 3.5 %fusion.25 = (f32[256]{0:T(256)}, f32[256,1024]{1,0:T(8,128)S(1)}) fusion(s32[256]{0:T(256)S(1)} %bitcast.122, f32[]{:T(128)} %bitcast.114, bf16[2,1024,768]{1,2,0:T(8,128)(2,1)} %all-gather.7.cloned.1.call-done, bf16[1,256,768]{1,2,0:T(8,128)(2,1)S(1)} %copy-done.3, f32[]{:T(128)} %bitcast.111), kind=kOutput, calls=%fused_computation.31 | convolution fusion | flops 406060800 | bytes 3017728 | tf_op jit(solution)/shard_map/dot_general | solution.py:52
  182.0 0.0 copy-done.5
  182.0 1.0 fusion.33
  182.9 0.2 fusion.53
  183.1 0.9 copy.39
  184.0 29.9 %reduce-scatter.4.cloned.1.call-done = f32[96,768]{1,0:T(8,128)} async-done(((f32[768,768]{1,0:T(8,128)}), f32[96,768]{1,0:T(8,128)}) %reduce-scatter.4.cloned.1.call-update) | async-done | bytes 294928
  (4 shorter events, 0.0 us)
Async XLA Ops:
  7.2 1.1 copy-start
  7.2 70.6 %copy-start.1 = (bf16[1,256,3072]{2,1,0:T(8,128)(2,1)S(1)}, bf16[1,256,3072]{2,1,0:T(8,128)(2,1)}, u32[]{:S(2)}) copy-start(bf16[1,256,3072]{2,1,0:T(8,128)(2,1)} %param.7) | copy-start | bytes 4718596
  7.2 70.6 %all-gather.5.cloned.1.call-start = ((), (), s32[]{:S(2)}) async-start(), calls=%async_computation.2 | async-start | bytes 4866048 | tf_op jit(solution)/shard_map/all_gather | solution.py:28
  8.9 116.6 %all-gather.7.cloned.1.call-start = ((), (), s32[]{:S(2)}) async-start(), calls=%async_computation.3 | async-start | bytes 3932160 | tf_op jit(solution)/shard_map/all_gather | solution.py:42
  77.8 3.9 %copy-start.2 = (bf16[1,256,768]{1,2,0:T(8,128)(2,1)S(1)}, bf16[1,256,768]{1,2,0:T(8,128)(2,1)}, u32[]{:S(2)}) copy-start(bf16[1,256,768]{1,2,0:T(8,128)(2,1)} %fusion.38) | copy-start | bytes 1179652
  81.6 2.4 %copy-start.4 = (s32[1,256]{1,0:T(1,128)S(1)}, s32[1,256]{1,0:T(1,128)}, u32[]{:S(2)}) copy-start(s32[1,256]{1,0:T(1,128)} %param.9) | copy-start | bytes 3076
  82.7 89.6 %all-gather.9.cloned.1.call-start = ((), (), s32[]{:S(2)}) async-start(), calls=%async_computation.4 | async-start | bytes 1966080 | tf_op jit(solution)/shard_map/all_gather | solution.py:94
  132.2 81.8 %reduce-scatter.4.cloned.1.call-start = ((), (), s32[]{:S(2)}) async-start(), calls=%async_computation.5 | async-start | bytes 2654208
  177.5 1.0 copy-start.3
  178.5 3.5 %copy-start.5 = (bf16[2,1024,768]{1,2,0:T(8,128)(2,1)S(1)}, bf16[2,1024,768]{1,2,0:T(8,128)(2,1)}, u32[]{:S(2)}) copy-start(bf16[2,1024,768]{1,2,0:T(8,128)(2,1)} %all-gather.7.cloned.1.call-done) | copy-start | bytes 9437188
Sparse Core Ops, SparseCore 0:
  11.5 66.2 all-gather.4
  82.8 42.6 all-gather.6
  132.3 39.9 all-gather.8
  177.7 36.2 reduce-scatter.3

commit v2 on v1

v2 whole, which is shorter than its diff:
```python
import jax
import jax.numpy as jnp
from jax import lax
from jax.sharding import PartitionSpec as P

epsilon = 1e-06


def partner_pairs(count, step):
    if count & (count - 1) == 0:
        return [(source, source ^ step) for source in range(count)]
    return [(source, (source + step) % count) for source in range(count)]


def partner_of(index, count, step):
    if count & (count - 1) == 0:
        return index ^ step
    return (index - step) % count


def body(
    picture_vector_list,
    caption_latent_matrix,
    linear_map_matrix,
    target_match_index,
    sharpness_factor,
    offset_term,
):
    image_rows = picture_vector_list[0]
    hidden_rows = caption_latent_matrix[0]
    label_rows = target_match_index[0]
    row_count = image_rows.shape[0]
    hid = hidden_rows.shape[1]
    blocks = lax.axis_size("blk")
    my_index = lax.axis_index("blk")
    chunk = hid // blocks
    multiplier_amount = sharpness_factor[0]
    offset_value = offset_term[0]

    def exchange(value, step):
        return lax.ppermute(value, "blk", partner_pairs(blocks, step))

    w_full = lax.all_gather(linear_map_matrix, "group", axis=0, tiled=True)

    image_float = image_rows.astype(jnp.float32)
    image_scale = lax.rsqrt(jnp.sum(image_float * image_float, axis=1, keepdims=True) + epsilon)
    image_dir = image_float * image_scale
    image_unit = image_dir.astype(jnp.bfloat16)

    source = [my_index] + [partner_of(my_index, blocks, k) for k in range(1, blocks)]
    own_hidden_chunk = lax.dynamic_slice_in_dim(hidden_rows, my_index * chunk, chunk, 1)
    hidden_from = [own_hidden_chunk]
    image_from = [image_unit]
    label_from = [label_rows]
    for k in range(1, blocks):
        target = partner_of(my_index, blocks, k)
        outgoing = jnp.concatenate(
            [lax.dynamic_slice_in_dim(hidden_rows, target * chunk, chunk, 1), image_unit], axis=1
        )
        incoming = exchange(outgoing, k)
        hidden_from.append(incoming[:, :chunk])
        image_from.append(incoming[:, chunk:])
        label_from.append(exchange(label_rows, k))

    projected = jnp.dot(hidden_rows, w_full, preferred_element_type=jnp.float32)
    text_scale = lax.rsqrt(jnp.sum(projected * projected, axis=1, keepdims=True) + epsilon)
    text_dir = projected * text_scale
    text_unit = text_dir.astype(jnp.bfloat16)
    text_from = [text_unit] + [exchange(text_unit, k) for k in range(1, blocks)]

    def weights_of(logits, pair_sign):
        return (-pair_sign * jax.nn.sigmoid(-pair_sign * logits) * multiplier_amount).astype(
            jnp.bfloat16
        )

    local = jnp.arange(row_count, dtype=jnp.int32)

    own_columns = my_index * row_count + local
    text_unit_grad = jnp.zeros(text_unit.shape, jnp.float32)
    for k in range(blocks):
        scores_t = lax.dot_general(
            image_from[k], text_unit, (((1,), (1,)), ((), ())), preferred_element_type=jnp.float32
        )
        logits_t = multiplier_amount * scores_t + offset_value
        pair_sign_t = jnp.where(label_from[k][:, None] == own_columns[None, :], 1.0, -1.0).astype(
            jnp.float32
        )
        text_unit_grad = text_unit_grad + lax.dot_general(
            weights_of(logits_t, pair_sign_t),
            image_from[k],
            (((0,), (0,)), ((), ())),
            preferred_element_type=jnp.float32,
        )
    projection_output_gradient = (
        text_scale
        * (text_unit_grad - text_dir * jnp.sum(text_dir * text_unit_grad, axis=1, keepdims=True))
    ).astype(jnp.bfloat16)
    grad_from = [projection_output_gradient] + [
        exchange(projection_output_gradient, k) for k in range(1, blocks)
    ]
    partial = jnp.zeros((chunk, projection_output_gradient.shape[1]), jnp.float32)
    for k in range(blocks):
        partial = partial + lax.dot_general(
            hidden_from[k], grad_from[k], (((0,), (0,)), ((), ())), preferred_element_type=jnp.float32
        )
    projection_grad = lax.psum_scatter(partial, "group", scatter_dimension=0, tiled=True)

    loss_local = jnp.zeros((row_count,), jnp.float32)
    image_unit_grad = jnp.zeros(image_unit.shape, jnp.float32)
    for k in range(blocks):
        scores = lax.dot_general(
            image_unit, text_from[k], (((1,), (1,)), ((), ())), preferred_element_type=jnp.float32
        )
        logits = multiplier_amount * scores + offset_value
        columns = source[k] * row_count + local
        pair_sign = jnp.where(label_rows[:, None] == columns[None, :], 1.0, -1.0).astype(
            jnp.float32
        )
        loss_local = loss_local + -jnp.sum(jax.nn.log_sigmoid(pair_sign * logits), axis=1)
        image_unit_grad = image_unit_grad + jnp.dot(
            weights_of(logits, pair_sign), text_from[k], preferred_element_type=jnp.float32
        )
    image_grad = (
        image_scale
        * (
            image_unit_grad
            - image_dir * jnp.sum(image_dir * image_unit_grad, axis=1, keepdims=True)
        )
    ).astype(jnp.bfloat16)
    return (loss_local[None], image_grad[None], projection_grad)


def solution(mesh):
    return jax.shard_map(
        body,
        mesh=mesh,
        in_specs=(
            P("group", "blk", None),
            P("group", "blk", None),
            P("group", None),
            P("group", "blk"),
            P(),
            P(),
        ),
        out_specs=(P("group", "blk"), P("group", "blk", None), P(("blk", "group"), None)),
        check_vma=False,
    )
```

time: 221 us -> 148 us (0.67)
  waiting for transfers between devices: 139 us -> 84.7 us
  blocking collectives: 35.8 us -> 0 us
  starting transfers between devices: 0.16 us -> 16.6 us
  local copies, waits for them, and re-layouts: 9.92 us -> 2.03 us
  matrix products: 16.1 us -> 23.9 us
    all_gather x3 -> x1, waiting for transfers between devices: 109 us -> 42.8 us  [body(): w_full = lax.all_gather(linear_map_matrix, 'group', axis=0, tiled=True)]
    unnamed x5 -> x2, waiting for transfers between devices: 30 us -> 0.7 us
    all_to_all x1 -> x0, blocking collectives: 27.8 us -> none  [body(): lax.all_to_all(hidden_rows, 'blk', split_axis=1, concat_axis=0, tiled=True)]
    ppermute x0 -> x12, waiting for transfers between devices: none -> 27.7 us  [exchange(): return lax.ppermute(value, 'blk', partner_pairs(blocks, step))]
    ppermute x0 -> x12, starting transfers between devices: none -> 16.5 us  [exchange(): return lax.ppermute(value, 'blk', partner_pairs(blocks, step))]
    reduce_scatter x0 -> x1, waiting for transfers between devices: none -> 13.5 us  [body(): lax.psum_scatter(partial, 'group', scatter_dimension=0, tiled=True)]
    all_gather x1 -> x0, blocking collectives: 8.03 us -> none  [body(): lax.all_gather(label_rows.astype(jnp.float32), 'blk', axis=0, tiled=True)]
    dot_general x4 -> x16, matrix products: 12.3 us -> 19.6 us  [the longest x4 9.27 us: body(): lax.dot_general(weights_of(logits_t, pair_sign_t), image_from[k], (((0,),...]
  transfers between devices with their start and end apart: 4 -> 14, of which waited for: 4 -> 6; matrix products, arithmetic and copies ran while one was open for 5% -> 16% of each run, Pallas kernels for 0% -> 0%
where the time goes in v2:
time: 148 us
  waiting for transfers between devices  84.7 us (57%)
  matrix products  23.9 us (16%)
  starting transfers between devices  16.6 us (11%)
  between operations  15.5 us (10%)
  other arithmetic  5.24 us (4%)
  local copies, waits for them, and re-layouts  2.03 us (1%)
    all_gather x1, waiting for transfers between devices, body(): w_full = lax.all_gather(linear_map_matrix, 'group', axis=0, tiled=True)  42.8 us
    ppermute x12, waiting for transfers between devices, exchange(): return lax.ppermute(value, 'blk', partner_pairs(blocks, step))  27.7 us
    ppermute x12, starting transfers between devices, exchange(): return lax.ppermute(value, 'blk', partner_pairs(blocks, step))  16.5 us
    reduce_scatter x1, waiting for transfers between devices, body(): lax.psum_scatter(partial, 'group', scatter_dimension=0, tiled=True)  13.5 us
    dot_general x4, matrix products, body(): lax.dot_general(weights_of(logits_t, pair_sign_t), image_from[k], (((0,),...  9.27 us
    dot_general x4, matrix products, body(): lax.dot_general(hidden_from[k], grad_from[k], (((0,), (0,)), ((), ())), p...  6.62 us
    dot_general x1, matrix products, body(): projected = jnp.dot(hidden_rows, w_full, preferred_element_type=jnp.float32)  4.28 us
  transfers between devices with their start and end apart: 14, of which 6 were waited for; matrix products, arithmetic and copies ran while one was open for 16% of the time, Pallas kernels for 0%

profile of v2, /device:TPU:0, one launch (start us, length us, event | category | flops | bytes accessed | tf_op | source)
XLA Modules:
  0.0 147.9 jit_solution(15230081478559116382)
XLA Ops:
  7.2 0.0 copy-start
  7.2 0.0 all-gather.2.cloned.1.call-start
  7.2 0.7 all-gather.2.cloned.1.call-update
  7.9 0.0 reduce-scatter.2.cloned.1.call-start
  8.0 4.0 %collective-permute-start.7 = (s32[256]{0:T(256)}, s32[256]{0:T(256)}, u32[]{:S(2)}, u32[]{:S(2)}) collective-permute-start(s32[256]{0:T(256)} %bitcast.66), channel_id=1, source_target_pairs={{0,24},{8,16},{16,8},{24,0},{1,25},{9,17},{17,9},{25,1},{2,26},{10... | collective-permute-start | bytes 3080 | tf_op jit(solution)/shard_map/ppermute | solution.py:41
  11.9 0.5 collective-permute-start.3
  12.4 1.2 fusion.43
  13.6 1.3 dynamic-slice_bitcast_fusion.1
  14.9 0.0 copy-done
  14.9 0.1 fusion.38
  15.1 1.3 pad_maximum_fusion.1
  16.4 0.1 collective-permute-start.6
  16.5 2.8 %collective-permute-start.8 = (bf16[256,1536]{1,0:T(8,128)(2,1)}, bf16[256,1536]{1,0:T(8,128)(2,1)}, u32[]{:S(2)}, u32[]{:S(2)}) collective-permute-start(bf16[256,1536]{1,0:T(8,128)(2,1)} %get-tuple-element.11), channel_id=1, source_target_pairs={{0,24},{8,16},{16,8},{24,0},{1,25},{9,17},{17,9},{25,1},{2,26},{10... | collective-permute-start | bytes 2359304 | tf_op jit(solution)/shard_map/ppermute | solution.py:41
  19.4 0.5 collective-permute-start.4
  21.2 0.0 copy-start.4
  21.2 0.0 copy-start.3
  21.3 42.8 %all-gather.2.cloned.1.call-done = bf16[3072,768]{1,0:T(8,128)(2,1)} async-done(((bf16[384,768]{1,0:T(8,128)(2,1)}), bf16[3072,768]{1,0:T(8,128)(2,1)}) %all-gather.2.cloned.1.call-update) | async-done | bytes 4718608 | tf_op jit(solution)/shard_map/all_gather | solution.py:43
  64.1 4.3 %multiply_reduce_fusion.1 = (f32[256]{0:T(256)S(1)}, f32[256,768]{1,0:T(8,128)S(1)}) fusion(bf16[3072,768]{1,0:T(8,128)(2,1)} %all-gather.2.cloned.1.call-done, bf16[1,256,3072]{2,1,0:T(8,128)(2,1)} %param.7), kind=kOutput, calls=%fused_computation.63 | convolution fusion | flops 1208352512 | bytes 7078912 | tf_op jit(solution)/shard_map/dot_general | solution.py:65
  68.4 0.1 multiply_convert_fusion.1
  68.5 0.3 fusion.4
  68.8 0.0 copy-start.1
  68.8 0.7 copy-done.1
  69.5 0.0 copy-done.3
  69.5 1.3 fusion.161
  70.8 0.0 collective-permute-done.3
  70.8 1.5 collective-permute-start.5
  72.3 0.0 collective-permute-done.4
  72.3 3.0 %convolution_add_fusion.1 = f32[256,768]{1,0:T(8,128)} fusion(f32[256,768]{1,0:T(8,128)} %fusion.161, bf16[256,768]{1,0:T(8,128)(2,1)S(1)} %multiply_convert_fusion.1, bf16[256,1536]{1,0:T(8,128)(2,1)} %collective-permute-done.4, s32[256]{0:T(256)} %collective-permute-done.3, f32[]{:T(128)} %bitcast.62, f32[]{:T(128)} %bitcast.49, s32[256]{0:T(256)S(1)} %iota_add_fusion.3), kind=kOutput, calls=%fused_computation.5 | convolution fusion | flops 202309632 | bytes 2754568 | tf_op jit(solution)/shard_map/dot_general | solution.py:88
  75.3 0.0 collective-permute-done.7
  75.3 0.0 collective-permute-done.8
  75.3 0.0 copy-done.4
  75.3 2.8 %fusion.35 = f32[256,768]{1,0:T(8,128)} fusion(bf16[256,768]{1,0:T(8,128)(2,1)S(1)} %multiply_convert_fusion.1, bf16[256,1536]{1,0:T(8,128)(2,1)} %collective-permute-done.8, s32[256]{0:T(256)} %collective-permute-done.7, f32[]{:T(128)} %bitcast.60, f32[]{:T(128)} %bitcast.48, s32[256]{0:T(256)S(1)} %iota_add_fusion.3), kind=kOutput, calls=%fused_computation.47 | convolution fusion | flops 202113024 | bytes 1968136 | tf_op jit(solution)/shard_map/dot_general | solution.py:88
  78.1 0.0 collective-permute-done.5
  78.1 0.0 collective-permute-done.6
  78.1 2.2 %multiply_reduce_fusion = (f32[256]{0:T(256)S(1)}, f32[256,768]{1,0:T(8,128)S(1)}) fusion(f32[256,768]{1,0:T(8,128)S(1)} %get-tuple-element.14, f32[256]{0:T(256)S(1)} %add_rsqrt_fusion, f32[256,768]{1,0:T(8,128)} %fusion.35, f32[256,768]{1,0:T(8,128)} %convolution_add_fusion.1, bf16[256,1536]{1,0:T(8,128)(2,1)S(1)} %collective-permute-done.6, ...), kind=kOutput, calls=%fused_computation.62 | convolution fusion | flops 203095808 | bytes 4329480 | tf_op jit(solution)/shard_map/dot_general | solution.py:88
  80.3 0.9 multiply_convert_fusion
  81.2 1.5 collective-permute-start.9
  82.7 0.5 collective-permute-start.11
  83.2 1.5 collective-permute-start.10
  84.7 1.6 %fusion.59 = f32[768,768]{1,0:T(8,128)S(1)} fusion(bf16[256,768]{1,0:T(8,128)(2,1)} %multiply_convert_fusion, bf16[1,256,3072]{2,1,0:T(8,128)(2,1)} %param.7, s32[]{:T(128)S(6)} %select_n.57), kind=kOutput, calls=%fused_computation.79 | convolution fusion | flops 301989888 | bytes 3145732 | tf_op jit(solution)/shard_map/dot_general | solution.py:103
  86.3 7.1 %collective-permute-done.9 = bf16[256,768]{1,0:T(8,128)(2,1)S(1)} collective-permute-done((bf16[256,768]{1,0:T(8,128)(2,1)}, bf16[256,768]{1,0:T(8,128)(2,1)S(1)}, u32[]{:S(2)}, u32[]{:S(2)}) %collective-permute-start.9) | collective-permute-done | bytes 393248 | tf_op jit(solution)/shard_map/ppermute | solution.py:41
  93.4 1.5 %fusion.51 = f32[768,768]{1,0:T(8,128)S(1)} fusion(bf16[256,768]{1,0:T(8,128)(2,1)S(1)} %collective-permute-done.9, bf16[256,1536]{1,0:T(8,128)(2,1)} %collective-permute-done.4), kind=kOutput, calls=%fused_computation.74 | convolution fusion | flops 301989888 | bytes 3145728 | tf_op jit(solution)/shard_map/dot_general | solution.py:103
  94.9 7.4 %collective-permute-done.10 = bf16[256,768]{1,0:T(8,128)(2,1)S(1)} collective-permute-done((bf16[256,768]{1,0:T(8,128)(2,1)}, bf16[256,768]{1,0:T(8,128)(2,1)S(1)}, u32[]{:S(2)}, u32[]{:S(2)}) %collective-permute-start.10) | collective-permute-done | bytes 393248 | tf_op jit(solution)/shard_map/ppermute | solution.py:41
  102.3 0.5 fusion.49
  102.8 0.0 collective-permute-done.11
  102.8 3.0 %add_add_fusion = f32[768,768]{1,0:T(8,128)} fusion(f32[768,768]{1,0:T(8,128)S(1)} %fusion.49, f32[768,768]{1,0:T(8,128)S(1)} %fusion.59, f32[768,768]{1,0:T(8,128)S(1)} %fusion.51, bf16[256,768]{1,0:T(8,128)(2,1)S(1)} %collective-permute-done.11, bf16[256,1536]{1,0:T(8,128)(2,1)} %collective-permute-done.8), kind=kOutput, calls=%fused_computation | convolution fusion | flops 303759360 | bytes 10223616 | tf_op jit(solution)/shard_map/dot_general | solution.py:103
  105.8 0.0 reduce-scatter.2.cloned.1.call-update
  105.8 2.5 %collective-permute-start.2 = (bf16[256,768]{1,0:T(8,128)(2,1)S(1)}, bf16[256,768]{1,0:T(8,128)(2,1)S(1)}, u32[]{:S(2)}, u32[]{:S(2)}) collective-permute-start(bf16[256,768]{1,0:T(8,128)(2,1)S(1)} %multiply_convert_fusion.1), channel_id=1, source_target_pairs={{0,24},{8,16},{16,8},{24,0},{1,25},{9,17},{17,9},{25,1},{2,26},{10... | collective-permute-start | bytes 1179656 | tf_op jit(solution)/shard_map/ppermute | solution.py:41
  108.3 0.5 collective-permute-start.1
  108.8 0.6 collective-permute-start
  109.4 0.0 copy-done.2
  109.4 0.4 fusion.163
  109.8 9.0 %collective-permute-done.2 = bf16[256,768]{1,0:T(8,128)(2,1)S(1)} collective-permute-done((bf16[256,768]{1,0:T(8,128)(2,1)S(1)}, bf16[256,768]{1,0:T(8,128)(2,1)S(1)}, u32[]{:S(2)}, u32[]{:S(2)}) %collective-permute-start.2) | collective-permute-done | bytes 393248 | tf_op jit(solution)/shard_map/ppermute | solution.py:41
  118.8 0.3 fusion.7
  119.2 4.2 %collective-permute-done.1 = bf16[256,768]{1,0:T(8,128)(2,1)S(1)} collective-permute-done((bf16[256,768]{1,0:T(8,128)(2,1)S(1)}, bf16[256,768]{1,0:T(8,128)(2,1)S(1)}, u32[]{:S(2)}, u32[]{:S(2)}) %collective-permute-start.1) | collective-permute-done | bytes 393248 | tf_op jit(solution)/shard_map/ppermute | solution.py:41
  123.4 0.3 fusion.6
  123.7 0.0 collective-permute-done
  123.7 0.9 fusion.95
  124.6 0.6 add_add_fusion.1
  125.2 0.4 fusion.113
  125.6 0.4 convolution_add_fusion.3
  126.1 0.6 fusion.39
  126.6 1.0 fusion.44
  127.6 13.5 %reduce-scatter.2.cloned.1.call-done = f32[96,768]{1,0:T(8,128)} async-done(((f32[768,768]{1,0:T(8,128)}), f32[96,768]{1,0:T(8,128)}) %reduce-scatter.2.cloned.1.call-update) | async-done | bytes 294928 | tf_op jit(solution)/shard_map/reduce_scatter | solution.py:106
  (8 shorter events, 0.0 us)
Async XLA Ops:
  7.2 7.8 %copy-start = (bf16[1,256,768]{2,1,0:T(8,128)(2,1)S(1)}, bf16[1,256,768]{2,1,0:T(8,128)(2,1)}, u32[]{:S(2)}) copy-start(bf16[1,256,768]{2,1,0:T(8,128)(2,1)} %param.6) | copy-start | bytes 1179652
  7.2 56.9 %all-gather.2.cloned.1.call-start = ((), (), s32[]{:S(2)}) async-start(), calls=%async_computation.1 | async-start | bytes 5308416 | tf_op jit(solution)/shard_map/all_gather | solution.py:43
  7.9 133.2 %reduce-scatter.2.cloned.1.call-start = ((), (), s32[]{:S(2)}) async-start(), calls=%async_computation.2 | async-start | bytes 2654208 | tf_op jit(solution)/shard_map/reduce_scatter | solution.py:106
  8.0 67.3 %collective-permute-start.7 = (s32[256]{0:T(256)}, s32[256]{0:T(256)}, u32[]{:S(2)}, u32[]{:S(2)}) collective-permute-start(s32[256]{0:T(256)} %bitcast.66), channel_id=1, source_target_pairs={{0,24},{8,16},{16,8},{24,0},{1,25},{9,17},{17,9},{25,1},{2,26},{10... | collective-permute-start | bytes 3080 | tf_op jit(solution)/shard_map/ppermute | solution.py:41
  11.9 58.9 %collective-permute-start.3 = (s32[256]{0:T(256)}, s32[256]{0:T(256)}, u32[]{:S(2)}, u32[]{:S(2)}) collective-permute-start(s32[256]{0:T(256)} %bitcast.67), channel_id=1, source_target_pairs={{0,8},{8,0},{16,24},{24,16},{1,9},{9,1},{17,25},{25,17},{2,10},{10... | collective-permute-start | bytes 3080 | tf_op jit(solution)/shard_map/ppermute | solution.py:41
  16.4 61.7 %collective-permute-start.6 = (bf16[256,1536]{1,0:T(8,128)(2,1)S(1)}, bf16[256,1536]{1,0:T(8,128)(2,1)S(1)}, u32[]{:S(2)}, u32[]{:S(2)}) collective-permute-start(bf16[256,1536]{1,0:T(8,128)(2,1)S(1)} %get-tuple-element.10), channel_id=1, source_target_pairs={{0,16},{8,24},{16,0},{24,8},{1,17},{9,25},{17,1},{25,9},{2,18},{10... | collective-permute-start | bytes 2359304 | tf_op jit(solution)/shard_map/ppermute | solution.py:41
  16.5 58.7 %collective-permute-start.8 = (bf16[256,1536]{1,0:T(8,128)(2,1)}, bf16[256,1536]{1,0:T(8,128)(2,1)}, u32[]{:S(2)}, u32[]{:S(2)}) collective-permute-start(bf16[256,1536]{1,0:T(8,128)(2,1)} %get-tuple-element.11), channel_id=1, source_target_pairs={{0,24},{8,16},{16,8},{24,0},{1,25},{9,17},{17,9},{25,1},{2,26},{10... | collective-permute-start | bytes 2359304 | tf_op jit(solution)/shard_map/ppermute | solution.py:41
  19.4 52.9 %collective-permute-start.4 = (bf16[256,1536]{1,0:T(8,128)(2,1)}, bf16[256,1536]{1,0:T(8,128)(2,1)}, u32[]{:S(2)}, u32[]{:S(2)}) collective-permute-start(bf16[256,1536]{1,0:T(8,128)(2,1)} %get-tuple-element.12), channel_id=1, source_target_pairs={{0,8},{8,0},{16,24},{24,16},{1,9},{9,1},{17,25},{25,17},{2,10},{10... | collective-permute-start | bytes 2359304 | tf_op jit(solution)/shard_map/ppermute | solution.py:41
  21.2 54.0 %copy-start.4 = (s32[256]{0:T(256)}, s32[256]{0:T(256)S(1)}, u32[]{:S(2)}) copy-start(s32[256]{0:T(256)S(1)} %iota_add_fusion.3) | copy-start | bytes 3076
  21.2 48.3 %copy-start.3 = (s32[1,256]{1,0:T(1,128)S(1)}, s32[1,256]{1,0:T(1,128)}, u32[]{:S(2)}) copy-start(s32[1,256]{1,0:T(1,128)} %param.9) | copy-start | bytes 3076
  68.8 0.7 copy-start.1
  70.8 7.3 %collective-permute-start.5 = (s32[256]{0:T(256)S(1)}, s32[256]{0:T(256)}, u32[]{:S(2)}, u32[]{:S(2)}) collective-permute-start(s32[256]{0:T(256)S(1)} %bitcast.69), channel_id=1, source_target_pairs={{0,16},{8,24},{16,0},{24,8},{1,17},{9,25},{17,1},{25,9},{2,18},{10... | collective-permute-start | bytes 3080 | tf_op jit(solution)/shard_map/ppermute | solution.py:41
  81.2 12.2 %collective-permute-start.9 = (bf16[256,768]{1,0:T(8,128)(2,1)}, bf16[256,768]{1,0:T(8,128)(2,1)S(1)}, u32[]{:S(2)}, u32[]{:S(2)}) collective-permute-start(bf16[256,768]{1,0:T(8,128)(2,1)} %multiply_convert_fusion), channel_id=1, source_target_pairs={{0,8},{8,0},{16,24},{24,16},{1,9},{9,1},{17,25},{25,17},{2,10},{10... | collective-permute-start | bytes 1179656 | tf_op jit(solution)/shard_map/ppermute | solution.py:41
  82.7 20.1 %collective-permute-start.11 = (bf16[256,768]{1,0:T(8,128)(2,1)}, bf16[256,768]{1,0:T(8,128)(2,1)S(1)}, u32[]{:S(2)}, u32[]{:S(2)}) collective-permute-start(bf16[256,768]{1,0:T(8,128)(2,1)} %multiply_convert_fusion), channel_id=1, source_target_pairs={{0,24},{8,16},{16,8},{24,0},{1,25},{9,17},{17,9},{25,1},{2,26},{10... | collective-permute-start | bytes 1179656 | tf_op jit(solution)/shard_map/ppermute | solution.py:41
  83.2 19.1 %collective-permute-start.10 = (bf16[256,768]{1,0:T(8,128)(2,1)}, bf16[256,768]{1,0:T(8,128)(2,1)S(1)}, u32[]{:S(2)}, u32[]{:S(2)}) collective-permute-start(bf16[256,768]{1,0:T(8,128)(2,1)} %multiply_convert_fusion), channel_id=1, source_target_pairs={{0,16},{8,24},{16,0},{24,8},{1,17},{9,25},{17,1},{25,9},{2,18},{10... | collective-permute-start | bytes 1179656 | tf_op jit(solution)/shard_map/ppermute | solution.py:41
  105.8 3.6 %copy-start.2 = (f32[256,256]{0,1:T(8,128)S(1)}, f32[256,256]{0,1:T(8,128)}, u32[]{:S(2)}) copy-start(f32[256,256]{0,1:T(8,128)} %copy-done.1) | copy-start | bytes 786436
  105.8 3.6 %copy-start.5 = (s32[256]{0:T(256)S(1)}, s32[256]{0:T(256)}, u32[]{:S(2)}) copy-start(s32[256]{0:T(256)} %copy-done.4) | copy-start | bytes 3076
  105.8 13.0 %collective-permute-start.2 = (bf16[256,768]{1,0:T(8,128)(2,1)S(1)}, bf16[256,768]{1,0:T(8,128)(2,1)S(1)}, u32[]{:S(2)}, u32[]{:S(2)}) collective-permute-start(bf16[256,768]{1,0:T(8,128)(2,1)S(1)} %multiply_convert_fusion.1), channel_id=1, source_target_pairs={{0,24},{8,16},{16,8},{24,0},{1,25},{9,17},{17,9},{25,1},{2,26},{10... | collective-permute-start | bytes 1179656 | tf_op jit(solution)/shard_map/ppermute | solution.py:41
  108.3 15.1 %collective-permute-start.1 = (bf16[256,768]{1,0:T(8,128)(2,1)S(1)}, bf16[256,768]{1,0:T(8,128)(2,1)S(1)}, u32[]{:S(2)}, u32[]{:S(2)}) collective-permute-start(bf16[256,768]{1,0:T(8,128)(2,1)S(1)} %multiply_convert_fusion.1), channel_id=1, source_target_pairs={{0,16},{8,24},{16,0},{24,8},{1,17},{9,25},{17,1},{25,9},{2,18},{10... | collective-permute-start | bytes 1179656 | tf_op jit(solution)/shard_map/ppermute | solution.py:41
  108.8 14.9 %collective-permute-start = (bf16[256,768]{1,0:T(8,128)(2,1)S(1)}, bf16[256,768]{1,0:T(8,128)(2,1)S(1)}, u32[]{:S(2)}, u32[]{:S(2)}) collective-permute-start(bf16[256,768]{1,0:T(8,128)(2,1)S(1)} %multiply_convert_fusion.1), channel_id=1, source_target_pairs={{0,8},{8,0},{16,24},{24,16},{1,9},{9,1},{17,25},{25,17},{2,10},{10... | collective-permute-start | bytes 1179656 | tf_op jit(solution)/shard_map/ppermute | solution.py:41
Sparse Core Ops, SparseCore 0:
  9.6 54.3 all-gather.1
  105.9 35.1 reduce-scatter.1

commit v3 on v2

--- a/solution.py
+++ b/solution.py
@@ -40,7 +40,18 @@
     def exchange(value, step):
         return lax.ppermute(value, "blk", partner_pairs(blocks, step))
 
-    w_full = lax.all_gather(linear_map_matrix, "group", axis=0, tiled=True)
+    shard_rows = linear_map_matrix.shape[0]
+    piece_rows = shard_rows // blocks
+    groups = lax.axis_size("group")
+    w_piece = lax.dynamic_slice_in_dim(linear_map_matrix, my_index * piece_rows, piece_rows, 0)
+    w_quarter = lax.all_gather(w_piece, "group", axis=0, tiled=False)
+    w_parts = jnp.zeros((groups, blocks, piece_rows, w_piece.shape[1]), w_piece.dtype)
+    w_parts = lax.dynamic_update_slice_in_dim(w_parts, w_quarter[:, None], my_index, 1)
+    for k in range(1, blocks):
+        w_parts = lax.dynamic_update_slice_in_dim(
+            w_parts, exchange(w_quarter, k)[:, None], partner_of(my_index, blocks, k), 1
+        )
+    w_full = w_parts.reshape(groups * shard_rows, w_piece.shape[1])
 
     image_float = image_rows.astype(jnp.float32)
     image_scale = lax.rsqrt(jnp.sum(image_float * image_float, axis=1, keepdims=True) + epsilon)
@@ -54,12 +65,11 @@
     label_from = [label_rows]
     for k in range(1, blocks):
         target = partner_of(my_index, blocks, k)
-        outgoing = jnp.concatenate(
-            [lax.dynamic_slice_in_dim(hidden_rows, target * chunk, chunk, 1), image_unit], axis=1
+        outgoing, _ = lax.optimization_barrier(
+            (lax.dynamic_slice_in_dim(hidden_rows, target * chunk, chunk, 1), w_full)
         )
-        incoming = exchange(outgoing, k)
-        hidden_from.append(incoming[:, :chunk])
-        image_from.append(incoming[:, chunk:])
+        hidden_from.append(exchange(outgoing, k))
+        image_from.append(exchange(image_unit, k))
         label_from.append(exchange(label_rows, k))
 
     projected = jnp.dot(hidden_rows, w_full, preferred_element_type=jnp.float32)
@@ -95,9 +105,11 @@
         text_scale
         * (text_unit_grad - text_dir * jnp.sum(text_dir * text_unit_grad, axis=1, keepdims=True))
     ).astype(jnp.bfloat16)
-    grad_from = [projection_output_gradient] + [
-        exchange(projection_output_gradient, k) for k in range(1, blocks)
-    ]
+    grad_send, hidden_remote = lax.optimization_barrier(
+        (projection_output_gradient, hidden_from[1:])
+    )
+    hidden_from = hidden_from[:1] + list(hidden_remote)
+    grad_from = [projection_output_gradient] + [exchange(grad_send, k) for k in range(1, blocks)]
     partial = jnp.zeros((chunk, projection_output_gradient.shape[1]), jnp.float32)
     for k in range(blocks):
         partial = partial + lax.dot_general(

time: 148 us -> 196 us (1.32)
  waiting for transfers between devices: 84.7 us -> 124 us
  local copies, waits for them, and re-layouts: 2.03 us -> 8.27 us
  starting transfers between devices: 16.6 us -> 22.2 us
  matrix products: 23.9 us -> 21 us
    ppermute x12 -> x18, waiting for transfers between devices: 27.7 us -> 82 us  [exchange(): return lax.ppermute(value, 'blk', partner_pairs(blocks, step))]
    all_gather x1, waiting for transfers between devices: 42.8 us -> 26.6 us  [body(): w_quarter = lax.all_gather(w_piece, 'group', axis=0, tiled=False)]
    ppermute x12 -> x18, starting transfers between devices: 16.5 us -> 22.1 us  [exchange(): return lax.ppermute(value, 'blk', partner_pairs(blocks, step))]
    dynamic_update_slice x0 -> x4, local copies, waits for them, and re-layouts: none -> 4.24 us  [the longest x3 4.13 us: body(): lax.dynamic_update_slice_in_dim(w_parts, exchange(w_quarter, k)[:, None],...]
    dot_general x1, matrix products: 4.28 us -> 1.48 us  [body(): projected = jnp.dot(hidden_rows, w_full, preferred_element_type=jnp.float32)]
  transfers between devices with their start and end apart: 14 -> 20, of which waited for: 6 -> 11; matrix products, arithmetic and copies ran while one was open for 16% -> 14% of each run, Pallas kernels for 0% -> 0%
where the time goes in v3:
time: 196 us; the launch traced here: 195 us
  waiting for transfers between devices  124 us (63%)
  starting transfers between devices  22.2 us (11%)
  matrix products  21 us (11%)
  between operations  15.6 us (8%)
  local copies, waits for them, and re-layouts  8.27 us (4%)
  other arithmetic  4.02 us (2%)
    ppermute x18, waiting for transfers between devices, exchange(): return lax.ppermute(value, 'blk', partner_pairs(blocks, step))  82 us
    all_gather x1, waiting for transfers between devices, body(): w_quarter = lax.all_gather(w_piece, 'group', axis=0, tiled=False)  26.6 us
    ppermute x18, starting transfers between devices, exchange(): return lax.ppermute(value, 'blk', partner_pairs(blocks, step))  22.1 us
    reduce_scatter x1, waiting for transfers between devices, body(): lax.psum_scatter(partial, 'group', scatter_dimension=0, tiled=True)  15.3 us
    dot_general x4, matrix products, body(): lax.dot_general(weights_of(logits_t, pair_sign_t), image_from[k], (((0,),...  8.19 us
    dot_general x4, matrix products, body(): lax.dot_general(hidden_from[k], grad_from[k], (((0,), (0,)), ((), ())), p...  7.51 us
    dynamic_update_slice x3, local copies, waits for them, and re-layouts, body(): lax.dynamic_update_slice_in_dim(w_parts, exchange(w_quarter, k)[:, None],...  4.13 us
  transfers between devices with their start and end apart: 20, of which 11 were waited for; matrix products, arithmetic and copies ran while one was open for 14% of the time, Pallas kernels for 0%

profile of v3, /device:TPU:0, one launch (start us, length us, event | category | flops | bytes accessed | tf_op | source)
XLA Modules:
  0.0 195.1 jit_solution(6354938305030355816)
XLA Ops:
  7.2 0.0 all-gather.3.cloned.1.call-start
  7.2 1.0 copy-done
  8.2 0.7 constant_dynamic-slice_fusion
  8.9 0.0 all-gather.3.cloned.1.call-update
  8.9 0.0 reduce-scatter.2.cloned.1.call-start
  9.0 26.6 %all-gather.3.cloned.1.call-done = bf16[768,768]{1,0:T(8,128)(2,1)} async-done(((bf16[96,768]{1,0:T(8,128)(2,1)}), bf16[768,768]{1,0:T(8,128)(2,1)}) %all-gather.3.cloned.1.call-update) | async-done | bytes 1179664 | tf_op jit(solution)/shard_map/all_gather | solution.py:47
  35.6 1.5 collective-permute-start
  37.1 1.5 collective-permute-start.1
  38.6 1.2 fusion.43
  39.7 0.6 collective-permute-start.2
  40.3 1.1 fusion.38
  41.5 1.5 collective-permute-start.7
  43.0 1.5 collective-permute-start.11
  45.8 1.1 dynamic-slice_bitcast_fusion
  46.9 0.5 broadcast_in_dim.58
  47.4 0.7 copy-done.4
  48.2 0.1 constant_dynamic-update-slice_fusion
  48.3 16.5 %collective-permute-done = bf16[8,96,768]{2,1,0:T(8,128)(2,1)} collective-permute-done((bf16[8,96,768]{2,1,0:T(8,128)(2,1)}, bf16[8,96,768]{2,1,0:T(8,128)(2,1)}, u32[]{:S(2)}, u32[]{:S(2)}) %collective-permute-start) | collective-permute-done | bytes 1179680 | tf_op jit(solution)/shard_map/ppermute | solution.py:41
  64.7 1.5 collective-permute-start.6
  66.2 1.4 bitcast_dynamic-update-slice_fusion.1
  67.6 22.4 %collective-permute-done.1 = bf16[8,96,768]{2,1,0:T(8,128)(2,1)} collective-permute-done((bf16[8,96,768]{2,1,0:T(8,128)(2,1)}, bf16[8,96,768]{2,1,0:T(8,128)(2,1)}, u32[]{:S(2)}, u32[]{:S(2)}) %collective-permute-start.1) | collective-permute-done | bytes 1179680 | tf_op jit(solution)/shard_map/ppermute | solution.py:41
  90.0 1.5 collective-permute-start.10
  91.5 1.4 bitcast_dynamic-update-slice_fusion
  92.9 0.5 collective-permute-start.9
  93.5 1.4 bitcast_dynamic-update-slice_fusion.2
  94.8 1.5 multiply_reduce_fusion
  96.3 0.1 bitcast_convert_fusion
  96.4 0.3 fusion.4
  96.8 1.4 fusion.151
  98.1 8.1 %collective-permute-done.6 = s32[256]{0:T(256)S(1)} collective-permute-done((s32[256]{0:T(256)S(1)}, s32[256]{0:T(256)S(1)}, u32[]{:S(2)}, u32[]{:S(2)}) %collective-permute-start.6) | collective-permute-done | bytes 1056 | tf_op jit(solution)/shard_map/ppermute | solution.py:41
  106.2 1.5 collective-permute-start.8
  107.7 1.4 collective-permute-start.12
  109.1 3.0 %convolution_add_fusion.1 = f32[256,768]{0,1:T(8,128)} fusion(f32[256,768]{0,1:T(8,128)} %fusion.151, bf16[256,768]{1,0:T(8,128)(2,1)} %collective-permute-done.7, bf16[256,768]{0,1:T(8,128)(2,1)S(1)} %bitcast_convert_fusion, s32[256]{0:T(256)S(1)} %collective-permute-done.6, f32[]{:T(128)} %bitcast.96, f32[]{:T(128)} %bitcast.83, s32[256]{0:T(256)S(1)} %iota_add_fusion.3), kind=kOutput, calls=%fused_computation.5 | convolution fusion | flops 202309632 | bytes 2361352 | tf_op jit(solution)/shard_map/dot_general | solution.py:98
  112.1 0.6 collective-permute-start.13
  112.7 1.5 collective-permute-start.14
  114.2 1.7 fusion.35
  115.9 2.1 %fusion.44 = (f32[256]{0:T(256)S(1)}, f32[256,768]{0,1:T(8,128)S(1)}) fusion(f32[768,256]{1,0:T(8,128)S(1)} %get-tuple-element.25, f32[256]{0:T(256)S(1)} %add_rsqrt_fusion, f32[256,768]{0,1:T(8,128)} %fusion.35, f32[256,768]{0,1:T(8,128)} %convolution_add_fusion.1, bf16[256,768]{1,0:T(8,128)(2,1)S(1)} %collective-permute-done.9, ...), kind=kOutput, calls=%fused_computation.64 | convolution fusion | flops 203095808 | bytes 3936264 | tf_op jit(solution)/shard_map/dot_general | solution.py:98
  118.0 0.1 fusion.47
  118.2 1.9 collective-permute-done.12
  120.0 10.7 %collective-permute-done.13 = bf16[256,768]{1,0:T(8,128)(2,1)} collective-permute-done((bf16[256,768]{1,0:T(8,128)(2,1)}, bf16[256,768]{1,0:T(8,128)(2,1)}, u32[]{:S(2)}, u32[]{:S(2)}) %collective-permute-start.13) | collective-permute-done | bytes 393248 | tf_op jit(solution)/shard_map/ppermute | solution.py:41
  130.8 0.6 collective-permute-start.15
  131.4 0.6 collective-permute-start.16
  131.9 1.5 fusion.49
  133.4 2.4 %collective-permute-start.17 = (bf16[256,768]{0,1:T(8,128)(2,1)S(1)}, bf16[256,768]{0,1:T(8,128)(2,1)S(1)}, u32[]{:S(2)}, u32[]{:S(2)}) collective-permute-start(bf16[256,768]{0,1:T(8,128)(2,1)S(1)} %fusion.47), channel_id=1, source_target_pairs={{0,24},{8,16},{16,8},{24,0},{1,25},{9,17},{17,9},{25,1},{2,26},{10... | collective-permute-start | bytes 1179656 | tf_op jit(solution)/shard_map/ppermute | solution.py:41
  135.8 7.0 %collective-permute-done.15 = bf16[256,768]{0,1:T(8,128)(2,1)S(1)} collective-permute-done((bf16[256,768]{0,1:T(8,128)(2,1)S(1)}, bf16[256,768]{0,1:T(8,128)(2,1)S(1)}, u32[]{:S(2)}, u32[]{:S(2)}) %collective-permute-start.15) | collective-permute-done | bytes 393248 | tf_op jit(solution)/shard_map/ppermute | solution.py:41
  142.8 1.5 fusion.155
  144.3 4.1 %collective-permute-done.16 = bf16[256,768]{0,1:T(8,128)(2,1)S(1)} collective-permute-done((bf16[256,768]{0,1:T(8,128)(2,1)S(1)}, bf16[256,768]{0,1:T(8,128)(2,1)S(1)}, u32[]{:S(2)}, u32[]{:S(2)}) %collective-permute-start.16) | collective-permute-done | bytes 393248 | tf_op jit(solution)/shard_map/ppermute | solution.py:41
  148.4 1.5 fusion.156
  150.0 3.0 %add_add_fusion = f32[768,768]{1,0:T(8,128)} fusion(f32[768,768]{1,0:T(8,128)S(1)} %fusion.156, f32[768,768]{1,0:T(8,128)S(1)} %fusion.49, f32[768,768]{1,0:T(8,128)S(1)} %fusion.155, bf16[256,768]{1,0:T(8,128)(2,1)} %collective-permute-done.14, bf16[256,768]{0,1:T(8,128)(2,1)S(1)} %collective-permute-done.17), kind=kOutput, calls=%fused_computation | convolution fusion | flops 303759360 | bytes 10223616 | tf_op jit(solution)/shard_map/dot_general | solution.py:115
  153.0 1.5 collective-permute-start.5
  154.5 1.4 collective-permute-start.4
  155.9 0.6 collective-permute-start.3
  156.5 0.4 fusion.153
  157.0 7.6 %collective-permute-done.5 = bf16[256,768]{0,1:T(8,128)(2,1)S(1)} collective-permute-done((bf16[256,768]{0,1:T(8,128)(2,1)S(1)}, bf16[256,768]{0,1:T(8,128)(2,1)S(1)}, u32[]{:S(2)}, u32[]{:S(2)}) %collective-permute-start.5) | collective-permute-done | bytes 393248 | tf_op jit(solution)/shard_map/ppermute | solution.py:41
  164.5 0.3 fusion.7
  164.9 3.7 %collective-permute-done.4 = bf16[256,768]{0,1:T(8,128)(2,1)S(1)} collective-permute-done((bf16[256,768]{0,1:T(8,128)(2,1)S(1)}, bf16[256,768]{0,1:T(8,128)(2,1)S(1)}, u32[]{:S(2)}, u32[]{:S(2)}) %collective-permute-start.4) | collective-permute-done | bytes 393248 | tf_op jit(solution)/shard_map/ppermute | solution.py:41
  168.6 0.3 fusion.6
  168.9 1.0 fusion.85
  169.9 0.6 add_add_fusion.1
  170.5 0.4 fusion.103
  171.0 0.4 convolution_add_fusion.3
  171.4 0.6 fusion.39
  172.0 1.0 fusion.48
  173.0 15.3 %reduce-scatter.2.cloned.1.call-done = f32[96,768]{1,0:T(8,128)} async-done(((f32[768,768]{1,0:T(8,128)}), f32[96,768]{1,0:T(8,128)}) %reduce-scatter.2.cloned.1.call-update) | async-done | bytes 294928 | tf_op jit(solution)/shard_map/reduce_scatter | solution.py:118
  (29 shorter events, 0.1 us)
Async XLA Ops:
  7.2 1.1 copy-start
  7.2 38.6 %copy-start.2 = (bf16[1,256,3072]{2,1,0:T(8,128)(2,1)S(1)}, bf16[1,256,3072]{2,1,0:T(8,128)(2,1)}, u32[]{:S(2)}) copy-start(bf16[1,256,3072]{2,1,0:T(8,128)(2,1)} %param.7) | copy-start | bytes 4718596
  7.2 28.4 %all-gather.3.cloned.1.call-start = ((), (), s32[]{:S(2)}) async-start(), calls=%async_computation.2 | async-start | bytes 1327104 | tf_op jit(solution)/shard_map/all_gather | solution.py:47
  8.9 179.4 %reduce-scatter.2.cloned.1.call-start = ((), (), s32[]{:S(2)}) async-start(), calls=%async_computation.1 | async-start | bytes 2654208 | tf_op jit(solution)/shard_map/reduce_scatter | solution.py:118
  35.6 29.1 %collective-permute-start = (bf16[8,96,768]{2,1,0:T(8,128)(2,1)}, bf16[8,96,768]{2,1,0:T(8,128)(2,1)}, u32[]{:S(2)}, u32[]{:S(2)}) collective-permute-start(bf16[8,96,768]{2,1,0:T(8,128)(2,1)} %bitcast.101), channel_id=1, source_target_pairs={{0,8},{8,0},{16,24},{24,16},{1,9},{9,1},{17,25},{25,17},{2,10},{10... | collective-permute-start | bytes 3538952 | tf_op jit(solution)/shard_map/ppermute | solution.py:41
  37.1 52.9 %collective-permute-start.1 = (bf16[8,96,768]{2,1,0:T(8,128)(2,1)}, bf16[8,96,768]{2,1,0:T(8,128)(2,1)}, u32[]{:S(2)}, u32[]{:S(2)}) collective-permute-start(bf16[8,96,768]{2,1,0:T(8,128)(2,1)} %bitcast.102), channel_id=1, source_target_pairs={{0,16},{8,24},{16,0},{24,8},{1,17},{9,25},{17,1},{25,9},{2,18},{10... | collective-permute-start | bytes 3538952 | tf_op jit(solution)/shard_map/ppermute | solution.py:41
  39.7 53.2 %collective-permute-start.2 = (bf16[8,96,768]{2,1,0:T(8,128)(2,1)}, bf16[8,96,768]{2,1,0:T(8,128)(2,1)}, u32[]{:S(2)}, u32[]{:S(2)}) collective-permute-start(bf16[8,96,768]{2,1,0:T(8,128)(2,1)} %bitcast.103), channel_id=1, source_target_pairs={{0,24},{8,16},{16,8},{24,0},{1,25},{9,17},{17,9},{25,1},{2,26},{10... | collective-permute-start | bytes 3538952 | tf_op jit(solution)/shard_map/ppermute | solution.py:41
  41.5 66.2 %collective-permute-start.7 = (bf16[256,768]{1,0:T(8,128)(2,1)S(1)}, bf16[256,768]{1,0:T(8,128)(2,1)}, u32[]{:S(2)}, u32[]{:S(2)}) collective-permute-start(bf16[256,768]{1,0:T(8,128)(2,1)S(1)} %fusion.38), channel_id=1, source_target_pairs={{0,8},{8,0},{16,24},{24,16},{1,9},{9,1},{17,25},{25,17},{2,10},{10... | collective-permute-start | bytes 1179656 | tf_op jit(solution)/shard_map/ppermute | solution.py:41
  43.0 69.7 %collective-permute-start.11 = (bf16[256,768]{1,0:T(8,128)(2,1)S(1)}, bf16[256,768]{1,0:T(8,128)(2,1)S(1)}, u32[]{:S(2)}, u32[]{:S(2)}) collective-permute-start(bf16[256,768]{1,0:T(8,128)(2,1)S(1)} %fusion.38), channel_id=1, source_target_pairs={{0,24},{8,16},{16,8},{24,0},{1,25},{9,17},{17,9},{25,1},{2,26},{10... | collective-permute-start | bytes 1179656 | tf_op jit(solution)/shard_map/ppermute | solution.py:41
  46.9 1.3 copy-start.4
  48.2 16.6 %copy-start.7 = (s32[1,256]{1,0:T(1,128)S(1)}, s32[1,256]{1,0:T(1,128)}, u32[]{:S(2)}) copy-start(s32[1,256]{1,0:T(1,128)} %param.9) | copy-start | bytes 3076
  64.7 41.5 %collective-permute-start.6 = (s32[256]{0:T(256)S(1)}, s32[256]{0:T(256)S(1)}, u32[]{:S(2)}, u32[]{:S(2)}) collective-permute-start(s32[256]{0:T(256)S(1)} %bitcast.105), channel_id=1, source_target_pairs={{0,8},{8,0},{16,24},{24,16},{1,9},{9,1},{17,25},{25,17},{2,10},{10... | collective-permute-start | bytes 3080 | tf_op jit(solution)/shard_map/ppermute | solution.py:41
  67.6 27.2 %copy-start.3 = (bf16[1,256,3072]{2,1,0:T(8,128)(2,1)S(1)}, bf16[1,256,3072]{2,1,0:T(8,128)(2,1)}, u32[]{:S(2)}) copy-start(bf16[1,256,3072]{2,1,0:T(8,128)(2,1)} %param.7) | copy-start | bytes 4718596
  90.0 22.1 %collective-permute-start.10 = (s32[256]{0:T(256)S(1)}, s32[256]{0:T(256)S(1)}, u32[]{:S(2)}, u32[]{:S(2)}) collective-permute-start(s32[256]{0:T(256)S(1)} %bitcast.106), channel_id=1, source_target_pairs={{0,24},{8,16},{16,8},{24,0},{1,25},{9,17},{17,9},{25,1},{2,26},{10... | collective-permute-start | bytes 3080 | tf_op jit(solution)/shard_map/ppermute | solution.py:41
  92.9 23.0 %collective-permute-start.9 = (bf16[256,768]{1,0:T(8,128)(2,1)S(1)}, bf16[256,768]{1,0:T(8,128)(2,1)S(1)}, u32[]{:S(2)}, u32[]{:S(2)}) collective-permute-start(bf16[256,768]{1,0:T(8,128)(2,1)S(1)} %fusion.38), channel_id=1, source_target_pairs={{0,16},{8,24},{16,0},{24,8},{1,17},{9,25},{17,1},{25,9},{2,18},{10... | collective-permute-start | bytes 1179656 | tf_op jit(solution)/shard_map/ppermute | solution.py:41
  96.8 10.9 %copy-start.5 = (f32[256,256]{0,1:T(8,128)}, f32[256,256]{0,1:T(8,128)S(1)}, u32[]{:S(2)}) copy-start(f32[256,256]{0,1:T(8,128)S(1)} %fusion.4) | copy-start | bytes 786436
  106.2 9.7 %collective-permute-start.8 = (s32[256]{0:T(256)S(1)}, s32[256]{0:T(256)S(1)}, u32[]{:S(2)}, u32[]{:S(2)}) collective-permute-start(s32[256]{0:T(256)S(1)} %bitcast.108), channel_id=1, source_target_pairs={{0,16},{8,24},{16,0},{24,8},{1,17},{9,25},{17,1},{25,9},{2,18},{10... | collective-permute-start | bytes 3080 | tf_op jit(solution)/shard_map/ppermute | solution.py:41
  107.7 12.4 %collective-permute-start.12 = (bf16[256,768]{1,0:T(8,128)(2,1)}, bf16[256,768]{1,0:T(8,128)(2,1)}, u32[]{:S(2)}, u32[]{:S(2)}) collective-permute-start(bf16[256,768]{1,0:T(8,128)(2,1)} %get-tuple-element.10), channel_id=1, source_target_pairs={{0,8},{8,0},{16,24},{24,16},{1,9},{9,1},{17,25},{25,17},{2,10},{10... | collective-permute-start | bytes 1179656 | tf_op jit(solution)/shard_map/ppermute | solution.py:41
  112.1 18.6 %collective-permute-start.13 = (bf16[256,768]{1,0:T(8,128)(2,1)}, bf16[256,768]{1,0:T(8,128)(2,1)}, u32[]{:S(2)}, u32[]{:S(2)}) collective-permute-start(bf16[256,768]{1,0:T(8,128)(2,1)} %get-tuple-element.11), channel_id=1, source_target_pairs={{0,16},{8,24},{16,0},{24,8},{1,17},{9,25},{17,1},{25,9},{2,18},{10... | collective-permute-start | bytes 1179656 | tf_op jit(solution)/shard_map/ppermute | solution.py:41
  112.7 18.0 %collective-permute-start.14 = (bf16[256,768]{1,0:T(8,128)(2,1)}, bf16[256,768]{1,0:T(8,128)(2,1)}, u32[]{:S(2)}, u32[]{:S(2)}) collective-permute-start(bf16[256,768]{1,0:T(8,128)(2,1)} %get-tuple-element.12), channel_id=1, source_target_pairs={{0,24},{8,16},{16,8},{24,0},{1,25},{9,17},{17,9},{25,1},{2,26},{10... | collective-permute-start | bytes 1179656 | tf_op jit(solution)/shard_map/ppermute | solution.py:41
  130.8 12.1 %collective-permute-start.15 = (bf16[256,768]{0,1:T(8,128)(2,1)S(1)}, bf16[256,768]{0,1:T(8,128)(2,1)S(1)}, u32[]{:S(2)}, u32[]{:S(2)}) collective-permute-start(bf16[256,768]{0,1:T(8,128)(2,1)S(1)} %fusion.47), channel_id=1, source_target_pairs={{0,8},{8,0},{16,24},{24,16},{1,9},{9,1},{17,25},{25,17},{2,10},{10... | collective-permute-start | bytes 1179656 | tf_op jit(solution)/shard_map/ppermute | solution.py:41
  131.4 17.1 %collective-permute-start.16 = (bf16[256,768]{0,1:T(8,128)(2,1)S(1)}, bf16[256,768]{0,1:T(8,128)(2,1)S(1)}, u32[]{:S(2)}, u32[]{:S(2)}) collective-permute-start(bf16[256,768]{0,1:T(8,128)(2,1)S(1)} %fusion.47), channel_id=1, source_target_pairs={{0,16},{8,24},{16,0},{24,8},{1,17},{9,25},{17,1},{25,9},{2,18},{10... | collective-permute-start | bytes 1179656 | tf_op jit(solution)/shard_map/ppermute | solution.py:41
  133.4 16.5 %collective-permute-start.17 = (bf16[256,768]{0,1:T(8,128)(2,1)S(1)}, bf16[256,768]{0,1:T(8,128)(2,1)S(1)}, u32[]{:S(2)}, u32[]{:S(2)}) collective-permute-start(bf16[256,768]{0,1:T(8,128)(2,1)S(1)} %fusion.47), channel_id=1, source_target_pairs={{0,24},{8,16},{16,8},{24,0},{1,25},{9,17},{17,9},{25,1},{2,26},{10... | collective-permute-start | bytes 1179656 | tf_op jit(solution)/shard_map/ppermute | solution.py:41
  152.9 3.6 %copy-start.6 = (f32[256,256]{0,1:T(8,128)S(1)}, f32[256,256]{0,1:T(8,128)}, u32[]{:S(2)}) copy-start(f32[256,256]{0,1:T(8,128)} %copy-done.5) | copy-start | bytes 786436
  153.0 11.6 %collective-permute-start.5 = (bf16[256,768]{0,1:T(8,128)(2,1)S(1)}, bf16[256,768]{0,1:T(8,128)(2,1)S(1)}, u32[]{:S(2)}, u32[]{:S(2)}) collective-permute-start(bf16[256,768]{0,1:T(8,128)(2,1)S(1)} %bitcast_convert_fusion), channel_id=1, source_target_pairs={{0,24},{8,16},{16,8},{24,0},{1,25},{9,17},{17,9},{25,1},{2,26},{10... | collective-permute-start | bytes 1179656 | tf_op jit(solution)/shard_map/ppermute | solution.py:41
  154.5 14.1 %collective-permute-start.4 = (bf16[256,768]{0,1:T(8,128)(2,1)S(1)}, bf16[256,768]{0,1:T(8,128)(2,1)S(1)}, u32[]{:S(2)}, u32[]{:S(2)}) collective-permute-start(bf16[256,768]{0,1:T(8,128)(2,1)S(1)} %bitcast_convert_fusion), channel_id=1, source_target_pairs={{0,16},{8,24},{16,0},{24,8},{1,17},{9,25},{17,1},{25,9},{2,18},{10... | collective-permute-start | bytes 1179656 | tf_op jit(solution)/shard_map/ppermute | solution.py:41
  155.9 13.0 %collective-permute-start.3 = (bf16[256,768]{0,1:T(8,128)(2,1)S(1)}, bf16[256,768]{0,1:T(8,128)(2,1)S(1)}, u32[]{:S(2)}, u32[]{:S(2)}) collective-permute-start(bf16[256,768]{0,1:T(8,128)(2,1)S(1)} %bitcast_convert_fusion), channel_id=1, source_target_pairs={{0,8},{8,0},{16,24},{24,16},{1,9},{9,1},{17,25},{25,17},{2,10},{10... | collective-permute-start | bytes 1179656 | tf_op jit(solution)/shard_map/ppermute | solution.py:41
  169.9 1.5 copy-start.1
Sparse Core Ops, SparseCore 0:
  10.2 25.3 all-gather.2
  153.1 35.1 reduce-scatter.1

commit v4 on v2

--- a/solution.py
+++ b/solution.py
@@ -75,22 +75,23 @@
 
     local = jnp.arange(row_count, dtype=jnp.int32)
 
+    image_group = jnp.concatenate(image_from, axis=0)
+    label_group = jnp.concatenate(label_from, axis=0)
+    hidden_group = jnp.concatenate(hidden_from, axis=0)
     own_columns = my_index * row_count + local
-    text_unit_grad = jnp.zeros(text_unit.shape, jnp.float32)
-    for k in range(blocks):
-        scores_t = lax.dot_general(
-            image_from[k], text_unit, (((1,), (1,)), ((), ())), preferred_element_type=jnp.float32
-        )
-        logits_t = multiplier_amount * scores_t + offset_value
-        pair_sign_t = jnp.where(label_from[k][:, None] == own_columns[None, :], 1.0, -1.0).astype(
-            jnp.float32
-        )
-        text_unit_grad = text_unit_grad + lax.dot_general(
-            weights_of(logits_t, pair_sign_t),
-            image_from[k],
-            (((0,), (0,)), ((), ())),
-            preferred_element_type=jnp.float32,
-        )
+    scores_t = lax.dot_general(
+        image_group, text_unit, (((1,), (1,)), ((), ())), preferred_element_type=jnp.float32
+    )
+    logits_t = multiplier_amount * scores_t + offset_value
+    pair_sign_t = jnp.where(label_group[:, None] == own_columns[None, :], 1.0, -1.0).astype(
+        jnp.float32
+    )
+    text_unit_grad = lax.dot_general(
+        weights_of(logits_t, pair_sign_t),
+        image_group,
+        (((0,), (0,)), ((), ())),
+        preferred_element_type=jnp.float32,
+    )
     projection_output_gradient = (
         text_scale
         * (text_unit_grad - text_dir * jnp.sum(text_dir * text_unit_grad, axis=1, keepdims=True))
@@ -98,11 +99,12 @@
     grad_from = [projection_output_gradient] + [
         exchange(projection_output_gradient, k) for k in range(1, blocks)
     ]
-    partial = jnp.zeros((chunk, projection_output_gradient.shape[1]), jnp.float32)
-    for k in range(blocks):
-        partial = partial + lax.dot_general(
-            hidden_from[k], grad_from[k], (((0,), (0,)), ((), ())), preferred_element_type=jnp.float32
-        )
+    partial = lax.dot_general(
+        hidden_group,
+        jnp.concatenate(grad_from, axis=0),
+        (((0,), (0,)), ((), ())),
+        preferred_element_type=jnp.float32,
+    )
     projection_grad = lax.psum_scatter(partial, "group", scatter_dimension=0, tiled=True)
 
     loss_local = jnp.zeros((row_count,), jnp.float32)

time: 148 us -> 139 us (0.939)
  matrix products: 23.9 us -> 14.6 us
  waiting for transfers between devices: 84.7 us -> 79.3 us
  local copies, waits for them, and re-layouts: 2.03 us -> 6.27 us
    all_gather x1, waiting for transfers between devices: 42.8 us -> 5.26 us  [body(): w_full = lax.all_gather(linear_map_matrix, 'group', axis=0, tiled=True)]
    ppermute x12, waiting for transfers between devices: 27.7 us -> 63.4 us  [exchange(): return lax.ppermute(value, 'blk', partner_pairs(blocks, step))]
    dot_general x8 -> x2, matrix products: 15.9 us -> 7.18 us  [the longest x1 4.31 us: body(): lax.dot_general(weights_of(logits_t, pair_sign_t), image_group, (((0,), (...]
    slice x0 -> x3, local copies, waits for them, and re-layouts: none -> 3.97 us  [body(): image_from.append(incoming[:, chunk:])]
    reduce_scatter x1, waiting for transfers between devices: 13.5 us -> 9.96 us  [body(): lax.psum_scatter(partial, 'group', scatter_dimension=0, tiled=True)]
  transfers between devices with their start and end apart: 14 -> 14, of which waited for: 6 -> 8; matrix products, arithmetic and copies ran while one was open for 16% -> 11% of each run, Pallas kernels for 0% -> 0%
where the time goes in v4:
time: 139 us; the launch traced here: 138 us
  waiting for transfers between devices  79.3 us (57%)
  starting transfers between devices  16.8 us (12%)
  between operations  15.5 us (11%)
  matrix products  14.6 us (11%)
  local copies, waits for them, and re-layouts  6.27 us (5%)
  other arithmetic  5.82 us (4%)
    ppermute x12, waiting for transfers between devices, exchange(): return lax.ppermute(value, 'blk', partner_pairs(blocks, step))  63.4 us
    ppermute x12, starting transfers between devices, exchange(): return lax.ppermute(value, 'blk', partner_pairs(blocks, step))  16.7 us
    reduce_scatter x1, waiting for transfers between devices, body(): lax.psum_scatter(partial, 'group', scatter_dimension=0, tiled=True)  9.96 us
    all_gather x1, waiting for transfers between devices, body(): w_full = lax.all_gather(linear_map_matrix, 'group', axis=0, tiled=True)  5.26 us
    dot_general x1, matrix products, body(): lax.dot_general(weights_of(logits_t, pair_sign_t), image_group, (((0,), (...  4.31 us
    slice x3, local copies, waits for them, and re-layouts, body(): image_from.append(incoming[:, chunk:])  3.97 us
    dot_general x1, matrix products, body(): projected = jnp.dot(hidden_rows, w_full, preferred_element_type=jnp.float32)  3.79 us
    dot_general x1, matrix products, body(): lax.dot_general(hidden_group, jnp.concatenate(grad_from, axis=0), (((0,),...  2.87 us
  transfers between devices with their start and end apart: 14, of which 8 were waited for; matrix products, arithmetic and copies ran while one was open for 11% of the time, Pallas kernels for 0%

profile of v4, /device:TPU:0, one launch (start us, length us, event | category | flops | bytes accessed | tf_op | source)
XLA Modules:
  0.0 138.3 jit_solution(1702687966365194213)
XLA Ops:
  7.2 0.0 all-gather.2.cloned.1.call-start
  7.2 0.7 all-gather.2.cloned.1.call-update
  7.9 0.0 reduce-scatter.2.cloned.1.call-start
  8.0 1.2 fusion.42
  9.1 0.0 copy-start
  9.1 2.3 %dynamic-slice_bitcast_fusion.3 = (bf16[256,768]{1,0:T(8,128)(2,1)}, bf16[256,768]{1,0:T(8,128)(2,1)S(1)}, bf16[256,768]{1,0:T(8,128)(2,1)S(1)}, bf16[256,768]{1,0:T(8,128)(2,1)S(1)}) fusion(bf16[1,256,3072]{2,1,0:T(8,128)(2,1)} %param.7, s32[]{:T(128)S(6)} %select_n.51, s32[]{:T(128)S(6)} %select_n.52, s32[]{:T(128)S(6)} %select_n.54, s32[]{:T(128)S(6)} %select_n.53), kind=kLoop, calls=%fused_computation.74 | loop fusion | bytes 3145744 | tf_op jit(solution)/shard_map/dynamic_slice | solution.py:51
  11.4 0.0 copy-done
  11.4 0.1 fusion.37
  11.5 0.0 copy-start.5
  11.6 1.3 pad_maximum_fusion.5
  12.9 3.9 %collective-permute-start.5 = (bf16[256,1536]{1,0:T(8,128)(2,1)S(1)}, bf16[256,1536]{1,0:T(8,128)(2,1)S(1)}, u32[]{:S(2)}, u32[]{:S(2)}) collective-permute-start(bf16[256,1536]{1,0:T(8,128)(2,1)S(1)} %get-tuple-element.19), channel_id=1, source_target_pairs={{0,24},{8,16},{16,8},{24,0},{1,25},{9,17},{17,9},{25,1},{2,26},{10... | collective-permute-start | bytes 2359304 | tf_op jit(solution)/shard_map/ppermute | solution.py:41
  16.8 0.5 collective-permute-start.4
  17.3 0.1 collective-permute-start.3
  17.4 0.0 copy-done.5
  17.4 2.9 %collective-permute-start.8 = (s32[256]{0:T(256)S(1)}, s32[256]{0:T(256)S(1)}, u32[]{:S(2)}, u32[]{:S(2)}) collective-permute-start(s32[256]{0:T(256)S(1)} %bitcast.53), channel_id=1, source_target_pairs={{0,24},{8,16},{16,8},{24,0},{1,25},{9,17},{17,9},{25,1},{2,26},{10... | collective-permute-start | bytes 3080 | tf_op jit(solution)/shard_map/ppermute | solution.py:41
  20.3 0.5 collective-permute-start.7
  20.8 30.5 %collective-permute-done.8 = s32[256]{0:T(256)S(1)} collective-permute-done((s32[256]{0:T(256)S(1)}, s32[256]{0:T(256)S(1)}, u32[]{:S(2)}, u32[]{:S(2)}) %collective-permute-start.8) | collective-permute-done | bytes 1056 | tf_op jit(solution)/shard_map/ppermute | solution.py:41
  51.2 1.7 %collective-permute-start.6 = (s32[256]{0:T(256)S(1)}, s32[256]{0:T(256)S(1)}, u32[]{:S(2)}, u32[]{:S(2)}) collective-permute-start(s32[256]{0:T(256)S(1)} %bitcast.55), channel_id=1, source_target_pairs={{0,8},{8,0},{16,24},{24,16},{1,9},{9,1},{17,25},{25,17},{2,10},{10... | collective-permute-start | bytes 3080 | tf_op jit(solution)/shard_map/ppermute | solution.py:41
  52.9 0.6 iota_add_fusion.3
  54.8 0.0 collective-permute-done.7
  54.8 0.0 collective-permute-done.6
  54.8 0.0 collective-permute-done.5
  54.8 0.8 fusion.131
  55.6 0.0 copy-start.1
  55.6 0.0 collective-permute-done.4
  55.6 2.2 %fusion.130 = (bf16[256,768]{1,0:T(8,128)(2,1)}, bf16[256,768]{1,0:T(8,128)(2,1)}) fusion(bf16[256,1536]{1,0:T(8,128)(2,1)} %collective-permute-done.4), kind=kLoop, calls=%fused_computation.166 | loop fusion | bytes 1572864 | tf_op jit(solution)/shard_map/slice | solution.py:62
  57.8 0.0 collective-permute-done.3
  57.8 1.0 fusion.129
  58.8 5.3 %all-gather.2.cloned.1.call-done = bf16[3072,768]{1,0:T(8,128)(2,1)} async-done(((bf16[384,768]{1,0:T(8,128)(2,1)}), bf16[3072,768]{1,0:T(8,128)(2,1)}) %all-gather.2.cloned.1.call-update) | async-done | bytes 4718608 | tf_op jit(solution)/shard_map/all_gather | solution.py:43
  64.1 0.0 copy-done.1
  64.1 3.8 %multiply_reduce_fusion.1 = (f32[256]{0:T(256)S(1)}, f32[256,768]{1,0:T(8,128)S(1)}) fusion(bf16[3072,768]{1,0:T(8,128)(2,1)} %all-gather.2.cloned.1.call-done, bf16[1,256,3072]{2,1,0:T(8,128)(2,1)S(1)} %copy-done.1), kind=kOutput, calls=%fused_computation.58 | convolution fusion | flops 1208352512 | bytes 7078912 | tf_op jit(solution)/shard_map/dot_general | solution.py:65
  67.9 0.1 multiply_convert_fusion.1
  68.0 4.3 %multiply_reduce_fusion = (f32[256]{0:T(256)}, f32[256,768]{1,0:T(8,128)S(1)}) fusion(f32[256,768]{1,0:T(8,128)S(1)} %get-tuple-element.21, f32[256]{0:T(256)S(1)} %add_rsqrt_fusion, bf16[256,768]{1,0:T(8,128)(2,1)} %get-tuple-element.15, bf16[256,768]{1,0:T(8,128)(2,1)} %get-tuple-element.13, bf16[256,768]{1,0:T(8,128)(2,1)} %get-tuple-element.11, ...), kind=kOutput, calls=%fused_computation.57 | convolution fusion | flops 821624576 | bytes 3546120 | tf_op jit(solution)/shard_map/dot_general | solution.py:89
  72.3 0.0 copy-start.2
  72.3 1.0 multiply_convert_fusion
  73.3 2.4 %collective-permute-start.11 = (bf16[256,768]{1,0:T(8,128)(2,1)S(1)}, bf16[256,768]{1,0:T(8,128)(2,1)S(1)}, u32[]{:S(2)}, u32[]{:S(2)}) collective-permute-start(bf16[256,768]{1,0:T(8,128)(2,1)S(1)} %multiply_convert_fusion), channel_id=1, source_target_pairs={{0,24},{8,16},{16,8},{24,0},{1,25},{9,17},{17,9},{25,1},{2,26},{10... | collective-permute-start | bytes 1179656 | tf_op jit(solution)/shard_map/ppermute | solution.py:41
  75.7 0.6 collective-permute-start.10
  76.3 0.6 collective-permute-start.9
  76.9 9.4 %collective-permute-done.11 = bf16[256,768]{1,0:T(8,128)(2,1)S(1)} collective-permute-done((bf16[256,768]{1,0:T(8,128)(2,1)S(1)}, bf16[256,768]{1,0:T(8,128)(2,1)S(1)}, u32[]{:S(2)}, u32[]{:S(2)}) %collective-permute-start.11) | collective-permute-done | bytes 393248 | tf_op jit(solution)/shard_map/ppermute | solution.py:41
  86.3 7.7 %collective-permute-done.10 = bf16[256,768]{1,0:T(8,128)(2,1)S(1)} collective-permute-done((bf16[256,768]{1,0:T(8,128)(2,1)S(1)}, bf16[256,768]{1,0:T(8,128)(2,1)S(1)}, u32[]{:S(2)}, u32[]{:S(2)}) %collective-permute-start.10) | collective-permute-done | bytes 393248 | tf_op jit(solution)/shard_map/ppermute | solution.py:41
  93.9 0.1 collective-permute-done.9
  94.0 0.0 copy-done.2
  94.0 0.0 copy-done.3
  94.0 0.0 copy-done.4
  94.0 2.9 %fusion = f32[768,768]{1,0:T(8,128)} fusion(bf16[256,768]{1,0:T(8,128)(2,1)S(1)} %get-tuple-element.16, bf16[256,768]{1,0:T(8,128)(2,1)S(1)} %copy-done.2, bf16[256,768]{1,0:T(8,128)(2,1)S(1)} %copy-done.3, bf16[256,768]{1,0:T(8,128)(2,1)S(1)} %copy-done.4, bf16[256,768]{1,0:T(8,128)(2,1)S(1)} %collective-permute-done.11, ...), kind=kOutput, calls=%fused_computation | convolution fusion | flops 1220542464 | bytes 5505024 | tf_op jit(solution)/shard_map/dot_general | solution.py:102
  96.9 0.0 reduce-scatter.2.cloned.1.call-update
  96.9 1.5 %collective-permute-start.1 = (bf16[256,768]{1,0:T(8,128)(2,1)S(1)}, bf16[256,768]{1,0:T(8,128)(2,1)S(1)}, u32[]{:S(2)}, u32[]{:S(2)}) collective-permute-start(bf16[256,768]{1,0:T(8,128)(2,1)S(1)} %multiply_convert_fusion.1), channel_id=1, source_target_pairs={{0,16},{8,24},{16,0},{24,8},{1,17},{9,25},{17,1},{25,9},{2,18},{10... | collective-permute-start | bytes 1179656 | tf_op jit(solution)/shard_map/ppermute | solution.py:41
  98.4 1.5 %collective-permute-start.2 = (bf16[256,768]{1,0:T(8,128)(2,1)S(1)}, bf16[256,768]{1,0:T(8,128)(2,1)S(1)}, u32[]{:S(2)}, u32[]{:S(2)}) collective-permute-start(bf16[256,768]{1,0:T(8,128)(2,1)S(1)} %multiply_convert_fusion.1), channel_id=1, source_target_pairs={{0,24},{8,16},{16,8},{24,0},{1,25},{9,17},{17,9},{25,1},{2,26},{10... | collective-permute-start | bytes 1179656 | tf_op jit(solution)/shard_map/ppermute | solution.py:41
  99.9 0.6 collective-permute-start
  100.5 0.3 fusion.27
  100.8 0.0 copy-done.6
  100.8 0.4 fusion.90
  101.3 15.2 %collective-permute-done.1 = bf16[256,768]{1,0:T(8,128)(2,1)S(1)} collective-permute-done((bf16[256,768]{1,0:T(8,128)(2,1)S(1)}, bf16[256,768]{1,0:T(8,128)(2,1)S(1)}, u32[]{:S(2)}, u32[]{:S(2)}) %collective-permute-start.1) | collective-permute-done | bytes 393248 | tf_op jit(solution)/shard_map/ppermute | solution.py:41
  116.4 0.3 fusion.29
  116.7 0.0 collective-permute-done.2
  116.7 0.3 fusion.30
  117.0 0.6 collective-permute-done
  117.7 0.9 fusion.83
  118.5 0.6 add_add_fusion
  119.1 0.4 fusion.94
  119.6 0.4 convolution_add_fusion.1
  120.0 0.5 fusion.38
  120.6 1.0 fusion.49
  121.5 10.0 %reduce-scatter.2.cloned.1.call-done = f32[96,768]{1,0:T(8,128)} async-done(((f32[768,768]{1,0:T(8,128)}), f32[96,768]{1,0:T(8,128)}) %reduce-scatter.2.cloned.1.call-update) | async-done | bytes 294928 | tf_op jit(solution)/shard_map/reduce_scatter | solution.py:108
  (8 shorter events, 0.0 us)
Async XLA Ops:
  7.2 56.9 %all-gather.2.cloned.1.call-start = ((), (), s32[]{:S(2)}) async-start(), calls=%async_computation.1 | async-start | bytes 5308416 | tf_op jit(solution)/shard_map/all_gather | solution.py:43
  7.9 123.6 %reduce-scatter.2.cloned.1.call-start = ((), (), s32[]{:S(2)}) async-start(), calls=%async_computation.2 | async-start | bytes 2654208 | tf_op jit(solution)/shard_map/reduce_scatter | solution.py:108
  9.1 2.3 %copy-start = (bf16[1,256,768]{2,1,0:T(8,128)(2,1)S(1)}, bf16[1,256,768]{2,1,0:T(8,128)(2,1)}, u32[]{:S(2)}) copy-start(bf16[1,256,768]{2,1,0:T(8,128)(2,1)} %param.6) | copy-start | bytes 1179652
  11.5 5.8 %copy-start.5 = (s32[1,256]{1,0:T(1,128)S(1)}, s32[1,256]{1,0:T(1,128)}, u32[]{:S(2)}) copy-start(s32[1,256]{1,0:T(1,128)} %param.9) | copy-start | bytes 3076
  12.9 41.9 %collective-permute-start.5 = (bf16[256,1536]{1,0:T(8,128)(2,1)S(1)}, bf16[256,1536]{1,0:T(8,128)(2,1)S(1)}, u32[]{:S(2)}, u32[]{:S(2)}) collective-permute-start(bf16[256,1536]{1,0:T(8,128)(2,1)S(1)} %get-tuple-element.19), channel_id=1, source_target_pairs={{0,24},{8,16},{16,8},{24,0},{1,25},{9,17},{17,9},{25,1},{2,26},{10... | collective-permute-start | bytes 2359304 | tf_op jit(solution)/shard_map/ppermute | solution.py:41
  16.8 38.9 %collective-permute-start.4 = (bf16[256,1536]{1,0:T(8,128)(2,1)}, bf16[256,1536]{1,0:T(8,128)(2,1)}, u32[]{:S(2)}, u32[]{:S(2)}) collective-permute-start(bf16[256,1536]{1,0:T(8,128)(2,1)} %get-tuple-element.18), channel_id=1, source_target_pairs={{0,16},{8,24},{16,0},{24,8},{1,17},{9,25},{17,1},{25,9},{2,18},{10... | collective-permute-start | bytes 2359304 | tf_op jit(solution)/shard_map/ppermute | solution.py:41
  17.3 40.5 %collective-permute-start.3 = (bf16[256,1536]{1,0:T(8,128)(2,1)}, bf16[256,1536]{1,0:T(8,128)(2,1)S(1)}, u32[]{:S(2)}, u32[]{:S(2)}) collective-permute-start(bf16[256,1536]{1,0:T(8,128)(2,1)} %get-tuple-element.17), channel_id=1, source_target_pairs={{0,8},{8,0},{16,24},{24,16},{1,9},{9,1},{17,25},{25,17},{2,10},{10... | collective-permute-start | bytes 2359304 | tf_op jit(solution)/shard_map/ppermute | solution.py:41
  17.4 33.9 %collective-permute-start.8 = (s32[256]{0:T(256)S(1)}, s32[256]{0:T(256)S(1)}, u32[]{:S(2)}, u32[]{:S(2)}) collective-permute-start(s32[256]{0:T(256)S(1)} %bitcast.53), channel_id=1, source_target_pairs={{0,24},{8,16},{16,8},{24,0},{1,25},{9,17},{17,9},{25,1},{2,26},{10... | collective-permute-start | bytes 3080 | tf_op jit(solution)/shard_map/ppermute | solution.py:41
  20.3 34.5 %collective-permute-start.7 = (s32[256]{0:T(256)S(1)}, s32[256]{0:T(256)S(1)}, u32[]{:S(2)}, u32[]{:S(2)}) collective-permute-start(s32[256]{0:T(256)S(1)} %bitcast.54), channel_id=1, source_target_pairs={{0,16},{8,24},{16,0},{24,8},{1,17},{9,25},{17,1},{25,9},{2,18},{10... | collective-permute-start | bytes 3080 | tf_op jit(solution)/shard_map/ppermute | solution.py:41
  51.2 3.6 %collective-permute-start.6 = (s32[256]{0:T(256)S(1)}, s32[256]{0:T(256)S(1)}, u32[]{:S(2)}, u32[]{:S(2)}) collective-permute-start(s32[256]{0:T(256)S(1)} %bitcast.55), channel_id=1, source_target_pairs={{0,8},{8,0},{16,24},{24,16},{1,9},{9,1},{17,25},{25,17},{2,10},{10... | collective-permute-start | bytes 3080 | tf_op jit(solution)/shard_map/ppermute | solution.py:41
  55.6 8.4 %copy-start.1 = (bf16[1,256,3072]{2,1,0:T(8,128)(2,1)S(1)}, bf16[1,256,3072]{2,1,0:T(8,128)(2,1)}, u32[]{:S(2)}) copy-start(bf16[1,256,3072]{2,1,0:T(8,128)(2,1)} %param.7) | copy-start | bytes 4718596
  72.3 21.7 %copy-start.2 = (bf16[256,768]{1,0:T(8,128)(2,1)S(1)}, bf16[256,768]{1,0:T(8,128)(2,1)}, u32[]{:S(2)}) copy-start(bf16[256,768]{1,0:T(8,128)(2,1)} %get-tuple-element.14) | copy-start | bytes 1179652
  72.3 21.7 %copy-start.3 = (bf16[256,768]{1,0:T(8,128)(2,1)S(1)}, bf16[256,768]{1,0:T(8,128)(2,1)}, u32[]{:S(2)}) copy-start(bf16[256,768]{1,0:T(8,128)(2,1)} %get-tuple-element.12) | copy-start | bytes 1179652
  72.3 21.7 %copy-start.4 = (bf16[256,768]{1,0:T(8,128)(2,1)S(1)}, bf16[256,768]{1,0:T(8,128)(2,1)}, u32[]{:S(2)}) copy-start(bf16[256,768]{1,0:T(8,128)(2,1)} %get-tuple-element.7) | copy-start | bytes 1179652
  73.3 13.0 %collective-permute-start.11 = (bf16[256,768]{1,0:T(8,128)(2,1)S(1)}, bf16[256,768]{1,0:T(8,128)(2,1)S(1)}, u32[]{:S(2)}, u32[]{:S(2)}) collective-permute-start(bf16[256,768]{1,0:T(8,128)(2,1)S(1)} %multiply_convert_fusion), channel_id=1, source_target_pairs={{0,24},{8,16},{16,8},{24,0},{1,25},{9,17},{17,9},{25,1},{2,26},{10... | collective-permute-start | bytes 1179656 | tf_op jit(solution)/shard_map/ppermute | solution.py:41
  75.7 18.2 %collective-permute-start.10 = (bf16[256,768]{1,0:T(8,128)(2,1)S(1)}, bf16[256,768]{1,0:T(8,128)(2,1)S(1)}, u32[]{:S(2)}, u32[]{:S(2)}) collective-permute-start(bf16[256,768]{1,0:T(8,128)(2,1)S(1)} %multiply_convert_fusion), channel_id=1, source_target_pairs={{0,16},{8,24},{16,0},{24,8},{1,17},{9,25},{17,1},{25,9},{2,18},{10... | collective-permute-start | bytes 1179656 | tf_op jit(solution)/shard_map/ppermute | solution.py:41
  76.3 17.7 %collective-permute-start.9 = (bf16[256,768]{1,0:T(8,128)(2,1)S(1)}, bf16[256,768]{1,0:T(8,128)(2,1)S(1)}, u32[]{:S(2)}, u32[]{:S(2)}) collective-permute-start(bf16[256,768]{1,0:T(8,128)(2,1)S(1)} %multiply_convert_fusion), channel_id=1, source_target_pairs={{0,8},{8,0},{16,24},{24,16},{1,9},{9,1},{17,25},{25,17},{2,10},{10... | collective-permute-start | bytes 1179656 | tf_op jit(solution)/shard_map/ppermute | solution.py:41
  96.9 3.9 %copy-start.6 = (s32[256]{0:T(256)S(1)}, s32[256]{0:T(256)}, u32[]{:S(2)}) copy-start(s32[256]{0:T(256)} %iota_add_fusion.3) | copy-start | bytes 3076
  96.9 19.5 %collective-permute-start.1 = (bf16[256,768]{1,0:T(8,128)(2,1)S(1)}, bf16[256,768]{1,0:T(8,128)(2,1)S(1)}, u32[]{:S(2)}, u32[]{:S(2)}) collective-permute-start(bf16[256,768]{1,0:T(8,128)(2,1)S(1)} %multiply_convert_fusion.1), channel_id=1, source_target_pairs={{0,16},{8,24},{16,0},{24,8},{1,17},{9,25},{17,1},{25,9},{2,18},{10... | collective-permute-start | bytes 1179656 | tf_op jit(solution)/shard_map/ppermute | solution.py:41
  98.4 18.3 %collective-permute-start.2 = (bf16[256,768]{1,0:T(8,128)(2,1)S(1)}, bf16[256,768]{1,0:T(8,128)(2,1)S(1)}, u32[]{:S(2)}, u32[]{:S(2)}) collective-permute-start(bf16[256,768]{1,0:T(8,128)(2,1)S(1)} %multiply_convert_fusion.1), channel_id=1, source_target_pairs={{0,24},{8,16},{16,8},{24,0},{1,25},{9,17},{17,9},{25,1},{2,26},{10... | collective-permute-start | bytes 1179656 | tf_op jit(solution)/shard_map/ppermute | solution.py:41
  99.9 17.7 %collective-permute-start = (bf16[256,768]{1,0:T(8,128)(2,1)S(1)}, bf16[256,768]{1,0:T(8,128)(2,1)S(1)}, u32[]{:S(2)}, u32[]{:S(2)}) collective-permute-start(bf16[256,768]{1,0:T(8,128)(2,1)S(1)} %multiply_convert_fusion.1), channel_id=1, source_target_pairs={{0,8},{8,0},{16,24},{24,16},{1,9},{9,1},{17,25},{25,17},{2,10},{10... | collective-permute-start | bytes 1179656 | tf_op jit(solution)/shard_map/ppermute | solution.py:41
Sparse Core Ops, SparseCore 0:
  9.6 54.3 all-gather.1
  97.0 34.4 reduce-scatter.1

commit v5 on v2

--- a/solution.py
+++ b/solution.py
@@ -75,34 +75,44 @@
 
     local = jnp.arange(row_count, dtype=jnp.int32)
 
-    own_columns = my_index * row_count + local
-    text_unit_grad = jnp.zeros(text_unit.shape, jnp.float32)
-    for k in range(blocks):
+    image_group = jnp.concatenate(image_from, axis=0)
+    label_group = jnp.concatenate(label_from, axis=0)
+    halves = 2 if row_count % 16 == 0 else 1
+    half_rows = row_count // halves
+    partial = None
+    for h in range(halves):
+        rows = slice(h * half_rows, (h + 1) * half_rows)
+        text_part = text_unit[rows]
+        dir_part = text_dir[rows]
+        own_columns = my_index * row_count + h * half_rows + local[:half_rows]
         scores_t = lax.dot_general(
-            image_from[k], text_unit, (((1,), (1,)), ((), ())), preferred_element_type=jnp.float32
+            image_group, text_part, (((1,), (1,)), ((), ())), preferred_element_type=jnp.float32
         )
         logits_t = multiplier_amount * scores_t + offset_value
-        pair_sign_t = jnp.where(label_from[k][:, None] == own_columns[None, :], 1.0, -1.0).astype(
+        pair_sign_t = jnp.where(label_group[:, None] == own_columns[None, :], 1.0, -1.0).astype(
             jnp.float32
         )
-        text_unit_grad = text_unit_grad + lax.dot_general(
+        text_unit_grad = lax.dot_general(
             weights_of(logits_t, pair_sign_t),
-            image_from[k],
+            image_group,
             (((0,), (0,)), ((), ())),
             preferred_element_type=jnp.float32,
         )
-    projection_output_gradient = (
-        text_scale
-        * (text_unit_grad - text_dir * jnp.sum(text_dir * text_unit_grad, axis=1, keepdims=True))
-    ).astype(jnp.bfloat16)
-    grad_from = [projection_output_gradient] + [
-        exchange(projection_output_gradient, k) for k in range(1, blocks)
-    ]
-    partial = jnp.zeros((chunk, projection_output_gradient.shape[1]), jnp.float32)
-    for k in range(blocks):
-        partial = partial + lax.dot_general(
-            hidden_from[k], grad_from[k], (((0,), (0,)), ((), ())), preferred_element_type=jnp.float32
+        projection_output_gradient = (
+            text_scale[rows]
+            * (text_unit_grad - dir_part * jnp.sum(dir_part * text_unit_grad, axis=1, keepdims=True))
+        ).astype(jnp.bfloat16)
+        grad_from = [projection_output_gradient] + [
+            exchange(projection_output_gradient, k) for k in range(1, blocks)
+        ]
+        hidden_part = jnp.concatenate([block[rows] for block in hidden_from], axis=0)
+        term = lax.dot_general(
+            hidden_part,
+            jnp.concatenate(grad_from, axis=0),
+            (((0,), (0,)), ((), ())),
+            preferred_element_type=jnp.float32,
         )
+        partial = term if partial is None else partial + term
     projection_grad = lax.psum_scatter(partial, "group", scatter_dimension=0, tiled=True)
 
     loss_local = jnp.zeros((row_count,), jnp.float32)

time: 148 us -> 144 us (0.973)
  waiting for transfers between devices: 84.7 us -> 73.2 us
  local copies, waits for them, and re-layouts: 2.03 us -> 9.59 us
  matrix products: 23.9 us -> 17.5 us
  starting transfers between devices: 16.6 us -> 20.9 us
    all_gather x1, waiting for transfers between devices: 42.8 us -> 4.05 us  [body(): w_full = lax.all_gather(linear_map_matrix, 'group', axis=0, tiled=True)]
    ppermute x12 -> x15, waiting for transfers between devices: 27.7 us -> 57.9 us  [exchange(): return lax.ppermute(value, 'blk', partner_pairs(blocks, step))]
    slice x0 -> x8, local copies, waits for them, and re-layouts: none -> 7.76 us  [the longest x4 3.68 us: body(): block[rows]]
    dot_general x8 -> x4, matrix products: 15.9 us -> 10 us  [the longest x2 6.91 us: body(): lax.dot_general(weights_of(logits_t, pair_sign_t), image_group, (((0,), (...]
    ppermute x12 -> x15, starting transfers between devices: 16.5 us -> 20.9 us  [exchange(): return lax.ppermute(value, 'blk', partner_pairs(blocks, step))]
    reduce_scatter x1, waiting for transfers between devices: 13.5 us -> 10.5 us  [body(): lax.psum_scatter(partial, 'group', scatter_dimension=0, tiled=True)]
  transfers between devices with their start and end apart: 14 -> 17, of which waited for: 6 -> 8; matrix products, arithmetic and copies ran while one was open for 16% -> 13% of each run, Pallas kernels for 0% -> 0%
where the time goes in v5:
time: 144 us; the launch traced here: 143 us
  waiting for transfers between devices  73.2 us (51%)
  starting transfers between devices  20.9 us (15%)
  matrix products  17.5 us (12%)
  between operations  15.6 us (11%)
  local copies, waits for them, and re-layouts  9.59 us (7%)
  other arithmetic  6.42 us (4%)
    ppermute x15, waiting for transfers between devices, exchange(): return lax.ppermute(value, 'blk', partner_pairs(blocks, step))  57.9 us
    ppermute x15, starting transfers between devices, exchange(): return lax.ppermute(value, 'blk', partner_pairs(blocks, step))  20.9 us
    reduce_scatter x1, waiting for transfers between devices, body(): lax.psum_scatter(partial, 'group', scatter_dimension=0, tiled=True)  10.5 us
    dot_general x2, matrix products, body(): lax.dot_general(weights_of(logits_t, pair_sign_t), image_group, (((0,), (...  6.91 us
    all_gather x1, waiting for transfers between devices, body(): w_full = lax.all_gather(linear_map_matrix, 'group', axis=0, tiled=True)  4.05 us
    dot_general x1, matrix products, body(): projected = jnp.dot(hidden_rows, w_full, preferred_element_type=jnp.float32)  3.79 us
    slice x4, local copies, waits for them, and re-layouts, body(): block[rows]  3.68 us
    slice x3, local copies, waits for them, and re-layouts, body(): image_from.append(incoming[:, chunk:])  3.56 us
  transfers between devices with their start and end apart: 17, of which 8 were waited for; matrix products, arithmetic and copies ran while one was open for 13% of the time, Pallas kernels for 0%

profile of v5, /device:TPU:0, one launch (start us, length us, event | category | flops | bytes accessed | tf_op | source)
XLA Modules:
  0.0 143.2 jit_solution(10152741893392448722)
XLA Ops:
  7.2 0.0 all-gather.2.cloned.1.call-start
  7.2 0.7 all-gather.2.cloned.1.call-update
  7.9 0.0 reduce-scatter.2.cloned.1.call-start
  8.0 1.2 fusion.34
  9.1 1.3 dynamic-slice_bitcast_fusion.2
  10.5 0.1 fusion.29
  10.6 0.0 copy-start.7
  10.6 0.0 copy-start.1
  10.6 1.5 %pad_maximum_fusion.3 = (bf16[256,1536]{1,0:T(8,128)(2,1)}, bf16[256,1536]{1,0:T(8,128)(2,1)}, bf16[256,1536]{1,0:T(8,128)(2,1)}) fusion(bf16[256,768]{1,0:T(8,128)(2,1)S(1)} %fusion.29, bf16[256,768]{1,0:T(8,128)(2,1)S(1)} %get-tuple-element.13, bf16[256,768]{1,0:T(8,128)(2,1)S(1)} %get-tuple-element.15, bf16[256,768]{1,0:T(8,128)(2,1)S(1)} %get-tuple-element.14), kind=kLoop, calls=%fused_computation.39 | loop fusion | flops 3932160 | bytes 3932160 | tf_op jit(solution)/shard_map/concatenate | solution.py:57
  12.2 2.9 %collective-permute-start.3 = (bf16[256,1536]{1,0:T(8,128)(2,1)}, bf16[256,1536]{1,0:T(8,128)(2,1)}, u32[]{:S(2)}, u32[]{:S(2)}) collective-permute-start(bf16[256,1536]{1,0:T(8,128)(2,1)} %get-tuple-element.24), channel_id=1, source_target_pairs={{0,8},{8,0},{16,24},{24,16},{1,9},{9,1},{17,25},{25,17},{2,10},{10... | collective-permute-start | bytes 2359304 | tf_op jit(solution)/shard_map/ppermute | solution.py:41
  15.1 1.5 %collective-permute-start.4 = (bf16[256,1536]{1,0:T(8,128)(2,1)}, bf16[256,1536]{1,0:T(8,128)(2,1)}, u32[]{:S(2)}, u32[]{:S(2)}) collective-permute-start(bf16[256,1536]{1,0:T(8,128)(2,1)} %get-tuple-element.25), channel_id=1, source_target_pairs={{0,16},{8,24},{16,0},{24,8},{1,17},{9,25},{17,1},{25,9},{2,18},{10... | collective-permute-start | bytes 2359304 | tf_op jit(solution)/shard_map/ppermute | solution.py:41
  16.7 0.0 collective-permute-start.5
  16.7 2.9 %collective-permute-start.8 = (s32[256]{0:T(256)S(1)}, s32[256]{0:T(256)S(1)}, u32[]{:S(2)}, u32[]{:S(2)}) collective-permute-start(s32[256]{0:T(256)S(1)} %bitcast.56), channel_id=1, source_target_pairs={{0,24},{8,16},{16,8},{24,0},{1,25},{9,17},{17,9},{25,1},{2,26},{10... | collective-permute-start | bytes 3080 | tf_op jit(solution)/shard_map/ppermute | solution.py:41
  19.6 0.5 collective-permute-start.7
  20.1 0.5 slice_add_fusion.1
  20.6 30.5 %collective-permute-done.8 = s32[256]{0:T(256)S(1)} collective-permute-done((s32[256]{0:T(256)S(1)}, s32[256]{0:T(256)S(1)}, u32[]{:S(2)}, u32[]{:S(2)}) %collective-permute-start.8) | collective-permute-done | bytes 1056 | tf_op jit(solution)/shard_map/ppermute | solution.py:41
  51.1 1.4 collective-permute-start.6
  52.5 0.8 dynamic-slice_bitcast_fusion.4
  54.6 0.0 collective-permute-done.6
  54.7 0.0 collective-permute-done.3
  54.7 1.0 slice.97
  55.7 0.0 collective-permute-done.4
  55.7 1.8 %slice.98 = bf16[256,768]{1,0:T(8,128)(2,1)} slice(bf16[256,1536]{1,0:T(8,128)(2,1)} %collective-permute-done.4), slice={[0:256], [768:1536]} | slice | bytes 786432 | tf_op jit(solution)/shard_map/slice | solution.py:62
  57.5 0.8 slice.99
  58.3 1.8 %fusion.172 = (bf16[128,768]{1,0:T(8,128)(2,1)}, bf16[128,768]{1,0:T(8,128)(2,1)}) fusion(bf16[256,1536]{1,0:T(8,128)(2,1)} %collective-permute-done.3), kind=kLoop, calls=%fused_computation.212 | loop fusion | bytes 786432 | tf_op jit(solution)/shard_map/slice | solution.py:108
  60.0 4.0 %all-gather.2.cloned.1.call-done = bf16[3072,768]{1,0:T(8,128)(2,1)} async-done(((bf16[384,768]{1,0:T(8,128)(2,1)}), bf16[3072,768]{1,0:T(8,128)(2,1)}) %all-gather.2.cloned.1.call-update) | async-done | bytes 4718608 | tf_op jit(solution)/shard_map/all_gather | solution.py:43
  64.1 3.8 %multiply_reduce_fusion = (f32[256]{0:T(256)S(1)}, f32[256,768]{1,0:T(8,128)S(1)}) fusion(bf16[3072,768]{1,0:T(8,128)(2,1)} %all-gather.2.cloned.1.call-done, bf16[1,256,3072]{2,1,0:T(8,128)(2,1)S(1)} %copy-done.1), kind=kOutput, calls=%fused_computation.79 | convolution fusion | flops 1208352512 | bytes 7078912 | tf_op jit(solution)/shard_map/dot_general | solution.py:65
  67.9 0.5 fusion.175
  68.4 0.1 fusion.171
  68.6 0.3 copy-done.2
  68.9 3.1 %fusion.26 = f32[128,768]{1,0:T(8,128)} fusion(bf16[256,768]{1,0:T(8,128)(2,1)} %slice.99, bf16[256,768]{1,0:T(8,128)(2,1)S(1)} %copy-done.2, bf16[256,768]{1,0:T(8,128)(2,1)S(1)} %slice.97, bf16[256,768]{1,0:T(8,128)(2,1)S(1)} %fusion.29, s32[128]{0:T(128)} %get-tuple-element.30, f32[]{:T(128)} %bitcast.52, f32[]{:T(128)} %bitcast.41, ...), kind=kOutput, calls=%fused_computation.36 | convolution fusion | flops 416808960 | bytes 3741184 | tf_op jit(solution)/shard_map/dot_general | solution.py:95
  72.0 3.8 %multiply_reduce_fusion.2 = (f32[128]{0:T(128)}, f32[128]{0:T(128)}, f32[128,768]{1,0:T(8,128)}) fusion(f32[256,768]{1,0:T(8,128)S(1)} %get-tuple-element.10, f32[128,768]{1,0:T(8,128)} %fusion.26, bf16[256,768]{1,0:T(8,128)(2,1)} %slice.99, bf16[256,768]{1,0:T(8,128)(2,1)S(1)} %copy-done.2, bf16[256,768]{1,0:T(8,128)(2,1)S(1)} %slice.97, ...), kind=kOutput, calls=%fused_computation.94 | convolution fusion | flops 417201920 | bytes 4921856 | tf_op jit(solution)/shard_map/dot_general | solution.py:95
  75.8 1.4 multiply_convert_fusion.1
  77.2 2.4 %collective-permute-start.14 = (bf16[128,768]{1,0:T(8,128)(2,1)S(1)}, bf16[128,768]{1,0:T(8,128)(2,1)S(1)}, u32[]{:S(2)}, u32[]{:S(2)}) collective-permute-start(bf16[128,768]{1,0:T(8,128)(2,1)S(1)} %get-tuple-element.17), channel_id=1, source_target_pairs={{0,24},{8,16},{16,8},{24,0},{1,25},{9,17},{17,9},{25,1},{2,26},{10... | collective-permute-start | bytes 589832 | tf_op jit(solution)/shard_map/ppermute | solution.py:41
  79.6 1.0 fusion.173
  80.7 0.6 collective-permute-start.11
  81.3 1.5 %collective-permute-start.10 = (bf16[128,768]{1,0:T(8,128)(2,1)S(1)}, bf16[128,768]{1,0:T(8,128)(2,1)S(1)}, u32[]{:S(2)}, u32[]{:S(2)}) collective-permute-start(bf16[128,768]{1,0:T(8,128)(2,1)S(1)} %get-tuple-element.16), channel_id=1, source_target_pairs={{0,16},{8,24},{16,0},{24,8},{1,17},{9,25},{17,1},{25,9},{2,18},{10... | collective-permute-start | bytes 589832 | tf_op jit(solution)/shard_map/ppermute | solution.py:41
  82.8 1.5 %collective-permute-start.9 = (bf16[128,768]{1,0:T(8,128)(2,1)S(1)}, bf16[128,768]{1,0:T(8,128)(2,1)S(1)}, u32[]{:S(2)}, u32[]{:S(2)}) collective-permute-start(bf16[128,768]{1,0:T(8,128)(2,1)S(1)} %get-tuple-element.16), channel_id=1, source_target_pairs={{0,8},{8,0},{16,24},{24,16},{1,9},{9,1},{17,25},{25,17},{2,10},{10... | collective-permute-start | bytes 589832 | tf_op jit(solution)/shard_map/ppermute | solution.py:41
  84.2 0.6 collective-permute-start.13
  84.8 1.2 collective-permute-done.14
  86.0 1.5 %collective-permute-start.12 = (bf16[128,768]{1,0:T(8,128)(2,1)S(1)}, bf16[128,768]{1,0:T(8,128)(2,1)S(1)}, u32[]{:S(2)}, u32[]{:S(2)}) collective-permute-start(bf16[128,768]{1,0:T(8,128)(2,1)S(1)} %get-tuple-element.17), channel_id=1, source_target_pairs={{0,8},{8,0},{16,24},{24,16},{1,9},{9,1},{17,25},{25,17},{2,10},{10... | collective-permute-start | bytes 589832 | tf_op jit(solution)/shard_map/ppermute | solution.py:41
  87.5 10.3 %collective-permute-done.13 = bf16[128,768]{1,0:T(8,128)(2,1)S(1)} collective-permute-done((bf16[128,768]{1,0:T(8,128)(2,1)S(1)}, bf16[128,768]{1,0:T(8,128)(2,1)S(1)}, u32[]{:S(2)}, u32[]{:S(2)}) %collective-permute-start.13) | collective-permute-done | bytes 196640 | tf_op jit(solution)/shard_map/ppermute | solution.py:41
  97.8 0.1 collective-permute-done.12
  97.9 0.8 fusion.49
  98.7 0.1 copy-done.3
  98.8 0.1 copy-done.5
  98.9 2.3 %convolution_add_fusion = f32[768,768]{1,0:T(8,128)} fusion(f32[768,768]{1,0:T(8,128)S(1)} %fusion.49, bf16[128,768]{1,0:T(8,128)(2,1)S(1)} %get-tuple-element.22, bf16[128,768]{1,0:T(8,128)(2,1)S(1)} %get-tuple-element.20, bf16[128,768]{1,0:T(8,128)(2,1)S(1)} %copy-done.5, bf16[128,768]{1,0:T(8,128)(2,1)S(1)} %copy-done.3, ...), kind=kOutput, calls=%fused_computation | convolution fusion | flops 610861056 | bytes 6291456 | tf_op jit(solution)/shard_map/dot_general | solution.py:109
  101.2 0.0 reduce-scatter.2.cloned.1.call-update
  101.2 2.4 %collective-permute-start.2 = (bf16[256,768]{1,0:T(8,128)(2,1)S(1)}, bf16[256,768]{1,0:T(8,128)(2,1)S(1)}, u32[]{:S(2)}, u32[]{:S(2)}) collective-permute-start(bf16[256,768]{1,0:T(8,128)(2,1)S(1)} %get-tuple-element.9), channel_id=1, source_target_pairs={{0,24},{8,16},{16,8},{24,0},{1,25},{9,17},{17,9},{25,1},{2,26},{10... | collective-permute-start | bytes 1179656 | tf_op jit(solution)/shard_map/ppermute | solution.py:41
  103.6 0.6 collective-permute-start.1
  104.2 0.6 collective-permute-start
  104.8 0.3 fusion.21
  105.1 0.4 fusion.127
  105.5 8.7 %collective-permute-done.2 = bf16[256,768]{1,0:T(8,128)(2,1)S(1)} collective-permute-done((bf16[256,768]{1,0:T(8,128)(2,1)S(1)}, bf16[256,768]{1,0:T(8,128)(2,1)S(1)}, u32[]{:S(2)}, u32[]{:S(2)}) %collective-permute-start.2) | collective-permute-done | bytes 393248 | tf_op jit(solution)/shard_map/ppermute | solution.py:41
  114.2 0.3 fusion.24
  114.5 7.1 %collective-permute-done.1 = bf16[256,768]{1,0:T(8,128)(2,1)S(1)} collective-permute-done((bf16[256,768]{1,0:T(8,128)(2,1)S(1)}, bf16[256,768]{1,0:T(8,128)(2,1)S(1)}, u32[]{:S(2)}, u32[]{:S(2)}) %collective-permute-start.1) | collective-permute-done | bytes 393248 | tf_op jit(solution)/shard_map/ppermute | solution.py:41
  121.6 0.3 fusion.23
  121.9 0.9 fusion.104
  122.8 0.6 add_add_fusion
  123.4 0.4 fusion.131
  123.8 0.4 convolution_add_fusion.2
  124.3 0.5 fusion.30
  124.8 1.0 fusion.70
  125.8 10.5 %reduce-scatter.2.cloned.1.call-done = f32[96,768]{1,0:T(8,128)} async-done(((f32[768,768]{1,0:T(8,128)}), f32[96,768]{1,0:T(8,128)}) %reduce-scatter.2.cloned.1.call-update) | async-done | bytes 294928 | tf_op jit(solution)/shard_map/reduce_scatter | solution.py:116
  (24 shorter events, 0.1 us)
Async XLA Ops:
  7.2 3.3 %copy-start = (bf16[1,256,768]{2,1,0:T(8,128)(2,1)S(1)}, bf16[1,256,768]{2,1,0:T(8,128)(2,1)}, u32[]{:S(2)}) copy-start(bf16[1,256,768]{2,1,0:T(8,128)(2,1)} %param.6) | copy-start | bytes 1179652
  7.2 56.9 %all-gather.2.cloned.1.call-start = ((), (), s32[]{:S(2)}) async-start(), calls=%async_computation.1 | async-start | bytes 5308416 | tf_op jit(solution)/shard_map/all_gather | solution.py:43
  7.9 128.4 %reduce-scatter.2.cloned.1.call-start = ((), (), s32[]{:S(2)}) async-start(), calls=%async_computation.2 | async-start | bytes 2654208 | tf_op jit(solution)/shard_map/reduce_scatter | solution.py:116
  10.6 6.0 %copy-start.7 = (s32[1,256]{1,0:T(1,128)S(1)}, s32[1,256]{1,0:T(1,128)}, u32[]{:S(2)}) copy-start(s32[1,256]{1,0:T(1,128)} %param.9) | copy-start | bytes 3076
  10.6 41.9 %copy-start.1 = (bf16[1,256,3072]{2,1,0:T(8,128)(2,1)S(1)}, bf16[1,256,3072]{2,1,0:T(8,128)(2,1)}, u32[]{:S(2)}) copy-start(bf16[1,256,3072]{2,1,0:T(8,128)(2,1)} %param.7) | copy-start | bytes 4718596
  12.2 42.5 %collective-permute-start.3 = (bf16[256,1536]{1,0:T(8,128)(2,1)}, bf16[256,1536]{1,0:T(8,128)(2,1)}, u32[]{:S(2)}, u32[]{:S(2)}) collective-permute-start(bf16[256,1536]{1,0:T(8,128)(2,1)} %get-tuple-element.24), channel_id=1, source_target_pairs={{0,8},{8,0},{16,24},{24,16},{1,9},{9,1},{17,25},{25,17},{2,10},{10... | collective-permute-start | bytes 2359304 | tf_op jit(solution)/shard_map/ppermute | solution.py:41
  15.1 40.6 %collective-permute-start.4 = (bf16[256,1536]{1,0:T(8,128)(2,1)}, bf16[256,1536]{1,0:T(8,128)(2,1)}, u32[]{:S(2)}, u32[]{:S(2)}) collective-permute-start(bf16[256,1536]{1,0:T(8,128)(2,1)} %get-tuple-element.25), channel_id=1, source_target_pairs={{0,16},{8,24},{16,0},{24,8},{1,17},{9,25},{17,1},{25,9},{2,18},{10... | collective-permute-start | bytes 2359304 | tf_op jit(solution)/shard_map/ppermute | solution.py:41
  16.7 40.8 %collective-permute-start.5 = (bf16[256,1536]{1,0:T(8,128)(2,1)}, bf16[256,1536]{1,0:T(8,128)(2,1)S(1)}, u32[]{:S(2)}, u32[]{:S(2)}) collective-permute-start(bf16[256,1536]{1,0:T(8,128)(2,1)} %get-tuple-element.26), channel_id=1, source_target_pairs={{0,24},{8,16},{16,8},{24,0},{1,25},{9,17},{17,9},{25,1},{2,26},{10... | collective-permute-start | bytes 2359304 | tf_op jit(solution)/shard_map/ppermute | solution.py:41
  16.7 34.4 %collective-permute-start.8 = (s32[256]{0:T(256)S(1)}, s32[256]{0:T(256)S(1)}, u32[]{:S(2)}, u32[]{:S(2)}) collective-permute-start(s32[256]{0:T(256)S(1)} %bitcast.56), channel_id=1, source_target_pairs={{0,24},{8,16},{16,8},{24,0},{1,25},{9,17},{17,9},{25,1},{2,26},{10... | collective-permute-start | bytes 3080 | tf_op jit(solution)/shard_map/ppermute | solution.py:41
  19.6 35.0 %collective-permute-start.7 = (s32[256]{0:T(256)S(1)}, s32[256]{0:T(256)S(1)}, u32[]{:S(2)}, u32[]{:S(2)}) collective-permute-start(s32[256]{0:T(256)S(1)} %bitcast.57), channel_id=1, source_target_pairs={{0,16},{8,24},{16,0},{24,8},{1,17},{9,25},{17,1},{25,9},{2,18},{10... | collective-permute-start | bytes 3080 | tf_op jit(solution)/shard_map/ppermute | solution.py:41
  51.1 3.6 %collective-permute-start.6 = (s32[256]{0:T(256)S(1)}, s32[256]{0:T(256)S(1)}, u32[]{:S(2)}, u32[]{:S(2)}) collective-permute-start(s32[256]{0:T(256)S(1)} %bitcast.58), channel_id=1, source_target_pairs={{0,8},{8,0},{16,24},{24,16},{1,9},{9,1},{17,25},{25,17},{2,10},{10... | collective-permute-start | bytes 3080 | tf_op jit(solution)/shard_map/ppermute | solution.py:41
  67.9 1.0 copy-start.2
  75.8 22.1 %copy-start.4 = (bf16[128,768]{1,0:T(8,128)(2,1)S(1)}, bf16[128,768]{1,0:T(8,128)(2,1)}, u32[]{:S(2)}) copy-start(bf16[128,768]{1,0:T(8,128)(2,1)} %get-tuple-element.12) | copy-start | bytes 589828
  75.8 22.1 %copy-start.6 = (bf16[128,768]{1,0:T(8,128)(2,1)S(1)}, bf16[128,768]{1,0:T(8,128)(2,1)}, u32[]{:S(2)}) copy-start(bf16[128,768]{1,0:T(8,128)(2,1)} %get-tuple-element.19) | copy-start | bytes 589828
  77.2 8.8 %collective-permute-start.14 = (bf16[128,768]{1,0:T(8,128)(2,1)S(1)}, bf16[128,768]{1,0:T(8,128)(2,1)S(1)}, u32[]{:S(2)}, u32[]{:S(2)}) collective-permute-start(bf16[128,768]{1,0:T(8,128)(2,1)S(1)} %get-tuple-element.17), channel_id=1, source_target_pairs={{0,24},{8,16},{16,8},{24,0},{1,25},{9,17},{17,9},{25,1},{2,26},{10... | collective-permute-start | bytes 589832 | tf_op jit(solution)/shard_map/ppermute | solution.py:41
  80.7 18.1 %collective-permute-start.11 = (bf16[128,768]{1,0:T(8,128)(2,1)S(1)}, bf16[128,768]{1,0:T(8,128)(2,1)S(1)}, u32[]{:S(2)}, u32[]{:S(2)}) collective-permute-start(bf16[128,768]{1,0:T(8,128)(2,1)S(1)} %get-tuple-element.16), channel_id=1, source_target_pairs={{0,24},{8,16},{16,8},{24,0},{1,25},{9,17},{17,9},{25,1},{2,26},{10... | collective-permute-start | bytes 589832 | tf_op jit(solution)/shard_map/ppermute | solution.py:41
  81.3 17.4 %collective-permute-start.10 = (bf16[128,768]{1,0:T(8,128)(2,1)S(1)}, bf16[128,768]{1,0:T(8,128)(2,1)S(1)}, u32[]{:S(2)}, u32[]{:S(2)}) collective-permute-start(bf16[128,768]{1,0:T(8,128)(2,1)S(1)} %get-tuple-element.16), channel_id=1, source_target_pairs={{0,16},{8,24},{16,0},{24,8},{1,17},{9,25},{17,1},{25,9},{2,18},{10... | collective-permute-start | bytes 589832 | tf_op jit(solution)/shard_map/ppermute | solution.py:41
  82.8 16.0 %collective-permute-start.9 = (bf16[128,768]{1,0:T(8,128)(2,1)S(1)}, bf16[128,768]{1,0:T(8,128)(2,1)S(1)}, u32[]{:S(2)}, u32[]{:S(2)}) collective-permute-start(bf16[128,768]{1,0:T(8,128)(2,1)S(1)} %get-tuple-element.16), channel_id=1, source_target_pairs={{0,8},{8,0},{16,24},{24,16},{1,9},{9,1},{17,25},{25,17},{2,10},{10... | collective-permute-start | bytes 589832 | tf_op jit(solution)/shard_map/ppermute | solution.py:41
  84.2 13.6 %collective-permute-start.13 = (bf16[128,768]{1,0:T(8,128)(2,1)S(1)}, bf16[128,768]{1,0:T(8,128)(2,1)S(1)}, u32[]{:S(2)}, u32[]{:S(2)}) collective-permute-start(bf16[128,768]{1,0:T(8,128)(2,1)S(1)} %get-tuple-element.17), channel_id=1, source_target_pairs={{0,16},{8,24},{16,0},{24,8},{1,17},{9,25},{17,1},{25,9},{2,18},{10... | collective-permute-start | bytes 589832 | tf_op jit(solution)/shard_map/ppermute | solution.py:41
  86.0 11.9 %collective-permute-start.12 = (bf16[128,768]{1,0:T(8,128)(2,1)S(1)}, bf16[128,768]{1,0:T(8,128)(2,1)S(1)}, u32[]{:S(2)}, u32[]{:S(2)}) collective-permute-start(bf16[128,768]{1,0:T(8,128)(2,1)S(1)} %get-tuple-element.17), channel_id=1, source_target_pairs={{0,8},{8,0},{16,24},{24,16},{1,9},{9,1},{17,25},{25,17},{2,10},{10... | collective-permute-start | bytes 589832 | tf_op jit(solution)/shard_map/ppermute | solution.py:41
  97.9 0.9 copy-start.3
  97.9 1.0 copy-start.5
  101.2 13.0 %collective-permute-start.2 = (bf16[256,768]{1,0:T(8,128)(2,1)S(1)}, bf16[256,768]{1,0:T(8,128)(2,1)S(1)}, u32[]{:S(2)}, u32[]{:S(2)}) collective-permute-start(bf16[256,768]{1,0:T(8,128)(2,1)S(1)} %get-tuple-element.9), channel_id=1, source_target_pairs={{0,24},{8,16},{16,8},{24,0},{1,25},{9,17},{17,9},{25,1},{2,26},{10... | collective-permute-start | bytes 1179656 | tf_op jit(solution)/shard_map/ppermute | solution.py:41
  103.6 18.0 %collective-permute-start.1 = (bf16[256,768]{1,0:T(8,128)(2,1)S(1)}, bf16[256,768]{1,0:T(8,128)(2,1)S(1)}, u32[]{:S(2)}, u32[]{:S(2)}) collective-permute-start(bf16[256,768]{1,0:T(8,128)(2,1)S(1)} %get-tuple-element.9), channel_id=1, source_target_pairs={{0,16},{8,24},{16,0},{24,8},{1,17},{9,25},{17,1},{25,9},{2,18},{10... | collective-permute-start | bytes 1179656 | tf_op jit(solution)/shard_map/ppermute | solution.py:41
  104.2 17.7 %collective-permute-start = (bf16[256,768]{1,0:T(8,128)(2,1)S(1)}, bf16[256,768]{1,0:T(8,128)(2,1)S(1)}, u32[]{:S(2)}, u32[]{:S(2)}) collective-permute-start(bf16[256,768]{1,0:T(8,128)(2,1)S(1)} %get-tuple-element.9), channel_id=1, source_target_pairs={{0,8},{8,0},{16,24},{24,16},{1,9},{9,1},{17,25},{25,17},{2,10},{10... | collective-permute-start | bytes 1179656 | tf_op jit(solution)/shard_map/ppermute | solution.py:41
Sparse Core Ops, SparseCore 0:
  9.6 54.3 all-gather.1
  101.3 34.9 reduce-scatter.1

commit v6 on v4

--- a/solution.py
+++ b/solution.py
@@ -105,7 +105,9 @@
         (((0,), (0,)), ((), ())),
         preferred_element_type=jnp.float32,
     )
-    projection_grad = lax.psum_scatter(partial, "group", scatter_dimension=0, tiled=True)
+    projection_grad = lax.psum_scatter(
+        partial.astype(jnp.bfloat16), "group", scatter_dimension=0, tiled=True
+    ).astype(jnp.float32)
 
     loss_local = jnp.zeros((row_count,), jnp.float32)
     image_unit_grad = jnp.zeros(image_unit.shape, jnp.float32)

time: 139 us -> 141 us (1.014)
  waiting for transfers between devices: 79.3 us -> 76.8 us
  other arithmetic: 5.82 us -> 8.19 us
    ppermute x12, waiting for transfers between devices: 63.4 us -> 55.3 us  [exchange(): return lax.ppermute(value, 'blk', partner_pairs(blocks, step))]
    reduce_scatter x1, waiting for transfers between devices: 9.96 us -> 15.5 us  [body(): lax.psum_scatter(partial.astype(jnp.bfloat16), 'group', scatter_dimension...]
    convert_element_type x0 -> x1, other arithmetic: none -> 1.64 us  [body(): projection_grad = lax.psum_scatter(partial.astype(jnp.bfloat16), 'group',...]
  transfers between devices with their start and end apart: 14 -> 14, of which waited for: 8 -> 6; matrix products, arithmetic and copies ran while one was open for 11% -> 13% of each run, Pallas kernels for 0% -> 0%
where the time goes in v6:
time: 141 us; the launch traced here: 140 us
  waiting for transfers between devices  76.8 us (54%)
  starting transfers between devices  17.5 us (12%)
  matrix products  15.8 us (11%)
  between operations  15.5 us (11%)
  other arithmetic  8.19 us (6%)
  local copies, waits for them, and re-layouts  6.26 us (4%)
    ppermute x12, waiting for transfers between devices, exchange(): return lax.ppermute(value, 'blk', partner_pairs(blocks, step))  55.3 us
    ppermute x12, starting transfers between devices, exchange(): return lax.ppermute(value, 'blk', partner_pairs(blocks, step))  17.5 us
    reduce_scatter x1, waiting for transfers between devices, body(): lax.psum_scatter(partial.astype(jnp.bfloat16), 'group', scatter_dimension...  15.5 us
    all_gather x1, waiting for transfers between devices, body(): w_full = lax.all_gather(linear_map_matrix, 'group', axis=0, tiled=True)  5.27 us
    dot_general x1, matrix products, body(): lax.dot_general(weights_of(logits_t, pair_sign_t), image_group, (((0,), (...  4.31 us
    dot_general x1, matrix products, body(): lax.dot_general(hidden_group, jnp.concatenate(grad_from, axis=0), (((0,),...  4.07 us
    slice x3, local copies, waits for them, and re-layouts, body(): hidden_from.append(incoming[:, :chunk])  3.96 us
    dot_general x1, matrix products, body(): projected = jnp.dot(hidden_rows, w_full, preferred_element_type=jnp.float32)  3.79 us
  transfers between devices with their start and end apart: 14, of which 6 were waited for; matrix products, arithmetic and copies ran while one was open for 13% of the time, Pallas kernels for 0%

profile of v6, /device:TPU:0, one launch (start us, length us, event | category | flops | bytes accessed | tf_op | source)
XLA Modules:
  0.0 140.1 jit_solution(1813661652439631994)
XLA Ops:
  7.2 0.0 all-gather.2.cloned.1.call-start
  7.2 0.7 all-gather.2.cloned.1.call-update
  7.9 0.0 reduce-scatter.2.cloned.1.call-start
  8.0 1.2 fusion.47
  9.1 0.0 copy-start
  9.1 2.3 %dynamic-slice_bitcast_fusion.3 = (bf16[256,768]{1,0:T(8,128)(2,1)}, bf16[256,768]{1,0:T(8,128)(2,1)S(1)}, bf16[256,768]{1,0:T(8,128)(2,1)S(1)}, bf16[256,768]{1,0:T(8,128)(2,1)S(1)}) fusion(bf16[1,256,3072]{2,1,0:T(8,128)(2,1)} %param.7, s32[]{:T(128)S(6)} %select_n.51, s32[]{:T(128)S(6)} %select_n.52, s32[]{:T(128)S(6)} %select_n.54, s32[]{:T(128)S(6)} %select_n.53), kind=kLoop, calls=%fused_computation.75 | loop fusion | bytes 3145744 | tf_op jit(solution)/shard_map/dynamic_slice | solution.py:51
  11.4 0.0 copy-done
  11.4 0.1 fusion.42
  11.5 0.0 copy-start.5
  11.6 1.3 pad_maximum_fusion.5
  12.9 3.9 %collective-permute-start.5 = (bf16[256,1536]{1,0:T(8,128)(2,1)S(1)}, bf16[256,1536]{1,0:T(8,128)(2,1)S(1)}, u32[]{:S(2)}, u32[]{:S(2)}) collective-permute-start(bf16[256,1536]{1,0:T(8,128)(2,1)S(1)} %get-tuple-element.19), channel_id=1, source_target_pairs={{0,24},{8,16},{16,8},{24,0},{1,25},{9,17},{17,9},{25,1},{2,26},{10... | collective-permute-start | bytes 2359304 | tf_op jit(solution)/shard_map/ppermute | solution.py:41
  16.8 0.5 collective-permute-start.4
  17.3 0.1 collective-permute-start.3
  17.4 0.0 copy-done.5
  17.4 2.9 %collective-permute-start.8 = (s32[256]{0:T(256)S(1)}, s32[256]{0:T(256)S(1)}, u32[]{:S(2)}, u32[]{:S(2)}) collective-permute-start(s32[256]{0:T(256)S(1)} %bitcast.53), channel_id=1, source_target_pairs={{0,24},{8,16},{16,8},{24,0},{1,25},{9,17},{17,9},{25,1},{2,26},{10... | collective-permute-start | bytes 3080 | tf_op jit(solution)/shard_map/ppermute | solution.py:41
  20.3 0.5 collective-permute-start.7
  20.8 30.5 %collective-permute-done.8 = s32[256]{0:T(256)S(1)} collective-permute-done((s32[256]{0:T(256)S(1)}, s32[256]{0:T(256)S(1)}, u32[]{:S(2)}, u32[]{:S(2)}) %collective-permute-start.8) | collective-permute-done | bytes 1056 | tf_op jit(solution)/shard_map/ppermute | solution.py:41
  51.2 1.7 %collective-permute-start.6 = (s32[256]{0:T(256)S(1)}, s32[256]{0:T(256)S(1)}, u32[]{:S(2)}, u32[]{:S(2)}) collective-permute-start(s32[256]{0:T(256)S(1)} %bitcast.55), channel_id=1, source_target_pairs={{0,8},{8,0},{16,24},{24,16},{1,9},{9,1},{17,25},{25,17},{2,10},{10... | collective-permute-start | bytes 3080 | tf_op jit(solution)/shard_map/ppermute | solution.py:41
  52.9 0.6 iota_add_fusion.3
  54.8 0.0 collective-permute-done.7
  54.8 0.0 collective-permute-done.6
  54.8 0.0 collective-permute-done.5
  54.8 0.8 fusion.136
  55.6 0.0 collective-permute-done.4
  55.6 2.2 %fusion.135 = (bf16[256,768]{1,0:T(8,128)(2,1)}, bf16[256,768]{1,0:T(8,128)(2,1)}) fusion(bf16[256,1536]{1,0:T(8,128)(2,1)} %collective-permute-done.4), kind=kLoop, calls=%fused_computation.167 | loop fusion | bytes 1572864 | tf_op jit(solution)/shard_map/slice | solution.py:61
  57.8 0.0 collective-permute-done.3
  57.8 1.0 fusion.134
  58.8 5.3 %all-gather.2.cloned.1.call-done = bf16[3072,768]{1,0:T(8,128)(2,1)} async-done(((bf16[384,768]{1,0:T(8,128)(2,1)}), bf16[3072,768]{1,0:T(8,128)(2,1)}) %all-gather.2.cloned.1.call-update) | async-done | bytes 4718608 | tf_op jit(solution)/shard_map/all_gather | solution.py:43
  64.1 0.0 copy-done.1
  64.1 3.8 %multiply_reduce_fusion.1 = (f32[256]{0:T(256)S(1)}, f32[256,768]{1,0:T(8,128)S(1)}) fusion(bf16[3072,768]{1,0:T(8,128)(2,1)} %all-gather.2.cloned.1.call-done, bf16[1,256,3072]{2,1,0:T(8,128)(2,1)S(1)} %copy-done.1), kind=kOutput, calls=%fused_computation.59 | convolution fusion | flops 1208352512 | bytes 7078912 | tf_op jit(solution)/shard_map/dot_general | solution.py:65
  67.9 0.1 multiply_convert_fusion.1
  68.0 4.3 %multiply_reduce_fusion = (f32[256]{0:T(256)}, f32[256,768]{1,0:T(8,128)S(1)}) fusion(f32[256,768]{1,0:T(8,128)S(1)} %get-tuple-element.21, f32[256]{0:T(256)S(1)} %add_rsqrt_fusion, bf16[256,768]{1,0:T(8,128)(2,1)} %get-tuple-element.16, bf16[256,768]{1,0:T(8,128)(2,1)} %get-tuple-element.14, bf16[256,768]{1,0:T(8,128)(2,1)} %get-tuple-element.12, ...), kind=kOutput, calls=%fused_computation.58 | convolution fusion | flops 821624576 | bytes 3546120 | tf_op jit(solution)/shard_map/dot_general | solution.py:89
  72.3 1.7 %multiply_convert_fusion = bf16[256,768]{1,0:T(8,128)(2,1)} fusion(f32[256,768]{1,0:T(8,128)S(1)} %get-tuple-element.26, f32[256,768]{1,0:T(8,128)S(1)} %get-tuple-element.21, f32[256]{0:T(256)} %get-tuple-element.25, f32[256]{0:T(256)S(1)} %add_rsqrt_fusion), kind=kLoop, calls=%fused_computation.57 | loop fusion | flops 983040 | bytes 1968128 | tf_op jit(solution)/shard_map/convert_element_type | solution.py:98
  74.0 2.4 %collective-permute-start.11 = (bf16[256,768]{1,0:T(8,128)(2,1)}, bf16[256,768]{1,0:T(8,128)(2,1)}, u32[]{:S(2)}, u32[]{:S(2)}) collective-permute-start(bf16[256,768]{1,0:T(8,128)(2,1)} %multiply_convert_fusion), channel_id=1, source_target_pairs={{0,24},{8,16},{16,8},{24,0},{1,25},{9,17},{17,9},{25,1},{2,26},{10... | collective-permute-start | bytes 1179656 | tf_op jit(solution)/shard_map/ppermute | solution.py:41
  76.4 0.6 collective-permute-start.10
  76.9 0.6 collective-permute-start.9
  77.5 1.5 %collective-permute-start.1 = (bf16[256,768]{1,0:T(8,128)(2,1)S(1)}, bf16[256,768]{1,0:T(8,128)(2,1)S(1)}, u32[]{:S(2)}, u32[]{:S(2)}) collective-permute-start(bf16[256,768]{1,0:T(8,128)(2,1)S(1)} %multiply_convert_fusion.1), channel_id=1, source_target_pairs={{0,16},{8,24},{16,0},{24,8},{1,17},{9,25},{17,1},{25,9},{2,18},{10... | collective-permute-start | bytes 1179656 | tf_op jit(solution)/shard_map/ppermute | solution.py:41
  79.0 1.5 %collective-permute-start.2 = (bf16[256,768]{1,0:T(8,128)(2,1)S(1)}, bf16[256,768]{1,0:T(8,128)(2,1)S(1)}, u32[]{:S(2)}, u32[]{:S(2)}) collective-permute-start(bf16[256,768]{1,0:T(8,128)(2,1)S(1)} %multiply_convert_fusion.1), channel_id=1, source_target_pairs={{0,24},{8,16},{16,8},{24,0},{1,25},{9,17},{17,9},{25,1},{2,26},{10... | collective-permute-start | bytes 1179656 | tf_op jit(solution)/shard_map/ppermute | solution.py:41
  80.4 0.3 fusion.32
  80.7 0.0 copy-start.3
  80.8 6.5 %collective-permute-done.11 = bf16[256,768]{1,0:T(8,128)(2,1)} collective-permute-done((bf16[256,768]{1,0:T(8,128)(2,1)}, bf16[256,768]{1,0:T(8,128)(2,1)}, u32[]{:S(2)}, u32[]{:S(2)}) %collective-permute-start.11) | collective-permute-done | bytes 393248 | tf_op jit(solution)/shard_map/ppermute | solution.py:41
  87.2 1.5 %collective-permute-start = (bf16[256,768]{1,0:T(8,128)(2,1)S(1)}, bf16[256,768]{1,0:T(8,128)(2,1)S(1)}, u32[]{:S(2)}, u32[]{:S(2)}) collective-permute-start(bf16[256,768]{1,0:T(8,128)(2,1)S(1)} %multiply_convert_fusion.1), channel_id=1, source_target_pairs={{0,8},{8,0},{16,24},{24,16},{1,9},{9,1},{17,25},{25,17},{2,10},{10... | collective-permute-start | bytes 1179656 | tf_op jit(solution)/shard_map/ppermute | solution.py:41
  88.7 7.0 %collective-permute-done.10 = bf16[256,768]{1,0:T(8,128)(2,1)} collective-permute-done((bf16[256,768]{1,0:T(8,128)(2,1)}, bf16[256,768]{1,0:T(8,128)(2,1)}, u32[]{:S(2)}, u32[]{:S(2)}) %collective-permute-start.10) | collective-permute-done | bytes 393248 | tf_op jit(solution)/shard_map/ppermute | solution.py:41
  95.7 0.0 collective-permute-done.9
  95.7 0.0 copy-done.2
  95.7 4.1 %fusion.17 = bf16[768,768]{1,0:T(8,128)(2,1)} fusion(bf16[256,768]{1,0:T(8,128)(2,1)} %collective-permute-done.11, bf16[256,768]{1,0:T(8,128)(2,1)} %collective-permute-done.10, bf16[256,768]{1,0:T(8,128)(2,1)} %collective-permute-done.9, bf16[256,768]{1,0:T(8,128)(2,1)} %multiply_convert_fusion, bf16[256,768]{1,0:T(8,128)(2,1)S(1)} %get-tuple-element.15, ...), kind=kOutput, calls=%fused_computation.18 | convolution fusion | flops 1221132288 | bytes 4325376 | tf_op jit(solution)/shard_map/dot_general | solution.py:102
  99.8 0.0 reduce-scatter.2.cloned.1.call-update
  99.8 0.0 copy-done.3
  99.8 0.4 fusion.95
  100.3 0.0 copy-start.4
  100.3 11.4 %collective-permute-done.1 = bf16[256,768]{1,0:T(8,128)(2,1)S(1)} collective-permute-done((bf16[256,768]{1,0:T(8,128)(2,1)S(1)}, bf16[256,768]{1,0:T(8,128)(2,1)S(1)}, u32[]{:S(2)}, u32[]{:S(2)}) %collective-permute-start.1) | collective-permute-done | bytes 393248 | tf_op jit(solution)/shard_map/ppermute | solution.py:41
  111.7 0.3 fusion.34
  112.0 0.0 collective-permute-done.2
  112.0 0.3 fusion.35
  112.3 0.0 collective-permute-done
  112.3 0.0 copy-done.4
  112.3 0.9 fusion.88
  113.2 0.6 add_add_fusion
  113.8 0.4 fusion.99
  114.2 0.4 convolution_add_fusion.1
  114.7 0.5 fusion.43
  115.2 1.0 fusion.54
  116.2 15.5 %reduce-scatter.2.cloned.1.call-done = bf16[96,768]{1,0:T(8,128)(2,1)} async-done(((bf16[768,768]{1,0:T(8,128)(2,1)}), bf16[96,768]{1,0:T(8,128)(2,1)}) %reduce-scatter.2.cloned.1.call-update) | async-done | bytes 147472 | tf_op jit(solution)/shard_map/reduce_scatter | solution.py:108
  131.7 1.6 %convert_element_type.51 = f32[96,768]{1,0:T(8,128)} convert(bf16[96,768]{1,0:T(8,128)(2,1)} %reduce-scatter.2.cloned.1.call-done) | non-fusion elementwise | flops 73728 | bytes 442368 | tf_op jit(solution)/shard_map/convert_element_type | solution.py:110
  (9 shorter events, 0.0 us)
Async XLA Ops:
  7.2 56.9 %all-gather.2.cloned.1.call-start = ((), (), s32[]{:S(2)}) async-start(), calls=%async_computation.1 | async-start | bytes 5308416 | tf_op jit(solution)/shard_map/all_gather | solution.py:43
  7.9 123.8 %reduce-scatter.2.cloned.1.call-start = ((), (), s32[]{:S(2)}) async-start(), calls=%async_computation.2 | async-start | bytes 1327104 | tf_op jit(solution)/shard_map/reduce_scatter | solution.py:108
  9.1 2.3 %copy-start = (bf16[1,256,768]{2,1,0:T(8,128)(2,1)S(1)}, bf16[1,256,768]{2,1,0:T(8,128)(2,1)}, u32[]{:S(2)}) copy-start(bf16[1,256,768]{2,1,0:T(8,128)(2,1)} %param.6) | copy-start | bytes 1179652
  11.5 5.8 %copy-start.5 = (s32[1,256]{1,0:T(1,128)S(1)}, s32[1,256]{1,0:T(1,128)}, u32[]{:S(2)}) copy-start(s32[1,256]{1,0:T(1,128)} %param.9) | copy-start | bytes 3076
  12.9 41.9 %collective-permute-start.5 = (bf16[256,1536]{1,0:T(8,128)(2,1)S(1)}, bf16[256,1536]{1,0:T(8,128)(2,1)S(1)}, u32[]{:S(2)}, u32[]{:S(2)}) collective-permute-start(bf16[256,1536]{1,0:T(8,128)(2,1)S(1)} %get-tuple-element.19), channel_id=1, source_target_pairs={{0,24},{8,16},{16,8},{24,0},{1,25},{9,17},{17,9},{25,1},{2,26},{10... | collective-permute-start | bytes 2359304 | tf_op jit(solution)/shard_map/ppermute | solution.py:41
  16.8 38.9 %collective-permute-start.4 = (bf16[256,1536]{1,0:T(8,128)(2,1)}, bf16[256,1536]{1,0:T(8,128)(2,1)}, u32[]{:S(2)}, u32[]{:S(2)}) collective-permute-start(bf16[256,1536]{1,0:T(8,128)(2,1)} %get-tuple-element.18), channel_id=1, source_target_pairs={{0,16},{8,24},{16,0},{24,8},{1,17},{9,25},{17,1},{25,9},{2,18},{10... | collective-permute-start | bytes 2359304 | tf_op jit(solution)/shard_map/ppermute | solution.py:41
  17.3 40.5 %collective-permute-start.3 = (bf16[256,1536]{1,0:T(8,128)(2,1)}, bf16[256,1536]{1,0:T(8,128)(2,1)S(1)}, u32[]{:S(2)}, u32[]{:S(2)}) collective-permute-start(bf16[256,1536]{1,0:T(8,128)(2,1)} %get-tuple-element.17), channel_id=1, source_target_pairs={{0,8},{8,0},{16,24},{24,16},{1,9},{9,1},{17,25},{25,17},{2,10},{10... | collective-permute-start | bytes 2359304 | tf_op jit(solution)/shard_map/ppermute | solution.py:41
  17.4 33.9 %collective-permute-start.8 = (s32[256]{0:T(256)S(1)}, s32[256]{0:T(256)S(1)}, u32[]{:S(2)}, u32[]{:S(2)}) collective-permute-start(s32[256]{0:T(256)S(1)} %bitcast.53), channel_id=1, source_target_pairs={{0,24},{8,16},{16,8},{24,0},{1,25},{9,17},{17,9},{25,1},{2,26},{10... | collective-permute-start | bytes 3080 | tf_op jit(solution)/shard_map/ppermute | solution.py:41
  20.3 34.5 %collective-permute-start.7 = (s32[256]{0:T(256)S(1)}, s32[256]{0:T(256)S(1)}, u32[]{:S(2)}, u32[]{:S(2)}) collective-permute-start(s32[256]{0:T(256)S(1)} %bitcast.54), channel_id=1, source_target_pairs={{0,16},{8,24},{16,0},{24,8},{1,17},{9,25},{17,1},{25,9},{2,18},{10... | collective-permute-start | bytes 3080 | tf_op jit(solution)/shard_map/ppermute | solution.py:41
  51.2 3.6 %collective-permute-start.6 = (s32[256]{0:T(256)S(1)}, s32[256]{0:T(256)S(1)}, u32[]{:S(2)}, u32[]{:S(2)}) collective-permute-start(s32[256]{0:T(256)S(1)} %bitcast.55), channel_id=1, source_target_pairs={{0,8},{8,0},{16,24},{24,16},{1,9},{9,1},{17,25},{25,17},{2,10},{10... | collective-permute-start | bytes 3080 | tf_op jit(solution)/shard_map/ppermute | solution.py:41
  55.6 8.4 %copy-start.1 = (bf16[1,256,3072]{2,1,0:T(8,128)(2,1)S(1)}, bf16[1,256,3072]{2,1,0:T(8,128)(2,1)}, u32[]{:S(2)}) copy-start(bf16[1,256,3072]{2,1,0:T(8,128)(2,1)} %param.7) | copy-start | bytes 4718596
  72.3 23.4 %copy-start.2 = (bf16[256,768]{1,0:T(8,128)(2,1)S(1)}, bf16[256,768]{1,0:T(8,128)(2,1)}, u32[]{:S(2)}) copy-start(bf16[256,768]{1,0:T(8,128)(2,1)} %get-tuple-element.13) | copy-start | bytes 1179652
  74.0 13.2 %collective-permute-start.11 = (bf16[256,768]{1,0:T(8,128)(2,1)}, bf16[256,768]{1,0:T(8,128)(2,1)}, u32[]{:S(2)}, u32[]{:S(2)}) collective-permute-start(bf16[256,768]{1,0:T(8,128)(2,1)} %multiply_convert_fusion), channel_id=1, source_target_pairs={{0,24},{8,16},{16,8},{24,0},{1,25},{9,17},{17,9},{25,1},{2,26},{10... | collective-permute-start | bytes 1179656 | tf_op jit(solution)/shard_map/ppermute | solution.py:41
  76.4 19.3 %collective-permute-start.10 = (bf16[256,768]{1,0:T(8,128)(2,1)}, bf16[256,768]{1,0:T(8,128)(2,1)}, u32[]{:S(2)}, u32[]{:S(2)}) collective-permute-start(bf16[256,768]{1,0:T(8,128)(2,1)} %multiply_convert_fusion), channel_id=1, source_target_pairs={{0,16},{8,24},{16,0},{24,8},{1,17},{9,25},{17,1},{25,9},{2,18},{10... | collective-permute-start | bytes 1179656 | tf_op jit(solution)/shard_map/ppermute | solution.py:41
  76.9 18.8 %collective-permute-start.9 = (bf16[256,768]{1,0:T(8,128)(2,1)}, bf16[256,768]{1,0:T(8,128)(2,1)}, u32[]{:S(2)}, u32[]{:S(2)}) collective-permute-start(bf16[256,768]{1,0:T(8,128)(2,1)} %multiply_convert_fusion), channel_id=1, source_target_pairs={{0,8},{8,0},{16,24},{24,16},{1,9},{9,1},{17,25},{25,17},{2,10},{10... | collective-permute-start | bytes 1179656 | tf_op jit(solution)/shard_map/ppermute | solution.py:41
  77.5 34.2 %collective-permute-start.1 = (bf16[256,768]{1,0:T(8,128)(2,1)S(1)}, bf16[256,768]{1,0:T(8,128)(2,1)S(1)}, u32[]{:S(2)}, u32[]{:S(2)}) collective-permute-start(bf16[256,768]{1,0:T(8,128)(2,1)S(1)} %multiply_convert_fusion.1), channel_id=1, source_target_pairs={{0,16},{8,24},{16,0},{24,8},{1,17},{9,25},{17,1},{25,9},{2,18},{10... | collective-permute-start | bytes 1179656 | tf_op jit(solution)/shard_map/ppermute | solution.py:41
  79.0 33.0 %collective-permute-start.2 = (bf16[256,768]{1,0:T(8,128)(2,1)S(1)}, bf16[256,768]{1,0:T(8,128)(2,1)S(1)}, u32[]{:S(2)}, u32[]{:S(2)}) collective-permute-start(bf16[256,768]{1,0:T(8,128)(2,1)S(1)} %multiply_convert_fusion.1), channel_id=1, source_target_pairs={{0,24},{8,16},{16,8},{24,0},{1,25},{9,17},{17,9},{25,1},{2,26},{10... | collective-permute-start | bytes 1179656 | tf_op jit(solution)/shard_map/ppermute | solution.py:41
  80.7 19.1 %copy-start.3 = (f32[256,256]{0,1:T(8,128)}, f32[256,256]{0,1:T(8,128)S(1)}, u32[]{:S(2)}) copy-start(f32[256,256]{0,1:T(8,128)S(1)} %fusion.32) | copy-start | bytes 786436
  87.2 25.1 %collective-permute-start = (bf16[256,768]{1,0:T(8,128)(2,1)S(1)}, bf16[256,768]{1,0:T(8,128)(2,1)S(1)}, u32[]{:S(2)}, u32[]{:S(2)}) collective-permute-start(bf16[256,768]{1,0:T(8,128)(2,1)S(1)} %multiply_convert_fusion.1), channel_id=1, source_target_pairs={{0,8},{8,0},{16,24},{24,16},{1,9},{9,1},{17,25},{25,17},{2,10},{10... | collective-permute-start | bytes 1179656 | tf_op jit(solution)/shard_map/ppermute | solution.py:41
  95.7 4.1 %copy-start.6 = (s32[256]{0:T(256)S(1)}, s32[256]{0:T(256)}, u32[]{:S(2)}) copy-start(s32[256]{0:T(256)} %iota_add_fusion.3) | copy-start | bytes 3076
  100.3 12.0 %copy-start.4 = (f32[256,256]{0,1:T(8,128)S(1)}, f32[256,256]{0,1:T(8,128)}, u32[]{:S(2)}) copy-start(f32[256,256]{0,1:T(8,128)} %copy-done.3) | copy-start | bytes 786436
Sparse Core Ops, SparseCore 0:
  9.6 54.3 all-gather.1
  99.9 31.6 reduce-scatter.1

commit v7 on v6

--- a/solution.py
+++ b/solution.py
@@ -105,9 +105,17 @@
         (((0,), (0,)), ((), ())),
         preferred_element_type=jnp.float32,
     )
+    groups = lax.axis_size("group")
+    parity = lax.axis_index("group") % 2
+    by_owner = partial.reshape(groups // 2, 2, partial.shape[0] // groups, partial.shape[1])
+    keep = lax.dynamic_index_in_dim(by_owner, parity, 1, keepdims=False)
+    give = lax.dynamic_index_in_dim(by_owner, 1 - parity, 1, keepdims=False)
+    mate_pairs = [(g, g ^ 1) for g in range(groups)]
+    chip_sum = keep + lax.ppermute(give, "group", mate_pairs)
+    same_core = [list(range(p, groups, 2)) for p in range(2)]
     projection_grad = lax.psum_scatter(
-        partial.astype(jnp.bfloat16), "group", scatter_dimension=0, tiled=True
-    ).astype(jnp.float32)
+        chip_sum, "group", scatter_dimension=0, axis_index_groups=same_core, tiled=True
+    ).reshape(partial.shape[0] // groups, partial.shape[1])
 
     loss_local = jnp.zeros((row_count,), jnp.float32)
     image_unit_grad = jnp.zeros(image_unit.shape, jnp.float32)

time: 141 us -> 141 us (level)
  waiting for transfers between devices: 76.8 us -> 69.7 us
  matrix products: 15.8 us -> 22 us
  local copies, waits for them, and re-layouts: 6.26 us -> 8.41 us
    reduce_scatter x1, waiting for transfers between devices: 15.5 us -> 3.89 us  [body(): lax.psum_scatter(chip_sum, 'group', scatter_dimension=0, axis_index_group...]
    ppermute x12, waiting for transfers between devices: 55.3 us -> 60 us  [exchange(): return lax.ppermute(value, 'blk', partner_pairs(blocks, step))]
    dot_general x4, matrix products: 1.87 us -> 5.84 us  [body(): jnp.dot(weights_of(logits, pair_sign), text_from[k], preferred_element_ty...]
    dot_general x4, matrix products: 1.79 us -> 5.49 us  [body(): lax.dot_general(image_unit, text_from[k], (((1,), (1,)), ((), ())), prefe...]
    add x0 -> x1, other arithmetic: none -> 2.44 us  [body(): chip_sum = keep + lax.ppermute(give, 'group', mate_pairs)]
    convert_element_type x1 -> x0, other arithmetic: 1.64 us -> none  [body(): projection_grad = lax.psum_scatter(partial.astype(jnp.bfloat16), 'group',...]
  transfers between devices with their start and end apart: 14 -> 15, of which waited for: 6 -> 8; matrix products, arithmetic and copies ran while one was open for 13% -> 18% of each run, Pallas kernels for 0% -> 0%
where the time goes in v7:
time: 141 us
  waiting for transfers between devices  69.7 us (49%)
  matrix products  22 us (16%)
  starting transfers between devices  16.6 us (12%)
  between operations  15.5 us (11%)
  local copies, waits for them, and re-layouts  8.41 us (6%)
  other arithmetic  8.29 us (6%)
    ppermute x12, waiting for transfers between devices, exchange(): return lax.ppermute(value, 'blk', partner_pairs(blocks, step))  60 us
    ppermute x12, starting transfers between devices, exchange(): return lax.ppermute(value, 'blk', partner_pairs(blocks, step))  16.6 us
    dot_general x4, matrix products, body(): jnp.dot(weights_of(logits, pair_sign), text_from[k], preferred_element_ty...  5.84 us
    dot_general x4, matrix products, body(): lax.dot_general(image_unit, text_from[k], (((1,), (1,)), ((), ())), prefe...  5.49 us
    all_gather x1, waiting for transfers between devices, body(): w_full = lax.all_gather(linear_map_matrix, 'group', axis=0, tiled=True)  5.07 us
    slice x3, local copies, waits for them, and re-layouts, body(): image_from.append(incoming[:, chunk:])  4.14 us
    reduce_scatter x1, waiting for transfers between devices, body(): lax.psum_scatter(chip_sum, 'group', scatter_dimension=0, axis_index_group...  3.89 us
    dot_general x1, matrix products, body(): projected = jnp.dot(hidden_rows, w_full, preferred_element_type=jnp.float32)  3.79 us
  transfers between devices with their start and end apart: 15, of which 8 were waited for; matrix products, arithmetic and copies ran while one was open for 18% of the time, Pallas kernels for 0%

profile of v7, /device:TPU:0, one launch (start us, length us, event | category | flops | bytes accessed | tf_op | source)
XLA Modules:
  0.0 140.6 jit_solution(16349565489740081941)
XLA Ops:
  7.2 0.0 all-gather.2.cloned.1.call-start
  7.2 0.7 all-gather.2.cloned.1.call-update
  7.9 0.0 reduce-scatter.2.cloned.1.call-start
  8.0 1.2 fusion.42
  9.1 0.0 copy-start
  9.1 2.3 %dynamic-slice_bitcast_fusion.4 = (bf16[256,768]{1,0:T(8,128)(2,1)}, bf16[256,768]{1,0:T(8,128)(2,1)S(1)}, bf16[256,768]{1,0:T(8,128)(2,1)S(1)}, bf16[256,768]{1,0:T(8,128)(2,1)S(1)}) fusion(bf16[1,256,3072]{2,1,0:T(8,128)(2,1)} %param.7, s32[]{:T(128)S(6)} %select_n.65, s32[]{:T(128)S(6)} %select_n.66, s32[]{:T(128)S(6)} %select_n.68, s32[]{:T(128)S(6)} %select_n.67), kind=kLoop, calls=%fused_computation.76 | loop fusion | bytes 3145744 | tf_op jit(solution)/shard_map/dynamic_slice | solution.py:51
  11.4 0.1 fusion.37
  11.5 0.0 copy-start.3
  11.6 1.4 pad_maximum_fusion.5
  12.9 3.9 %collective-permute-start.5 = (bf16[256,1536]{1,0:T(8,128)(2,1)S(1)}, bf16[256,1536]{1,0:T(8,128)(2,1)S(1)}, u32[]{:S(2)}, u32[]{:S(2)}) collective-permute-start(bf16[256,1536]{1,0:T(8,128)(2,1)S(1)} %get-tuple-element.19), channel_id=1, source_target_pairs={{0,24},{8,16},{16,8},{24,0},{1,25},{9,17},{17,9},{25,1},{2,26},{10... | collective-permute-start | bytes 2359304 | tf_op jit(solution)/shard_map/ppermute | solution.py:41
  16.8 0.5 collective-permute-start.4
  17.3 0.1 collective-permute-start.3
  17.4 2.9 %collective-permute-start.8 = (s32[256]{0:T(256)S(1)}, s32[256]{0:T(256)S(1)}, u32[]{:S(2)}, u32[]{:S(2)}) collective-permute-start(s32[256]{0:T(256)S(1)} %bitcast.61), channel_id=1, source_target_pairs={{0,24},{8,16},{16,8},{24,0},{1,25},{9,17},{17,9},{25,1},{2,26},{10... | collective-permute-start | bytes 3080 | tf_op jit(solution)/shard_map/ppermute | solution.py:41
  20.3 0.5 collective-permute-start.7
  20.8 30.5 %collective-permute-done.8 = s32[256]{0:T(256)S(1)} collective-permute-done((s32[256]{0:T(256)S(1)}, s32[256]{0:T(256)S(1)}, u32[]{:S(2)}, u32[]{:S(2)}) %collective-permute-start.8) | collective-permute-done | bytes 1056 | tf_op jit(solution)/shard_map/ppermute | solution.py:41
  51.3 1.7 %collective-permute-start.6 = (s32[256]{0:T(256)S(1)}, s32[256]{0:T(256)S(1)}, u32[]{:S(2)}, u32[]{:S(2)}) collective-permute-start(s32[256]{0:T(256)S(1)} %bitcast.63), channel_id=1, source_target_pairs={{0,8},{8,0},{16,24},{24,16},{1,9},{9,1},{17,25},{25,17},{2,10},{10... | collective-permute-start | bytes 3080 | tf_op jit(solution)/shard_map/ppermute | solution.py:41
  54.3 0.0 collective-permute-done.7
  54.3 0.6 collective-permute-done.6
  54.9 0.0 collective-permute-done.5
  54.9 0.9 fusion.131
  55.8 0.0 collective-permute-done.4
  55.8 2.2 %fusion.130 = (bf16[256,768]{1,0:T(8,128)(2,1)}, bf16[256,768]{1,0:T(8,128)(2,1)}) fusion(bf16[256,1536]{1,0:T(8,128)(2,1)} %collective-permute-done.4), kind=kLoop, calls=%fused_computation.168 | loop fusion | bytes 1572864 | tf_op jit(solution)/shard_map/slice | solution.py:62
  58.1 0.0 collective-permute-done.3
  58.1 1.0 fusion.129
  59.0 5.1 %all-gather.2.cloned.1.call-done = bf16[3072,768]{1,0:T(8,128)(2,1)} async-done(((bf16[384,768]{1,0:T(8,128)(2,1)}), bf16[3072,768]{1,0:T(8,128)(2,1)}) %all-gather.2.cloned.1.call-update) | async-done | bytes 4718608 | tf_op jit(solution)/shard_map/all_gather | solution.py:43
  64.1 3.8 %multiply_reduce_fusion.1 = (f32[256]{0:T(256)S(1)}, f32[256,768]{1,0:T(8,128)S(1)}) fusion(bf16[3072,768]{1,0:T(8,128)(2,1)} %all-gather.2.cloned.1.call-done, bf16[1,256,3072]{2,1,0:T(8,128)(2,1)S(1)} %copy-done.1), kind=kOutput, calls=%fused_computation.60 | convolution fusion | flops 1208352512 | bytes 7078912 | tf_op jit(solution)/shard_map/dot_general | solution.py:65
  67.9 0.1 multiply_convert_fusion.1
  68.0 3.6 %multiply_reduce_fusion = (f32[256]{0:T(256)S(1)}, f32[256,768]{1,0:T(8,128)S(1)}) fusion(f32[256,768]{1,0:T(8,128)S(1)} %get-tuple-element.21, f32[256]{0:T(256)S(1)} %add_rsqrt_fusion, bf16[256,768]{1,0:T(8,128)(2,1)} %get-tuple-element.15, bf16[256,768]{1,0:T(8,128)(2,1)} %get-tuple-element.13, bf16[256,768]{1,0:T(8,128)(2,1)} %get-tuple-element.11, ...), kind=kOutput, calls=%fused_computation.59 | convolution fusion | flops 821624576 | bytes 3546120 | tf_op jit(solution)/shard_map/dot_general | solution.py:89
  71.7 0.9 multiply_convert_fusion
  72.6 2.4 %collective-permute-start.11 = (bf16[256,768]{1,0:T(8,128)(2,1)}, bf16[256,768]{1,0:T(8,128)(2,1)S(1)}, u32[]{:S(2)}, u32[]{:S(2)}) collective-permute-start(bf16[256,768]{1,0:T(8,128)(2,1)} %multiply_convert_fusion), channel_id=1, source_target_pairs={{0,24},{8,16},{16,8},{24,0},{1,25},{9,17},{17,9},{25,1},{2,26},{10... | collective-permute-start | bytes 1179656 | tf_op jit(solution)/shard_map/ppermute | solution.py:41
  75.0 0.6 collective-permute-start.10
  75.5 0.6 collective-permute-start.9
  76.1 9.6 %collective-permute-done.11 = bf16[256,768]{1,0:T(8,128)(2,1)S(1)} collective-permute-done((bf16[256,768]{1,0:T(8,128)(2,1)}, bf16[256,768]{1,0:T(8,128)(2,1)S(1)}, u32[]{:S(2)}, u32[]{:S(2)}) %collective-permute-start.11) | collective-permute-done | bytes 393248 | tf_op jit(solution)/shard_map/ppermute | solution.py:41
  85.7 7.7 %collective-permute-done.10 = bf16[256,768]{1,0:T(8,128)(2,1)S(1)} collective-permute-done((bf16[256,768]{1,0:T(8,128)(2,1)}, bf16[256,768]{1,0:T(8,128)(2,1)S(1)}, u32[]{:S(2)}, u32[]{:S(2)}) %collective-permute-start.10) | collective-permute-done | bytes 393248 | tf_op jit(solution)/shard_map/ppermute | solution.py:41
  93.4 0.1 collective-permute-done.9
  93.5 0.7 copy-done.6
  94.2 0.2 copy-done.7
  94.3 3.3 %fusion = f32[768,768]{1,0:T(8,128)S(1)} fusion(bf16[256,768]{1,0:T(8,128)(2,1)} %get-tuple-element.16, bf16[256,768]{1,0:T(8,128)(2,1)} %get-tuple-element.14, bf16[256,768]{1,0:T(8,128)(2,1)} %get-tuple-element.12, bf16[256,768]{1,0:T(8,128)(2,1)} %get-tuple-element.7, bf16[256,768]{1,0:T(8,128)(2,1)} %copy-done.5, bf16[256,768]{1,0:T(8,128)(2,1)} %copy-done.6, ...), kind=kOutput, calls=%fused_computation | convolution fusion | flops 1220542464 | bytes 5505024 | tf_op jit(solution)/shard_map/dot_general | solution.py:102
  97.6 1.1 dynamic-slice_bitcast_fusion
  98.7 0.0 collective-permute-start.12
  98.7 0.6 iota_add_fusion
  99.3 1.5 %collective-permute-start.1 = (bf16[256,768]{1,0:T(8,128)(2,1)S(1)}, bf16[256,768]{1,0:T(8,128)(2,1)}, u32[]{:S(2)}, u32[]{:S(2)}) collective-permute-start(bf16[256,768]{1,0:T(8,128)(2,1)S(1)} %multiply_convert_fusion.1), channel_id=1, source_target_pairs={{0,16},{8,24},{16,0},{24,8},{1,17},{9,25},{17,1},{25,9},{2,18},{10... | collective-permute-start | bytes 1179656 | tf_op jit(solution)/shard_map/ppermute | solution.py:41
  100.8 1.5 %collective-permute-start.2 = (bf16[256,768]{1,0:T(8,128)(2,1)S(1)}, bf16[256,768]{1,0:T(8,128)(2,1)}, u32[]{:S(2)}, u32[]{:S(2)}) collective-permute-start(bf16[256,768]{1,0:T(8,128)(2,1)S(1)} %multiply_convert_fusion.1), channel_id=1, source_target_pairs={{0,24},{8,16},{16,8},{24,0},{1,25},{9,17},{17,9},{25,1},{2,26},{10... | collective-permute-start | bytes 1179656 | tf_op jit(solution)/shard_map/ppermute | solution.py:41
  102.2 0.6 collective-permute-start
  102.8 1.0 fusion.27
  103.8 0.0 collective-permute-done.12
  103.8 2.4 %bitcast_add_fusion = f32[4,96,768]{2,1,0:T(8,128)} fusion(f32[4,96,768]{2,1,0:T(8,128)} %collective-permute-done.12, f32[4,2,96,768]{3,2,1,0:T(8,128)S(1)} %bitcast.60, s32[]{:T(128)S(6)} %select_n.71), kind=kLoop, calls=%fused_computation.31 | loop fusion | flops 294912 | bytes 3538948 | tf_op jit(solution)/shard_map/add | solution.py:114
  106.2 0.0 reduce-scatter.2.cloned.1.call-update
  106.3 0.0 copy-start.2
  106.3 0.0 copy-start.4
  106.3 1.4 %fusion.90 = f32[256,768]{1,0:T(8,128)S(1)} fusion(bf16[256,768]{1,0:T(8,128)(2,1)S(1)} %multiply_convert_fusion.1, f32[256,256]{0,1:T(8,128)} %fusion.27, f32[]{:T(128)} %bitcast.50, s32[256]{0:T(256)S(1)} %bitcast.65, s32[256]{0:T(256)} %copy-done.8), kind=kOutput, calls=%fused_computation.125 | convolution fusion | flops 101318656 | bytes 1443844 | tf_op jit(solution)/shard_map/dot_general | solution.py:132
  107.7 11.6 %collective-permute-done.1 = bf16[256,768]{1,0:T(8,128)(2,1)} collective-permute-done((bf16[256,768]{1,0:T(8,128)(2,1)S(1)}, bf16[256,768]{1,0:T(8,128)(2,1)}, u32[]{:S(2)}, u32[]{:S(2)}) %collective-permute-start.1) | collective-permute-done | bytes 393248 | tf_op jit(solution)/shard_map/ppermute | solution.py:41
  119.3 1.3 fusion.29
  120.6 0.0 collective-permute-done.2
  120.7 1.3 fusion.30
  122.0 0.0 collective-permute-done
  122.0 0.0 copy-done.2
  122.0 1.9 %fusion.83 = (f32[256]{0:T(256)S(1)}, f32[256]{0:T(256)S(1)}, f32[256]{0:T(256)S(1)}, f32[256]{0:T(256)S(1)}, f32[256,256]{0,1:T(8,128)S(1)}) fusion(s32[256]{0:T(256)S(1)} %bitcast.66, s32[256]{0:T(256)S(1)} %iota_add_fusion.2, f32[256,256]{0,1:T(8,128)S(1)} %fusion.29, s32[256]{0:T(256)S(1)} %get-tuple-element.28, f32[256,256]{0,1:T(8,128)S(1)} %fusion.30, ...), kind=kOutput, calls=%fused_computation.118 | convolution fusion | flops 103676928 | bytes 1844232 | tf_op jit(solution)/shard_map/dot_general | solution.py:123
  123.9 0.6 add_add_fusion
  124.5 1.4 %fusion.94 = f32[256,768]{1,0:T(8,128)S(1)} fusion(bf16[256,768]{1,0:T(8,128)(2,1)} %collective-permute-done.2, f32[256,256]{0,1:T(8,128)S(1)} %fusion.30, f32[]{:T(128)} %bitcast.47, s32[256]{0:T(256)S(1)} %bitcast.67, s32[256]{0:T(256)S(1)} %copy-done.4), kind=kOutput, calls=%fused_computation.126 | convolution fusion | flops 101318656 | bytes 1443844 | tf_op jit(solution)/shard_map/dot_general | solution.py:132
  125.9 1.4 %convolution_add_fusion.1 = f32[256,768]{1,0:T(8,128)S(1)} fusion(f32[256,768]{1,0:T(8,128)S(1)} %fusion.90, bf16[256,768]{1,0:T(8,128)(2,1)} %collective-permute-done, f32[256,256]{0,1:T(8,128)S(1)} %get-tuple-element.22, f32[]{:T(128)} %bitcast.49, s32[256]{0:T(256)S(1)} %bitcast.68, s32[256]{0:T(256)S(1)} %iota_add_fusion.2), kind=kOutput, calls=%fused_computation.30 | convolution fusion | flops 101515264 | bytes 2230276 | tf_op jit(solution)/shard_map/dot_general | solution.py:132
  127.4 1.5 %fusion.38 = (f32[256]{0:T(256)S(1)}, f32[256,768]{1,0:T(8,128)S(1)}) fusion(bf16[1,256,768]{2,1,0:T(8,128)(2,1)S(1)} %copy-done, f32[256]{0:T(256)S(1)} %add_rsqrt_fusion.1, f32[256,768]{1,0:T(8,128)S(1)} %fusion.94, f32[256,768]{1,0:T(8,128)S(1)} %convolution_add_fusion.1, bf16[256,768]{1,0:T(8,128)(2,1)} %collective-permute-done.1, ...), kind=kOutput, calls=%fused_computation.53 | convolution fusion | flops 102498048 | bytes 3411972 | tf_op jit(solution)/shard_map/dot_general | solution.py:132
  128.9 1.0 fusion.49
  129.8 3.9 %reduce-scatter.2.cloned.1.call-done = f32[1,96,768]{2,1,0:T(8,128)} async-done(((f32[4,96,768]{2,1,0:T(8,128)}), f32[1,96,768]{2,1,0:T(8,128)}) %reduce-scatter.2.cloned.1.call-update) | async-done | bytes 294928 | tf_op jit(solution)/shard_map/reduce_scatter | solution.py:116
  (18 shorter events, 0.1 us)
Async XLA Ops:
  7.2 56.9 %all-gather.2.cloned.1.call-start = ((), (), s32[]{:S(2)}) async-start(), calls=%async_computation.1 | async-start | bytes 5308416 | tf_op jit(solution)/shard_map/all_gather | solution.py:43
  7.9 125.8 %reduce-scatter.2.cloned.1.call-start = ((), (), s32[]{:S(2)}) async-start(), calls=%async_computation.2 | async-start | bytes 1474560 | tf_op jit(solution)/shard_map/reduce_scatter | solution.py:116
  9.1 2.3 %copy-start = (bf16[1,256,768]{2,1,0:T(8,128)(2,1)S(1)}, bf16[1,256,768]{2,1,0:T(8,128)(2,1)}, u32[]{:S(2)}) copy-start(bf16[1,256,768]{2,1,0:T(8,128)(2,1)} %param.6) | copy-start | bytes 1179652
  11.5 5.8 %copy-start.3 = (s32[1,256]{1,0:T(1,128)S(1)}, s32[1,256]{1,0:T(1,128)}, u32[]{:S(2)}) copy-start(s32[1,256]{1,0:T(1,128)} %param.9) | copy-start | bytes 3076
  12.9 41.9 %collective-permute-start.5 = (bf16[256,1536]{1,0:T(8,128)(2,1)S(1)}, bf16[256,1536]{1,0:T(8,128)(2,1)S(1)}, u32[]{:S(2)}, u32[]{:S(2)}) collective-permute-start(bf16[256,1536]{1,0:T(8,128)(2,1)S(1)} %get-tuple-element.19), channel_id=1, source_target_pairs={{0,24},{8,16},{16,8},{24,0},{1,25},{9,17},{17,9},{25,1},{2,26},{10... | collective-permute-start | bytes 2359304 | tf_op jit(solution)/shard_map/ppermute | solution.py:41
  16.8 39.0 %collective-permute-start.4 = (bf16[256,1536]{1,0:T(8,128)(2,1)}, bf16[256,1536]{1,0:T(8,128)(2,1)}, u32[]{:S(2)}, u32[]{:S(2)}) collective-permute-start(bf16[256,1536]{1,0:T(8,128)(2,1)} %get-tuple-element.18), channel_id=1, source_target_pairs={{0,16},{8,24},{16,0},{24,8},{1,17},{9,25},{17,1},{25,9},{2,18},{10... | collective-permute-start | bytes 2359304 | tf_op jit(solution)/shard_map/ppermute | solution.py:41
  17.3 40.7 %collective-permute-start.3 = (bf16[256,1536]{1,0:T(8,128)(2,1)}, bf16[256,1536]{1,0:T(8,128)(2,1)S(1)}, u32[]{:S(2)}, u32[]{:S(2)}) collective-permute-start(bf16[256,1536]{1,0:T(8,128)(2,1)} %get-tuple-element.17), channel_id=1, source_target_pairs={{0,8},{8,0},{16,24},{24,16},{1,9},{9,1},{17,25},{25,17},{2,10},{10... | collective-permute-start | bytes 2359304 | tf_op jit(solution)/shard_map/ppermute | solution.py:41
  17.4 33.9 %collective-permute-start.8 = (s32[256]{0:T(256)S(1)}, s32[256]{0:T(256)S(1)}, u32[]{:S(2)}, u32[]{:S(2)}) collective-permute-start(s32[256]{0:T(256)S(1)} %bitcast.61), channel_id=1, source_target_pairs={{0,24},{8,16},{16,8},{24,0},{1,25},{9,17},{17,9},{25,1},{2,26},{10... | collective-permute-start | bytes 3080 | tf_op jit(solution)/shard_map/ppermute | solution.py:41
  20.3 34.0 %collective-permute-start.7 = (s32[256]{0:T(256)S(1)}, s32[256]{0:T(256)S(1)}, u32[]{:S(2)}, u32[]{:S(2)}) collective-permute-start(s32[256]{0:T(256)S(1)} %bitcast.62), channel_id=1, source_target_pairs={{0,16},{8,24},{16,0},{24,8},{1,17},{9,25},{17,1},{25,9},{2,18},{10... | collective-permute-start | bytes 3080 | tf_op jit(solution)/shard_map/ppermute | solution.py:41
  51.3 3.6 %collective-permute-start.6 = (s32[256]{0:T(256)S(1)}, s32[256]{0:T(256)S(1)}, u32[]{:S(2)}, u32[]{:S(2)}) collective-permute-start(s32[256]{0:T(256)S(1)} %bitcast.63), channel_id=1, source_target_pairs={{0,8},{8,0},{16,24},{24,16},{1,9},{9,1},{17,25},{25,17},{2,10},{10... | collective-permute-start | bytes 3080 | tf_op jit(solution)/shard_map/ppermute | solution.py:41
  53.0 15.1 %copy-start.8 = (s32[256]{0:T(256)}, s32[256]{0:T(256)S(1)}, u32[]{:S(2)}) copy-start(s32[256]{0:T(256)S(1)} %iota_add_fusion.3) | copy-start | bytes 3076
  55.8 8.3 %copy-start.1 = (bf16[1,256,3072]{2,1,0:T(8,128)(2,1)S(1)}, bf16[1,256,3072]{2,1,0:T(8,128)(2,1)}, u32[]{:S(2)}) copy-start(bf16[1,256,3072]{2,1,0:T(8,128)(2,1)} %param.7) | copy-start | bytes 4718596
  72.6 13.1 %collective-permute-start.11 = (bf16[256,768]{1,0:T(8,128)(2,1)}, bf16[256,768]{1,0:T(8,128)(2,1)S(1)}, u32[]{:S(2)}, u32[]{:S(2)}) collective-permute-start(bf16[256,768]{1,0:T(8,128)(2,1)} %multiply_convert_fusion), channel_id=1, source_target_pairs={{0,24},{8,16},{16,8},{24,0},{1,25},{9,17},{17,9},{25,1},{2,26},{10... | collective-permute-start | bytes 1179656 | tf_op jit(solution)/shard_map/ppermute | solution.py:41
  75.0 18.4 %collective-permute-start.10 = (bf16[256,768]{1,0:T(8,128)(2,1)}, bf16[256,768]{1,0:T(8,128)(2,1)S(1)}, u32[]{:S(2)}, u32[]{:S(2)}) collective-permute-start(bf16[256,768]{1,0:T(8,128)(2,1)} %multiply_convert_fusion), channel_id=1, source_target_pairs={{0,16},{8,24},{16,0},{24,8},{1,17},{9,25},{17,1},{25,9},{2,18},{10... | collective-permute-start | bytes 1179656 | tf_op jit(solution)/shard_map/ppermute | solution.py:41
  75.5 17.9 %collective-permute-start.9 = (bf16[256,768]{1,0:T(8,128)(2,1)}, bf16[256,768]{1,0:T(8,128)(2,1)S(1)}, u32[]{:S(2)}, u32[]{:S(2)}) collective-permute-start(bf16[256,768]{1,0:T(8,128)(2,1)} %multiply_convert_fusion), channel_id=1, source_target_pairs={{0,8},{8,0},{16,24},{24,16},{1,9},{9,1},{17,25},{25,17},{2,10},{10... | collective-permute-start | bytes 1179656 | tf_op jit(solution)/shard_map/ppermute | solution.py:41
  85.7 7.8 %copy-start.5 = (bf16[256,768]{1,0:T(8,128)(2,1)}, bf16[256,768]{1,0:T(8,128)(2,1)S(1)}, u32[]{:S(2)}) copy-start(bf16[256,768]{1,0:T(8,128)(2,1)S(1)} %collective-permute-done.11) | copy-start | bytes 1179652
  93.4 0.8 copy-start.6
  93.5 0.8 copy-start.7
  98.7 5.1 %collective-permute-start.12 = (f32[4,96,768]{2,1,0:T(8,128)}, f32[4,96,768]{2,1,0:T(8,128)}, u32[]{:S(2)}, u32[]{:S(2)}) collective-permute-start(f32[4,96,768]{2,1,0:T(8,128)} %dynamic-slice_bitcast_fusion), channel_id=1, source_target_pairs={{0,1},{1,0},{2,3},{3,2},{4,5},{5,4},{6,7},{7,6},{8,9},{9,8},{10,11... | collective-permute-start | bytes 3538952 | tf_op jit(solution)/shard_map/ppermute | solution.py:114
  99.3 20.0 %collective-permute-start.1 = (bf16[256,768]{1,0:T(8,128)(2,1)S(1)}, bf16[256,768]{1,0:T(8,128)(2,1)}, u32[]{:S(2)}, u32[]{:S(2)}) collective-permute-start(bf16[256,768]{1,0:T(8,128)(2,1)S(1)} %multiply_convert_fusion.1), channel_id=1, source_target_pairs={{0,16},{8,24},{16,0},{24,8},{1,17},{9,25},{17,1},{25,9},{2,18},{10... | collective-permute-start | bytes 1179656 | tf_op jit(solution)/shard_map/ppermute | solution.py:41
  100.8 19.9 %collective-permute-start.2 = (bf16[256,768]{1,0:T(8,128)(2,1)S(1)}, bf16[256,768]{1,0:T(8,128)(2,1)}, u32[]{:S(2)}, u32[]{:S(2)}) collective-permute-start(bf16[256,768]{1,0:T(8,128)(2,1)S(1)} %multiply_convert_fusion.1), channel_id=1, source_target_pairs={{0,24},{8,16},{16,8},{24,0},{1,25},{9,17},{17,9},{25,1},{2,26},{10... | collective-permute-start | bytes 1179656 | tf_op jit(solution)/shard_map/ppermute | solution.py:41
  102.2 19.7 %collective-permute-start = (bf16[256,768]{1,0:T(8,128)(2,1)S(1)}, bf16[256,768]{1,0:T(8,128)(2,1)}, u32[]{:S(2)}, u32[]{:S(2)}) collective-permute-start(bf16[256,768]{1,0:T(8,128)(2,1)S(1)} %multiply_convert_fusion.1), channel_id=1, source_target_pairs={{0,8},{8,0},{16,24},{24,16},{1,9},{9,1},{17,25},{25,17},{2,10},{10... | collective-permute-start | bytes 1179656 | tf_op jit(solution)/shard_map/ppermute | solution.py:41
  106.3 15.7 %copy-start.2 = (f32[256,256]{0,1:T(8,128)S(1)}, f32[256,256]{0,1:T(8,128)}, u32[]{:S(2)}) copy-start(f32[256,256]{0,1:T(8,128)} %fusion.27) | copy-start | bytes 786436
  106.3 15.7 %copy-start.4 = (s32[256]{0:T(256)S(1)}, s32[256]{0:T(256)}, u32[]{:S(2)}) copy-start(s32[256]{0:T(256)} %get-tuple-element.27) | copy-start | bytes 3076
  106.3 15.7 %copy-start.9 = (s32[256]{0:T(256)S(1)}, s32[256]{0:T(256)}, u32[]{:S(2)}) copy-start(s32[256]{0:T(256)} %copy-done.8) | copy-start | bytes 3076
Sparse Core Ops, SparseCore 0:
  9.6 54.3 all-gather.1
  106.4 27.3 reduce-scatter.1

commit v8 on v6

--- a/solution.py
+++ b/solution.py
@@ -78,6 +78,16 @@
     image_group = jnp.concatenate(image_from, axis=0)
     label_group = jnp.concatenate(label_from, axis=0)
     hidden_group = jnp.concatenate(hidden_from, axis=0)
+    groups = lax.axis_size("group")
+    parity = lax.axis_index("group") % 2
+    owner_rows = chunk // groups
+    by_owner = hidden_group.reshape(hidden_group.shape[0], groups // 2, 2, owner_rows)
+    hidden_keep = lax.dynamic_index_in_dim(by_owner, parity, 2, keepdims=False).reshape(
+        hidden_group.shape[0], chunk // 2
+    )
+    hidden_give = lax.dynamic_index_in_dim(by_owner, 1 - parity, 2, keepdims=False).reshape(
+        hidden_group.shape[0], chunk // 2
+    )
     own_columns = my_index * row_count + local
     scores_t = lax.dot_general(
         image_group, text_unit, (((1,), (1,)), ((), ())), preferred_element_type=jnp.float32
@@ -99,15 +109,19 @@
     grad_from = [projection_output_gradient] + [
         exchange(projection_output_gradient, k) for k in range(1, blocks)
     ]
-    partial = lax.dot_general(
-        hidden_group,
-        jnp.concatenate(grad_from, axis=0),
-        (((0,), (0,)), ((), ())),
-        preferred_element_type=jnp.float32,
-    )
+    grad_group = jnp.concatenate(grad_from, axis=0)
+
+    def rows_for(hidden_part):
+        return lax.dot_general(
+            hidden_part, grad_group, (((0,), (0,)), ((), ())), preferred_element_type=jnp.float32
+        ).reshape(groups // 2, owner_rows, grad_group.shape[1])
+    mate_pairs = [(g, g ^ 1) for g in range(groups)]
+    incoming = lax.ppermute(rows_for(hidden_give), "group", mate_pairs)
+    chip_sum = rows_for(hidden_keep) + incoming
+    same_core = [list(range(p, groups, 2)) for p in range(2)]
     projection_grad = lax.psum_scatter(
-        partial.astype(jnp.bfloat16), "group", scatter_dimension=0, tiled=True
-    ).astype(jnp.float32)
+        chip_sum, "group", scatter_dimension=0, axis_index_groups=same_core, tiled=True
+    ).reshape(owner_rows, grad_group.shape[1])
 
     loss_local = jnp.zeros((row_count,), jnp.float32)
     image_unit_grad = jnp.zeros(image_unit.shape, jnp.float32)

time: 141 us -> 143 us (1.014)
  matrix products: 15.8 us -> 22.9 us
  waiting for transfers between devices: 76.8 us -> 73.3 us
    reduce_scatter x1, waiting for transfers between devices: 15.5 us -> 8.49 us  [body(): lax.psum_scatter(chip_sum, 'group', scatter_dimension=0, axis_index_group...]
    slice x0 -> x3, local copies, waits for them, and re-layouts: none -> 3.13 us  [body(): image_from.append(incoming[:, chunk:])]
    slice x3, local copies, waits for them, and re-layouts: 3.96 us -> 1.25 us  [body(): hidden_from.append(incoming[:, :chunk])]
    dot_general x1 -> x2, matrix products: 4.07 us -> 6.72 us  [rows_for(): lax.dot_general(hidden_part, grad_group, (((0,), (0,)), ((), ())), prefer...]
    dot_general x4, matrix products: 1.87 us -> 3.87 us  [body(): jnp.dot(weights_of(logits, pair_sign), text_from[k], preferred_element_ty...]
    all_gather x1, waiting for transfers between devices: 5.27 us -> 7.07 us  [body(): w_full = lax.all_gather(linear_map_matrix, 'group', axis=0, tiled=True)]
    ppermute x12, waiting for transfers between devices: 55.3 us -> 57 us  [exchange(): return lax.ppermute(value, 'blk', partner_pairs(blocks, step))]
    dot_general x4, matrix products: 1.79 us -> 3.49 us  [body(): lax.dot_general(image_unit, text_from[k], (((1,), (1,)), ((), ())), prefe...]
  transfers between devices with their start and end apart: 14 -> 15, of which waited for: 6 -> 9; matrix products, arithmetic and copies ran while one was open for 13% -> 16% of each run, Pallas kernels for 0% -> 0%
where the time goes in v8:
time: 143 us; the launch traced here: 142 us
  waiting for transfers between devices  73.3 us (51%)
  matrix products  22.9 us (16%)
  starting transfers between devices  16.3 us (11%)
  between operations  15.6 us (11%)
  other arithmetic  8 us (6%)
  local copies, waits for them, and re-layouts  6.12 us (4%)
    ppermute x12, waiting for transfers between devices, exchange(): return lax.ppermute(value, 'blk', partner_pairs(blocks, step))  57 us
    ppermute x12, starting transfers between devices, exchange(): return lax.ppermute(value, 'blk', partner_pairs(blocks, step))  16.3 us
    reduce_scatter x1, waiting for transfers between devices, body(): lax.psum_scatter(chip_sum, 'group', scatter_dimension=0, axis_index_group...  8.49 us
    all_gather x1, waiting for transfers between devices, body(): w_full = lax.all_gather(linear_map_matrix, 'group', axis=0, tiled=True)  7.07 us
    dot_general x2, matrix products, rows_for(): lax.dot_general(hidden_part, grad_group, (((0,), (0,)), ((), ())), prefer...  6.72 us
    dot_general x1, matrix products, body(): lax.dot_general(weights_of(logits_t, pair_sign_t), image_group, (((0,), (...  4.56 us
    dot_general x1, matrix products, body(): projected = jnp.dot(hidden_rows, w_full, preferred_element_type=jnp.float32)  4.28 us
    dot_general x4, matrix products, body(): jnp.dot(weights_of(logits, pair_sign), text_from[k], preferred_element_ty...  3.87 us
  transfers between devices with their start and end apart: 15, of which 9 were waited for; matrix products, arithmetic and copies ran while one was open for 16% of the time, Pallas kernels for 0%

profile of v8, /device:TPU:0, one launch (start us, length us, event | category | flops | bytes accessed | tf_op | source)
XLA Modules:
  0.0 142.3 jit_solution(14928005566482219563)
XLA Ops:
  7.2 0.0 all-gather.2.cloned.1.call-start
  7.2 0.7 all-gather.2.cloned.1.call-update
  7.9 0.0 reduce-scatter.2.cloned.1.call-start
  8.0 1.5 %constant_dynamic-slice_fusion = (bf16[1,256,768]{2,1,0:T(8,128)(2,1)S(1)}, bf16[256,768]{1,0:T(8,128)(2,1)S(1)}, bf16[256,768]{1,0:T(8,128)(2,1)S(1)}, bf16[256,768]{1,0:T(8,128)(2,1)S(1)}) fusion(bf16[1,256,3072]{2,1,0:T(8,128)(2,1)} %param.7, s32[]{:T(128)S(6)} %select_n.65, s32[]{:T(128)S(6)} %select_n.66, s32[]{:T(128)S(6)} %select_n.68, s32[]{:T(128)S(6)} %select_n.67), kind=kLoop, calls=%fused_computation.140 | loop fusion | bytes 3145744 | tf_op jit(solution)/shard_map/dynamic_slice | solution.py:51
  9.5 0.2 fusion.27
  9.7 0.1 fusion.22
  9.8 0.0 copy-start.7
  9.8 1.5 %pad_maximum_fusion.6 = (bf16[256,1536]{1,0:T(8,128)(2,1)}, bf16[256,1536]{1,0:T(8,128)(2,1)}, bf16[256,1536]{1,0:T(8,128)(2,1)}) fusion(bf16[256,768]{1,0:T(8,128)(2,1)S(1)} %fusion.22, bf16[256,768]{1,0:T(8,128)(2,1)S(1)} %get-tuple-element.8, bf16[256,768]{1,0:T(8,128)(2,1)S(1)} %get-tuple-element.10, bf16[256,768]{1,0:T(8,128)(2,1)S(1)} %get-tuple-element.9), kind=kLoop, calls=%fused_computation.33 | loop fusion | flops 3932160 | bytes 3932160 | tf_op jit(solution)/shard_map/concatenate | solution.py:57
  11.4 2.9 %collective-permute-start.3 = (bf16[256,1536]{1,0:T(8,128)(2,1)}, bf16[256,1536]{1,0:T(8,128)(2,1)}, u32[]{:S(2)}, u32[]{:S(2)}) collective-permute-start(bf16[256,1536]{1,0:T(8,128)(2,1)} %get-tuple-element.17), channel_id=1, source_target_pairs={{0,8},{8,0},{16,24},{24,16},{1,9},{9,1},{17,25},{25,17},{2,10},{10... | collective-permute-start | bytes 2359304 | tf_op jit(solution)/shard_map/ppermute | solution.py:41
  14.3 1.5 %collective-permute-start.4 = (bf16[256,1536]{1,0:T(8,128)(2,1)}, bf16[256,1536]{1,0:T(8,128)(2,1)S(1)}, u32[]{:S(2)}, u32[]{:S(2)}) collective-permute-start(bf16[256,1536]{1,0:T(8,128)(2,1)} %get-tuple-element.18), channel_id=1, source_target_pairs={{0,16},{8,24},{16,0},{24,8},{1,17},{9,25},{17,1},{25,9},{2,18},{10... | collective-permute-start | bytes 2359304 | tf_op jit(solution)/shard_map/ppermute | solution.py:41
  15.8 0.0 collective-permute-start.5
  15.8 2.9 %collective-permute-start.8 = (s32[256]{0:T(256)S(1)}, s32[256]{0:T(256)S(1)}, u32[]{:S(2)}, u32[]{:S(2)}) collective-permute-start(s32[256]{0:T(256)S(1)} %bitcast.78), channel_id=1, source_target_pairs={{0,24},{8,16},{16,8},{24,0},{1,25},{9,17},{17,9},{25,1},{2,26},{10... | collective-permute-start | bytes 3080 | tf_op jit(solution)/shard_map/ppermute | solution.py:41
  18.8 0.5 collective-permute-start.7
  19.3 31.0 %collective-permute-done.8 = s32[256]{0:T(256)S(1)} collective-permute-done((s32[256]{0:T(256)S(1)}, s32[256]{0:T(256)S(1)}, u32[]{:S(2)}, u32[]{:S(2)}) %collective-permute-start.8) | collective-permute-done | bytes 1056 | tf_op jit(solution)/shard_map/ppermute | solution.py:41
  50.3 1.4 collective-permute-start.6
  51.7 0.6 iota_add_fusion.3
  53.6 0.0 collective-permute-done.7
  53.6 0.3 collective-permute-done.6
  53.9 0.0 collective-permute-done.3
  53.9 1.2 fusion.122
  55.1 0.0 collective-permute-done.4
  55.1 0.9 fusion.123
  56.0 1.0 fusion.124
  57.0 7.1 %all-gather.2.cloned.1.call-done = bf16[3072,768]{1,0:T(8,128)(2,1)} async-done(((bf16[384,768]{1,0:T(8,128)(2,1)}), bf16[3072,768]{1,0:T(8,128)(2,1)}) %all-gather.2.cloned.1.call-update) | async-done | bytes 4718608 | tf_op jit(solution)/shard_map/all_gather | solution.py:43
  64.1 4.3 %multiply_reduce_fusion.1 = (f32[256]{0:T(256)S(1)}, f32[256,768]{1,0:T(8,128)S(1)}) fusion(bf16[3072,768]{1,0:T(8,128)(2,1)} %all-gather.2.cloned.1.call-done, bf16[1,256,3072]{2,1,0:T(8,128)(2,1)} %param.7), kind=kOutput, calls=%fused_computation.51 | convolution fusion | flops 1208352512 | bytes 7078912 | tf_op jit(solution)/shard_map/dot_general | solution.py:65
  68.4 0.1 multiply_convert_fusion.1
  68.5 0.0 copy-start.1
  68.5 4.6 %multiply_reduce_fusion = (f32[256]{0:T(256)}, f32[256,768]{1,0:T(8,128)}) fusion(f32[256,768]{1,0:T(8,128)S(1)} %get-tuple-element.21, f32[256]{0:T(256)S(1)} %add_rsqrt_fusion, bf16[256,768]{1,0:T(8,128)(2,1)} %get-tuple-element.15, bf16[256,768]{1,0:T(8,128)(2,1)S(1)} %copy-done.5, bf16[256,768]{1,0:T(8,128)(2,1)S(1)} %get-tuple-element.11, ...), kind=kOutput, calls=%fused_computation.49 | convolution fusion | flops 821624576 | bytes 3546120 | tf_op jit(solution)/shard_map/dot_general | solution.py:99
  73.1 2.1 %multiply_convert_fusion = bf16[256,768]{1,0:T(8,128)(2,1)} fusion(f32[256,768]{1,0:T(8,128)} %get-tuple-element.26, f32[256,768]{1,0:T(8,128)S(1)} %get-tuple-element.21, f32[256]{0:T(256)} %get-tuple-element.25, f32[256]{0:T(256)S(1)} %add_rsqrt_fusion), kind=kLoop, calls=%fused_computation.48 | loop fusion | flops 983040 | bytes 1968128 | tf_op jit(solution)/shard_map/convert_element_type | solution.py:108
  75.2 2.4 %collective-permute-start.11 = (bf16[256,768]{1,0:T(8,128)(2,1)}, bf16[256,768]{1,0:T(8,128)(2,1)}, u32[]{:S(2)}, u32[]{:S(2)}) collective-permute-start(bf16[256,768]{1,0:T(8,128)(2,1)} %multiply_convert_fusion), channel_id=1, source_target_pairs={{0,24},{8,16},{16,8},{24,0},{1,25},{9,17},{17,9},{25,1},{2,26},{10... | collective-permute-start | bytes 1179656 | tf_op jit(solution)/shard_map/ppermute | solution.py:41
  77.6 0.6 collective-permute-start.10
  78.1 0.6 collective-permute-start.9
  78.7 0.2 copy.13
  78.9 0.2 copy.10
  79.1 0.2 copy.11
  79.2 0.9 copy.12
  80.2 1.2 pad_maximum_fusion
  81.4 0.0 copy-start.2
  81.4 7.0 %collective-permute-done.11 = bf16[256,768]{1,0:T(8,128)(2,1)} collective-permute-done((bf16[256,768]{1,0:T(8,128)(2,1)}, bf16[256,768]{1,0:T(8,128)(2,1)}, u32[]{:S(2)}, u32[]{:S(2)}) %collective-permute-start.11) | collective-permute-done | bytes 393248 | tf_op jit(solution)/shard_map/ppermute | solution.py:41
  88.4 7.7 %collective-permute-done.10 = bf16[256,768]{1,0:T(8,128)(2,1)} collective-permute-done((bf16[256,768]{1,0:T(8,128)(2,1)}, bf16[256,768]{1,0:T(8,128)(2,1)}, u32[]{:S(2)}, u32[]{:S(2)}) %collective-permute-start.10) | collective-permute-done | bytes 393248 | tf_op jit(solution)/shard_map/ppermute | solution.py:41
  96.1 0.1 collective-permute-done.9
  96.2 3.2 %fusion.28 = f32[4,96,768]{2,1,0:T(8,128)} fusion(bf16[1024,4,2,96]{0,3,2,1:T(8,128)(2,1)S(1)} %pad_maximum_fusion, s32[]{:T(128)S(6)} %select_n.72, bf16[256,768]{1,0:T(8,128)(2,1)} %collective-permute-done.11, bf16[256,768]{1,0:T(8,128)(2,1)} %collective-permute-done.10, bf16[256,768]{1,0:T(8,128)(2,1)} %collective-permute-done.9, ...), kind=kOutput, calls=%fused_computation.44 | convolution fusion | flops 610271232 | bytes 3538948 | tf_op jit(solution)/shard_map/dot_general | solution.py:115
  99.3 0.6 iota_add_fusion
  99.9 1.7 %collective-permute-start.2 = (bf16[256,768]{1,0:T(8,128)(2,1)S(1)}, bf16[256,768]{1,0:T(8,128)(2,1)S(1)}, u32[]{:S(2)}, u32[]{:S(2)}) collective-permute-start(bf16[256,768]{1,0:T(8,128)(2,1)S(1)} %copy-done.2), channel_id=1, source_target_pairs={{0,24},{8,16},{16,8},{24,0},{1,25},{9,17},{17,9},{25,1},{2,26},{10... | collective-permute-start | bytes 1179656 | tf_op jit(solution)/shard_map/ppermute | solution.py:41
  101.6 1.2 collective-permute-start.1
  102.8 0.6 collective-permute-start
  103.4 1.0 fusion.12
  104.4 3.6 %convolution_add_fusion = f32[4,96,768]{2,1,0:T(8,128)} fusion(f32[4,96,768]{2,1,0:T(8,128)} %collective-permute-done.12, bf16[1024,4,2,96]{0,3,2,1:T(8,128)(2,1)S(1)} %pad_maximum_fusion, s32[]{:T(128)S(6)} %select_n.70, bf16[256,768]{1,0:T(8,128)(2,1)} %collective-permute-done.11, bf16[256,768]{1,0:T(8,128)(2,1)} %collective-permute-done.10, ...), kind=kOutput, calls=%fused_computation.5 | convolution fusion | flops 610566144 | bytes 4718596 | tf_op jit(solution)/shard_map/dot_general | solution.py:115
  108.0 0.0 reduce-scatter.2.cloned.1.call-update
  108.0 0.0 copy-start.6
  108.0 0.0 copy-start.8
  108.0 1.4 %fusion.80 = f32[256,768]{1,0:T(8,128)S(1)} fusion(bf16[256,768]{1,0:T(8,128)(2,1)S(1)} %copy-done.2, f32[256,256]{0,1:T(8,128)} %fusion.12, f32[]{:T(128)} %bitcast.65, s32[256]{0:T(256)S(1)} %bitcast.82, s32[256]{0:T(256)} %iota_add_fusion.3), kind=kOutput, calls=%fused_computation.115 | convolution fusion | flops 101318656 | bytes 1443844 | tf_op jit(solution)/shard_map/dot_general | solution.py:138
  109.5 3.3 %collective-permute-done.2 = bf16[256,768]{1,0:T(8,128)(2,1)S(1)} collective-permute-done((bf16[256,768]{1,0:T(8,128)(2,1)S(1)}, bf16[256,768]{1,0:T(8,128)(2,1)S(1)}, u32[]{:S(2)}, u32[]{:S(2)}) %collective-permute-start.2) | collective-permute-done | bytes 393248 | tf_op jit(solution)/shard_map/ppermute | solution.py:41
  112.7 0.3 fusion.15
  113.1 7.7 %collective-permute-done.1 = bf16[256,768]{1,0:T(8,128)(2,1)S(1)} collective-permute-done((bf16[256,768]{1,0:T(8,128)(2,1)S(1)}, bf16[256,768]{1,0:T(8,128)(2,1)S(1)}, u32[]{:S(2)}, u32[]{:S(2)}) %collective-permute-start.1) | collective-permute-done | bytes 393248 | tf_op jit(solution)/shard_map/ppermute | solution.py:41
  120.7 0.3 fusion.14
  121.0 0.0 collective-permute-done
  121.1 1.9 %fusion.73 = (f32[256]{0:T(256)S(1)}, f32[256]{0:T(256)S(1)}, f32[256]{0:T(256)S(1)}, f32[256]{0:T(256)S(1)}, f32[256,256]{0,1:T(8,128)S(1)}) fusion(s32[256]{0:T(256)S(1)} %bitcast.83, s32[256]{0:T(256)S(1)} %iota_add_fusion.2, f32[256,256]{0,1:T(8,128)S(1)} %fusion.14, s32[256]{0:T(256)S(1)} %get-tuple-element.28, f32[256,256]{0,1:T(8,128)S(1)} %fusion.15, ...), kind=kOutput, calls=%fused_computation.108 | convolution fusion | flops 103676928 | bytes 1844232 | tf_op jit(solution)/shard_map/dot_general | solution.py:129
  123.0 0.6 add_add_fusion
  123.5 0.4 fusion.84
  124.0 1.4 %convolution_add_fusion.2 = f32[256,768]{1,0:T(8,128)S(1)} fusion(f32[256,768]{1,0:T(8,128)S(1)} %fusion.80, bf16[256,768]{1,0:T(8,128)(2,1)} %collective-permute-done, f32[256,256]{0,1:T(8,128)S(1)} %get-tuple-element.22, f32[]{:T(128)} %bitcast.64, s32[256]{0:T(256)S(1)} %bitcast.85, s32[256]{0:T(256)S(1)} %iota_add_fusion.2), kind=kOutput, calls=%fused_computation.18 | convolution fusion | flops 101515264 | bytes 2230276 | tf_op jit(solution)/shard_map/dot_general | solution.py:138
  125.5 0.5 fusion.23
  126.0 1.0 fusion.39
  127.0 8.5 %reduce-scatter.2.cloned.1.call-done = f32[1,96,768]{2,1,0:T(8,128)} async-done(((f32[4,96,768]{2,1,0:T(8,128)}), f32[1,96,768]{2,1,0:T(8,128)}) %reduce-scatter.2.cloned.1.call-update) | async-done | bytes 294928 | tf_op jit(solution)/shard_map/reduce_scatter | solution.py:122
  (22 shorter events, 0.1 us)
Async XLA Ops:
  7.2 56.9 %all-gather.2.cloned.1.call-start = ((), (), s32[]{:S(2)}) async-start(), calls=%async_computation.1 | async-start | bytes 5308416 | tf_op jit(solution)/shard_map/all_gather | solution.py:43
  7.9 127.5 %reduce-scatter.2.cloned.1.call-start = ((), (), s32[]{:S(2)}) async-start(), calls=%async_computation.2 | async-start | bytes 1474560 | tf_op jit(solution)/shard_map/reduce_scatter | solution.py:122
  8.0 1.5 %copy-start = (bf16[1,256,768]{2,1,0:T(8,128)(2,1)S(1)}, bf16[1,256,768]{2,1,0:T(8,128)(2,1)}, u32[]{:S(2)}) copy-start(bf16[1,256,768]{2,1,0:T(8,128)(2,1)} %param.6) | copy-start | bytes 1179652
  9.8 6.0 %copy-start.7 = (s32[1,256]{1,0:T(1,128)S(1)}, s32[1,256]{1,0:T(1,128)}, u32[]{:S(2)}) copy-start(s32[1,256]{1,0:T(1,128)} %param.9) | copy-start | bytes 3076
  11.4 42.5 %collective-permute-start.3 = (bf16[256,1536]{1,0:T(8,128)(2,1)}, bf16[256,1536]{1,0:T(8,128)(2,1)}, u32[]{:S(2)}, u32[]{:S(2)}) collective-permute-start(bf16[256,1536]{1,0:T(8,128)(2,1)} %get-tuple-element.17), channel_id=1, source_target_pairs={{0,8},{8,0},{16,24},{24,16},{1,9},{9,1},{17,25},{25,17},{2,10},{10... | collective-permute-start | bytes 2359304 | tf_op jit(solution)/shard_map/ppermute | solution.py:41
  14.3 40.8 %collective-permute-start.4 = (bf16[256,1536]{1,0:T(8,128)(2,1)}, bf16[256,1536]{1,0:T(8,128)(2,1)S(1)}, u32[]{:S(2)}, u32[]{:S(2)}) collective-permute-start(bf16[256,1536]{1,0:T(8,128)(2,1)} %get-tuple-element.18), channel_id=1, source_target_pairs={{0,16},{8,24},{16,0},{24,8},{1,17},{9,25},{17,1},{25,9},{2,18},{10... | collective-permute-start | bytes 2359304 | tf_op jit(solution)/shard_map/ppermute | solution.py:41
  15.8 40.2 %collective-permute-start.5 = (bf16[256,1536]{1,0:T(8,128)(2,1)}, bf16[256,1536]{1,0:T(8,128)(2,1)S(1)}, u32[]{:S(2)}, u32[]{:S(2)}) collective-permute-start(bf16[256,1536]{1,0:T(8,128)(2,1)} %get-tuple-element.19), channel_id=1, source_target_pairs={{0,24},{8,16},{16,8},{24,0},{1,25},{9,17},{17,9},{25,1},{2,26},{10... | collective-permute-start | bytes 2359304 | tf_op jit(solution)/shard_map/ppermute | solution.py:41
  15.8 34.4 %collective-permute-start.8 = (s32[256]{0:T(256)S(1)}, s32[256]{0:T(256)S(1)}, u32[]{:S(2)}, u32[]{:S(2)}) collective-permute-start(s32[256]{0:T(256)S(1)} %bitcast.78), channel_id=1, source_target_pairs={{0,24},{8,16},{16,8},{24,0},{1,25},{9,17},{17,9},{25,1},{2,26},{10... | collective-permute-start | bytes 3080 | tf_op jit(solution)/shard_map/ppermute | solution.py:41
  18.8 34.8 %collective-permute-start.7 = (s32[256]{0:T(256)S(1)}, s32[256]{0:T(256)S(1)}, u32[]{:S(2)}, u32[]{:S(2)}) collective-permute-start(s32[256]{0:T(256)S(1)} %bitcast.79), channel_id=1, source_target_pairs={{0,16},{8,24},{16,0},{24,8},{1,17},{9,25},{17,1},{25,9},{2,18},{10... | collective-permute-start | bytes 3080 | tf_op jit(solution)/shard_map/ppermute | solution.py:41
  50.3 3.6 %collective-permute-start.6 = (s32[256]{0:T(256)S(1)}, s32[256]{0:T(256)S(1)}, u32[]{:S(2)}, u32[]{:S(2)}) collective-permute-start(s32[256]{0:T(256)S(1)} %bitcast.80), channel_id=1, source_target_pairs={{0,8},{8,0},{16,24},{24,16},{1,9},{9,1},{17,25},{25,17},{2,10},{10... | collective-permute-start | bytes 3080 | tf_op jit(solution)/shard_map/ppermute | solution.py:41
  57.0 11.5 %copy-start.5 = (bf16[256,768]{1,0:T(8,128)(2,1)S(1)}, bf16[256,768]{1,0:T(8,128)(2,1)}, u32[]{:S(2)}) copy-start(bf16[256,768]{1,0:T(8,128)(2,1)} %get-tuple-element.13) | copy-start | bytes 1179652
  68.5 4.6 %copy-start.1 = (bf16[256,768]{1,0:T(8,128)(2,1)}, bf16[256,768]{1,0:T(8,128)(2,1)S(1)}, u32[]{:S(2)}) copy-start(bf16[256,768]{1,0:T(8,128)(2,1)S(1)} %multiply_convert_fusion.1) | copy-start | bytes 1179652
  73.1 6.0 %copy-start.3 = (bf16[256,768]{1,0:T(8,128)(2,1)S(1)}, bf16[256,768]{1,0:T(8,128)(2,1)}, u32[]{:S(2)}) copy-start(bf16[256,768]{1,0:T(8,128)(2,1)} %get-tuple-element.14) | copy-start | bytes 1179652
  75.2 4.0 %copy-start.4 = (bf16[256,768]{1,0:T(8,128)(2,1)S(1)}, bf16[256,768]{1,0:T(8,128)(2,1)}, u32[]{:S(2)}) copy-start(bf16[256,768]{1,0:T(8,128)(2,1)} %get-tuple-element.16) | copy-start | bytes 1179652
  75.2 13.2 %collective-permute-start.11 = (bf16[256,768]{1,0:T(8,128)(2,1)}, bf16[256,768]{1,0:T(8,128)(2,1)}, u32[]{:S(2)}, u32[]{:S(2)}) collective-permute-start(bf16[256,768]{1,0:T(8,128)(2,1)} %multiply_convert_fusion), channel_id=1, source_target_pairs={{0,24},{8,16},{16,8},{24,0},{1,25},{9,17},{17,9},{25,1},{2,26},{10... | collective-permute-start | bytes 1179656 | tf_op jit(solution)/shard_map/ppermute | solution.py:41
  77.6 18.5 %collective-permute-start.10 = (bf16[256,768]{1,0:T(8,128)(2,1)}, bf16[256,768]{1,0:T(8,128)(2,1)}, u32[]{:S(2)}, u32[]{:S(2)}) collective-permute-start(bf16[256,768]{1,0:T(8,128)(2,1)} %multiply_convert_fusion), channel_id=1, source_target_pairs={{0,16},{8,24},{16,0},{24,8},{1,17},{9,25},{17,1},{25,9},{2,18},{10... | collective-permute-start | bytes 1179656 | tf_op jit(solution)/shard_map/ppermute | solution.py:41
  78.1 18.0 %collective-permute-start.9 = (bf16[256,768]{1,0:T(8,128)(2,1)}, bf16[256,768]{1,0:T(8,128)(2,1)}, u32[]{:S(2)}, u32[]{:S(2)}) collective-permute-start(bf16[256,768]{1,0:T(8,128)(2,1)} %multiply_convert_fusion), channel_id=1, source_target_pairs={{0,8},{8,0},{16,24},{24,16},{1,9},{9,1},{17,25},{25,17},{2,10},{10... | collective-permute-start | bytes 1179656 | tf_op jit(solution)/shard_map/ppermute | solution.py:41
  81.4 18.5 %copy-start.2 = (bf16[256,768]{1,0:T(8,128)(2,1)S(1)}, bf16[256,768]{1,0:T(8,128)(2,1)}, u32[]{:S(2)}) copy-start(bf16[256,768]{1,0:T(8,128)(2,1)} %copy-done.1) | copy-start | bytes 1179652
  99.3 5.1 %collective-permute-start.12 = (f32[4,96,768]{2,1,0:T(8,128)}, f32[4,96,768]{2,1,0:T(8,128)}, u32[]{:S(2)}, u32[]{:S(2)}) collective-permute-start(f32[4,96,768]{2,1,0:T(8,128)} %fusion.28), channel_id=1, source_target_pairs={{0,1},{1,0},{2,3},{3,2},{4,5},{5,4},{6,7},{7,6},{8,9},{9,8},{10,11... | collective-permute-start | bytes 3538952 | tf_op jit(solution)/shard_map/ppermute | solution.py:119
  99.9 12.9 %collective-permute-start.2 = (bf16[256,768]{1,0:T(8,128)(2,1)S(1)}, bf16[256,768]{1,0:T(8,128)(2,1)S(1)}, u32[]{:S(2)}, u32[]{:S(2)}) collective-permute-start(bf16[256,768]{1,0:T(8,128)(2,1)S(1)} %copy-done.2), channel_id=1, source_target_pairs={{0,24},{8,16},{16,8},{24,0},{1,25},{9,17},{17,9},{25,1},{2,26},{10... | collective-permute-start | bytes 1179656 | tf_op jit(solution)/shard_map/ppermute | solution.py:41
  101.6 19.2 %collective-permute-start.1 = (bf16[256,768]{1,0:T(8,128)(2,1)S(1)}, bf16[256,768]{1,0:T(8,128)(2,1)S(1)}, u32[]{:S(2)}, u32[]{:S(2)}) collective-permute-start(bf16[256,768]{1,0:T(8,128)(2,1)S(1)} %copy-done.2), channel_id=1, source_target_pairs={{0,16},{8,24},{16,0},{24,8},{1,17},{9,25},{17,1},{25,9},{2,18},{10... | collective-permute-start | bytes 1179656 | tf_op jit(solution)/shard_map/ppermute | solution.py:41
  102.8 18.2 %collective-permute-start = (bf16[256,768]{1,0:T(8,128)(2,1)S(1)}, bf16[256,768]{1,0:T(8,128)(2,1)}, u32[]{:S(2)}, u32[]{:S(2)}) collective-permute-start(bf16[256,768]{1,0:T(8,128)(2,1)S(1)} %copy-done.2), channel_id=1, source_target_pairs={{0,8},{8,0},{16,24},{24,16},{1,9},{9,1},{17,25},{25,17},{2,10},{10... | collective-permute-start | bytes 1179656 | tf_op jit(solution)/shard_map/ppermute | solution.py:41
  108.0 13.1 %copy-start.6 = (f32[256,256]{0,1:T(8,128)S(1)}, f32[256,256]{0,1:T(8,128)}, u32[]{:S(2)}) copy-start(f32[256,256]{0,1:T(8,128)} %fusion.12) | copy-start | bytes 786436
  108.0 13.1 %copy-start.8 = (s32[256]{0:T(256)S(1)}, s32[256]{0:T(256)}, u32[]{:S(2)}) copy-start(s32[256]{0:T(256)} %get-tuple-element.27) | copy-start | bytes 3076
  108.0 13.1 %copy-start.9 = (s32[256]{0:T(256)S(1)}, s32[256]{0:T(256)}, u32[]{:S(2)}) copy-start(s32[256]{0:T(256)} %iota_add_fusion.3) | copy-start | bytes 3076
Sparse Core Ops, SparseCore 0:
  9.6 54.3 all-gather.1
  108.1 27.2 reduce-scatter.1

commit v9 on v4

--- a/solution.py
+++ b/solution.py
@@ -40,7 +40,14 @@
     def exchange(value, step):
         return lax.ppermute(value, "blk", partner_pairs(blocks, step))
 
-    w_full = lax.all_gather(linear_map_matrix, "group", axis=0, tiled=True)
+    groups = lax.axis_size("group")
+    parity = lax.axis_index("group") % 2
+    same_core = [list(range(p, groups, 2)) for p in range(2)]
+    w_own = lax.all_gather(linear_map_matrix, "group", axis=0, axis_index_groups=same_core)
+    shard_rows = linear_map_matrix.shape[0]
+    hidden_by_shard = hidden_rows.reshape(hidden_rows.shape[0], groups // 2, 2, shard_rows)
+    hidden_own = lax.dynamic_index_in_dim(hidden_by_shard, parity, 2, keepdims=False)
+    hidden_mate = lax.dynamic_index_in_dim(hidden_by_shard, 1 - parity, 2, keepdims=False)
 
     image_float = image_rows.astype(jnp.float32)
     image_scale = lax.rsqrt(jnp.sum(image_float * image_float, axis=1, keepdims=True) + epsilon)
@@ -62,7 +69,14 @@
         image_from.append(incoming[:, chunk:])
         label_from.append(exchange(label_rows, k))
 
-    projected = jnp.dot(hidden_rows, w_full, preferred_element_type=jnp.float32)
+    contract = (((1, 2), (0, 1)), ((), ()))
+    w_own, hidden_from, image_from, label_from = lax.optimization_barrier(
+        (w_own, hidden_from, image_from, label_from)
+    )
+    w_mate = lax.ppermute(w_own, "group", [(g, g ^ 1) for g in range(groups)])
+    projected = lax.dot_general(
+        hidden_own, w_own, contract, preferred_element_type=jnp.float32
+    ) + lax.dot_general(hidden_mate, w_mate, contract, preferred_element_type=jnp.float32)
     text_scale = lax.rsqrt(jnp.sum(projected * projected, axis=1, keepdims=True) + epsilon)
     text_dir = projected * text_scale
     text_unit = text_dir.astype(jnp.bfloat16)

time: 139 us -> 144 us (1.036)
  local copies, waits for them, and re-layouts: 6.27 us -> 12.4 us
  other arithmetic: 5.82 us -> 3.35 us
  waiting for transfers between devices: 79.3 us -> 81.4 us
    all_gather x1, waiting for transfers between devices: 5.26 us -> 10.7 us  [body(): lax.all_gather(linear_map_matrix, 'group', axis=0, axis_index_groups=same...]
    dynamic_slice x1 -> x2, local copies, waits for them, and re-layouts: 2.26 us -> 5.51 us  [the longest x1 3.24 us: body(): lax.dynamic_index_in_dim(hidden_by_shard, parity, 2, keepdims=False)]
    unnamed x14 -> x41, local copies, waits for them, and re-layouts: 0.03 us -> 2.84 us
    ppermute x12, waiting for transfers between devices: 63.4 us -> 60.7 us  [exchange(): return lax.ppermute(value, 'blk', partner_pairs(blocks, step))]
    dot_general x1 -> x2, matrix products: 3.79 us -> 3.45 us  [the longest x1 2.59 us: body(): lax.dot_general(hidden_mate, w_mate, contract, preferred_element_type=jnp...]
  transfers between devices with their start and end apart: 14 -> 15, of which waited for: 8 -> 9; matrix products, arithmetic and copies ran while one was open for 11% -> 11% of each run, Pallas kernels for 0% -> 0%
where the time goes in v9:
time: 144 us
  waiting for transfers between devices  81.4 us (57%)
  starting transfers between devices  17.1 us (12%)
  between operations  15.8 us (11%)
  matrix products  13.9 us (10%)
  local copies, waits for them, and re-layouts  12.4 us (9%)
  other arithmetic  3.35 us (2%)
    ppermute x12, waiting for transfers between devices, exchange(): return lax.ppermute(value, 'blk', partner_pairs(blocks, step))  60.7 us
    ppermute x12, starting transfers between devices, exchange(): return lax.ppermute(value, 'blk', partner_pairs(blocks, step))  17.1 us
    all_gather x1, waiting for transfers between devices, body(): lax.all_gather(linear_map_matrix, 'group', axis=0, axis_index_groups=same...  10.7 us
    reduce_scatter x1, waiting for transfers between devices, body(): lax.psum_scatter(partial, 'group', scatter_dimension=0, tiled=True)  9.33 us
    dot_general x1, matrix products, body(): lax.dot_general(weights_of(logits_t, pair_sign_t), image_group, (((0,), (...  3.89 us
    dynamic_slice x1, local copies, waits for them, and re-layouts, body(): lax.dynamic_index_in_dim(hidden_by_shard, parity, 2, keepdims=False)  3.24 us
    dot_general x1, matrix products, body(): lax.dot_general(hidden_group, jnp.concatenate(grad_from, axis=0), (((0,),...  2.9 us
  transfers between devices with their start and end apart: 15, of which 9 were waited for; matrix products, arithmetic and copies ran while one was open for 11% of the time, Pallas kernels for 0%

profile of v9, /device:TPU:0, one launch (start us, length us, event | category | flops | bytes accessed | tf_op | source)
XLA Modules:
  0.0 144.0 jit_solution(9128487693771043724)
XLA Ops:
  7.2 0.0 all-gather.3.cloned.1.call-start
  7.2 0.7 all-gather.3.cloned.1.call-update
  7.9 0.0 reduce-scatter.2.cloned.1.call-start
  8.0 1.2 fusion.41
  9.1 0.0 copy-start.1
  9.1 2.3 %dynamic-slice_bitcast_fusion = (bf16[256,768]{1,0:T(8,128)(2,1)S(1)}, bf16[256,768]{1,0:T(8,128)(2,1)S(1)}, bf16[256,768]{1,0:T(8,128)(2,1)}, bf16[256,768]{1,0:T(8,128)(2,1)S(1)}) fusion(bf16[1,256,3072]{2,1,0:T(8,128)(2,1)} %param.7, s32[]{:T(128)S(6)} %select_n.63, s32[]{:T(128)S(6)} %select_n.61, s32[]{:T(128)S(6)} %select_n.60, s32[]{:T(128)S(6)} %select_n.62), kind=kLoop, calls=%fused_computation.73 | loop fusion | bytes 3145744 | tf_op jit(solution)/shard_map/dynamic_slice | solution.py:65
  11.4 0.1 fusion.36
  11.5 0.0 copy-start.12
  11.6 0.2 pad_maximum_fusion
  11.8 4.0 %collective-permute-start.2 = (bf16[256,1536]{1,0:T(8,128)(2,1)S(1)}, bf16[256,1536]{1,0:T(8,128)(2,1)S(1)}, u32[]{:S(2)}, u32[]{:S(2)}) collective-permute-start(bf16[256,1536]{1,0:T(8,128)(2,1)S(1)} %get-tuple-element.45), channel_id=1, source_target_pairs={{0,24},{8,16},{16,8},{24,0},{1,25},{9,17},{17,9},{25,1},{2,26},{10... | collective-permute-start | bytes 2359304 | tf_op jit(solution)/shard_map/ppermute | solution.py:41
  15.7 0.5 collective-permute-start.1
  16.2 0.1 collective-permute-start
  16.4 2.8 %collective-permute-start.5 = (s32[256]{0:T(256)S(1)}, s32[256]{0:T(256)S(1)}, u32[]{:S(2)}, u32[]{:S(2)}) collective-permute-start(s32[256]{0:T(256)S(1)} %bitcast.68), channel_id=1, source_target_pairs={{0,24},{8,16},{16,8},{24,0},{1,25},{9,17},{17,9},{25,1},{2,26},{10... | collective-permute-start | bytes 3080 | tf_op jit(solution)/shard_map/ppermute | solution.py:41
  19.2 0.5 collective-permute-start.4
  19.7 14.4 %collective-permute-done.2 = bf16[256,1536]{1,0:T(8,128)(2,1)S(1)} collective-permute-done((bf16[256,1536]{1,0:T(8,128)(2,1)S(1)}, bf16[256,1536]{1,0:T(8,128)(2,1)S(1)}, u32[]{:S(2)}, u32[]{:S(2)}) %collective-permute-start.2) | collective-permute-done | bytes 786464 | tf_op jit(solution)/shard_map/ppermute | solution.py:41
  34.1 2.0 %collective-permute-start.3 = (s32[256]{0:T(256)S(1)}, s32[256]{0:T(256)S(1)}, u32[]{:S(2)}, u32[]{:S(2)}) collective-permute-start(s32[256]{0:T(256)S(1)} %bitcast.70), channel_id=1, source_target_pairs={{0,8},{8,0},{16,24},{24,16},{1,9},{9,1},{17,25},{25,17},{2,10},{10... | collective-permute-start | bytes 3080 | tf_op jit(solution)/shard_map/ppermute | solution.py:41
  36.1 1.0 fusion.126
  37.1 13.0 %collective-permute-done.1 = bf16[256,1536]{1,0:T(8,128)(2,1)S(1)} collective-permute-done((bf16[256,1536]{1,0:T(8,128)(2,1)S(1)}, bf16[256,1536]{1,0:T(8,128)(2,1)S(1)}, u32[]{:S(2)}, u32[]{:S(2)}) %collective-permute-start.1) | collective-permute-done | bytes 786464 | tf_op jit(solution)/shard_map/ppermute | solution.py:41
  50.1 0.9 fusion.127
  51.1 0.0 collective-permute-done
  51.1 0.9 fusion.128
  52.0 0.0 collective-permute-done.4
  52.0 0.0 copy-start.15
  52.0 0.0 collective-permute-done.3
  52.1 10.7 %all-gather.3.cloned.1.call-done = bf16[1536,768]{1,0:T(8,128)(2,1)} async-done(((bf16[384,768]{1,0:T(8,128)(2,1)}), bf16[1536,768]{1,0:T(8,128)(2,1)}) %all-gather.3.cloned.1.call-update) | async-done | bytes 2359312 | tf_op jit(solution)/shard_map/all_gather | solution.py:46
  62.8 1.2 reshape_squeeze.3
  65.3 0.0 copy-start.14
  65.3 0.0 copy-start.16
  65.4 3.2 %constant_dynamic-slice_fusion.1 = (bf16[256,4,1,384]{3,2,1,0:T(2,128)(2,1)S(1)}, bf16[256,4,1,384]{3,2,1,0:T(2,128)(2,1)S(1)}) fusion(bf16[256,4,2,384]{3,2,1,0:T(2,128)(2,1)S(1)} %reshape_squeeze.3, s32[]{:T(128)S(6)} %select_n.59, s32[]{:T(128)S(6)} %select_n.64), kind=kLoop, calls=%fused_computation.153 | loop fusion | bytes 3145736 | tf_op jit(solution)/shard_map/jit(dynamic_index_in_dim)/dynamic_slice | solution.py:49
  68.8 0.9 copy-done.5
  69.7 0.1 copy-done.4
  69.8 1.2 copy-done.11
  71.0 2.6 %convolution_bitcast_fusion = f32[256,768]{1,0:T(8,128)S(1)} fusion(bf16[4,384,768]{2,1,0:T(8,128)(2,1)} %collective-permute-done.6, bf16[256,4,1,384]{3,2,1,0:T(2,128)(2,1)S(1)} %get-tuple-element.34), kind=kOutput, calls=%fused_computation.25 | convolution fusion | flops 603979776 | bytes 3932160 | tf_op jit(solution)/shard_map/dot_general | solution.py:79
  73.6 0.9 multiply_reduce_fusion.1
  74.5 0.1 multiply_convert_fusion.1
  74.6 3.9 %multiply_reduce_fusion = (f32[256]{0:T(256)S(1)}, f32[256,768]{1,0:T(8,128)S(1)}) fusion(f32[256,768]{1,0:T(8,128)S(1)} %get-tuple-element.49, f32[256]{0:T(256)S(1)} %add_rsqrt_fusion, bf16[1024,768]{1,0:T(8,128)(2,1)} %copy-done.11, bf16[256,768]{1,0:T(8,128)(2,1)S(1)} %multiply_convert_fusion.1, f32[]{:T(128)} %bitcast.62, f32[]{:T(128)} %bitcast.53, ...), kind=kOutput, calls=%fused_computation.59 | convolution fusion | flops 809041664 | bytes 3546120 | tf_op jit(solution)/shard_map/dot_general | solution.py:103
  78.5 0.0 copy-start.10
  78.5 0.2 multiply_convert_fusion
  78.7 2.4 %collective-permute-start.12 = (bf16[256,768]{1,0:T(8,128)(2,1)S(1)}, bf16[256,768]{1,0:T(8,128)(2,1)S(1)}, u32[]{:S(2)}, u32[]{:S(2)}) collective-permute-start(bf16[256,768]{1,0:T(8,128)(2,1)S(1)} %multiply_convert_fusion), channel_id=1, source_target_pairs={{0,24},{8,16},{16,8},{24,0},{1,25},{9,17},{17,9},{25,1},{2,26},{10... | collective-permute-start | bytes 1179656 | tf_op jit(solution)/shard_map/ppermute | solution.py:41
  81.2 0.5 collective-permute-start.11
  81.7 0.6 collective-permute-start.10
  82.3 9.4 %collective-permute-done.12 = bf16[256,768]{1,0:T(8,128)(2,1)S(1)} collective-permute-done((bf16[256,768]{1,0:T(8,128)(2,1)S(1)}, bf16[256,768]{1,0:T(8,128)(2,1)S(1)}, u32[]{:S(2)}, u32[]{:S(2)}) %collective-permute-start.12) | collective-permute-done | bytes 393248 | tf_op jit(solution)/shard_map/ppermute | solution.py:41
  91.6 8.0 %collective-permute-done.11 = bf16[256,768]{1,0:T(8,128)(2,1)S(1)} collective-permute-done((bf16[256,768]{1,0:T(8,128)(2,1)S(1)}, bf16[256,768]{1,0:T(8,128)(2,1)S(1)}, u32[]{:S(2)}, u32[]{:S(2)}) %collective-permute-start.11) | collective-permute-done | bytes 393248 | tf_op jit(solution)/shard_map/ppermute | solution.py:41
  99.6 0.1 collective-permute-done.10
  99.7 2.9 %fusion = f32[768,768]{1,0:T(8,128)} fusion(bf16[256,768]{1,0:T(8,128)(2,1)S(1)} %copy-done.7, bf16[256,768]{1,0:T(8,128)(2,1)S(1)} %copy-done.8, bf16[256,768]{1,0:T(8,128)(2,1)S(1)} %copy-done.9, bf16[256,768]{1,0:T(8,128)(2,1)S(1)} %copy-done.10, bf16[256,768]{1,0:T(8,128)(2,1)S(1)} %collective-permute-done.12, ...), kind=kOutput, calls=%fused_computation | convolution fusion | flops 1220542464 | bytes 5505024 | tf_op jit(solution)/shard_map/dot_general | solution.py:116
  102.6 0.0 reduce-scatter.2.cloned.1.call-update
  102.6 1.8 %collective-permute-start.9 = (bf16[256,768]{1,0:T(8,128)(2,1)S(1)}, bf16[256,768]{1,0:T(8,128)(2,1)S(1)}, u32[]{:S(2)}, u32[]{:S(2)}) collective-permute-start(bf16[256,768]{1,0:T(8,128)(2,1)S(1)} %multiply_convert_fusion.1), channel_id=1, source_target_pairs={{0,24},{8,16},{16,8},{24,0},{1,25},{9,17},{17,9},{25,1},{2,26},{10... | collective-permute-start | bytes 1179656 | tf_op jit(solution)/shard_map/ppermute | solution.py:41
  104.4 1.2 collective-permute-start.8
  105.6 0.6 collective-permute-start.7
  106.2 0.3 fusion.26
  106.5 0.4 fusion.89
  106.9 8.7 %collective-permute-done.9 = bf16[256,768]{1,0:T(8,128)(2,1)S(1)} collective-permute-done((bf16[256,768]{1,0:T(8,128)(2,1)S(1)}, bf16[256,768]{1,0:T(8,128)(2,1)S(1)}, u32[]{:S(2)}, u32[]{:S(2)}) %collective-permute-start.9) | collective-permute-done | bytes 393248 | tf_op jit(solution)/shard_map/ppermute | solution.py:41
  115.6 0.3 fusion.29
  115.9 7.1 %collective-permute-done.8 = bf16[256,768]{1,0:T(8,128)(2,1)S(1)} collective-permute-done((bf16[256,768]{1,0:T(8,128)(2,1)S(1)}, bf16[256,768]{1,0:T(8,128)(2,1)S(1)}, u32[]{:S(2)}, u32[]{:S(2)}) %collective-permute-start.8) | collective-permute-done | bytes 393248 | tf_op jit(solution)/shard_map/ppermute | solution.py:41
  123.0 0.3 fusion.28
  123.4 0.9 fusion.82
  124.3 0.6 add_add_fusion
  124.8 0.4 fusion.93
  125.3 0.0 copy-start.2
  125.3 0.4 convolution_add_fusion.1
  125.7 0.5 copy-done.2
  126.3 0.5 fusion.37
  126.8 1.0 fusion.48
  127.8 9.3 %reduce-scatter.2.cloned.1.call-done = f32[96,768]{1,0:T(8,128)} async-done(((f32[768,768]{1,0:T(8,128)}), f32[96,768]{1,0:T(8,128)}) %reduce-scatter.2.cloned.1.call-update) | async-done | bytes 294928 | tf_op jit(solution)/shard_map/reduce_scatter | solution.py:122
  (40 shorter events, 0.2 us)
Async XLA Ops:
  7.2 55.6 %all-gather.3.cloned.1.call-start = ((), (), s32[]{:S(2)}) async-start(), calls=%async_computation.2 | async-start | bytes 2949120 | tf_op jit(solution)/shard_map/all_gather | solution.py:46
  7.9 129.2 %reduce-scatter.2.cloned.1.call-start = ((), (), s32[]{:S(2)}) async-start(), calls=%async_computation.1 | async-start | bytes 2654208 | tf_op jit(solution)/shard_map/reduce_scatter | solution.py:122
  9.1 2.3 %copy-start.1 = (bf16[1,256,768]{2,1,0:T(8,128)(2,1)S(1)}, bf16[1,256,768]{2,1,0:T(8,128)(2,1)}, u32[]{:S(2)}) copy-start(bf16[1,256,768]{2,1,0:T(8,128)(2,1)} %param.6) | copy-start | bytes 1179652
  11.5 4.8 %copy-start.12 = (s32[1,256]{1,0:T(1,128)S(1)}, s32[1,256]{1,0:T(1,128)}, u32[]{:S(2)}) copy-start(s32[1,256]{1,0:T(1,128)} %param.9) | copy-start | bytes 3076
  11.8 22.4 %collective-permute-start.2 = (bf16[256,1536]{1,0:T(8,128)(2,1)S(1)}, bf16[256,1536]{1,0:T(8,128)(2,1)S(1)}, u32[]{:S(2)}, u32[]{:S(2)}) collective-permute-start(bf16[256,1536]{1,0:T(8,128)(2,1)S(1)} %get-tuple-element.45), channel_id=1, source_target_pairs={{0,24},{8,16},{16,8},{24,0},{1,25},{9,17},{17,9},{25,1},{2,26},{10... | collective-permute-start | bytes 2359304 | tf_op jit(solution)/shard_map/ppermute | solution.py:41
  15.7 34.4 %collective-permute-start.1 = (bf16[256,1536]{1,0:T(8,128)(2,1)S(1)}, bf16[256,1536]{1,0:T(8,128)(2,1)S(1)}, u32[]{:S(2)}, u32[]{:S(2)}) collective-permute-start(bf16[256,1536]{1,0:T(8,128)(2,1)S(1)} %get-tuple-element.46), channel_id=1, source_target_pairs={{0,16},{8,24},{16,0},{24,8},{1,17},{9,25},{17,1},{25,9},{2,18},{10... | collective-permute-start | bytes 2359304 | tf_op jit(solution)/shard_map/ppermute | solution.py:41
  16.2 34.9 %collective-permute-start = (bf16[256,1536]{1,0:T(8,128)(2,1)S(1)}, bf16[256,1536]{1,0:T(8,128)(2,1)S(1)}, u32[]{:S(2)}, u32[]{:S(2)}) collective-permute-start(bf16[256,1536]{1,0:T(8,128)(2,1)S(1)} %get-tuple-element.47), channel_id=1, source_target_pairs={{0,8},{8,0},{16,24},{24,16},{1,9},{9,1},{17,25},{25,17},{2,10},{10... | collective-permute-start | bytes 2359304 | tf_op jit(solution)/shard_map/ppermute | solution.py:41
  16.4 35.7 %collective-permute-start.5 = (s32[256]{0:T(256)S(1)}, s32[256]{0:T(256)S(1)}, u32[]{:S(2)}, u32[]{:S(2)}) collective-permute-start(s32[256]{0:T(256)S(1)} %bitcast.68), channel_id=1, source_target_pairs={{0,24},{8,16},{16,8},{24,0},{1,25},{9,17},{17,9},{25,1},{2,26},{10... | collective-permute-start | bytes 3080 | tf_op jit(solution)/shard_map/ppermute | solution.py:41
  19.2 32.8 %collective-permute-start.4 = (s32[256]{0:T(256)S(1)}, s32[256]{0:T(256)S(1)}, u32[]{:S(2)}, u32[]{:S(2)}) collective-permute-start(s32[256]{0:T(256)S(1)} %bitcast.69), channel_id=1, source_target_pairs={{0,16},{8,24},{16,0},{24,8},{1,17},{9,25},{17,1},{25,9},{2,18},{10... | collective-permute-start | bytes 3080 | tf_op jit(solution)/shard_map/ppermute | solution.py:41
  34.1 17.9 %collective-permute-start.3 = (s32[256]{0:T(256)S(1)}, s32[256]{0:T(256)S(1)}, u32[]{:S(2)}, u32[]{:S(2)}) collective-permute-start(s32[256]{0:T(256)S(1)} %bitcast.70), channel_id=1, source_target_pairs={{0,8},{8,0},{16,24},{24,16},{1,9},{9,1},{17,25},{25,17},{2,10},{10... | collective-permute-start | bytes 3080 | tf_op jit(solution)/shard_map/ppermute | solution.py:41
  37.1 25.7 %copy-start = (bf16[1,256,3072]{2,1,0:T(8,128)(2,1)S(1)}, bf16[1,256,3072]{2,1,0:T(8,128)(2,1)}, u32[]{:S(2)}) copy-start(bf16[1,256,3072]{2,1,0:T(8,128)(2,1)} %param.7) | copy-start | bytes 4718596
  52.0 10.8 %copy-start.13 = (s32[256]{0:T(256)}, s32[256]{0:T(256)S(1)}, u32[]{:S(2)}) copy-start(s32[256]{0:T(256)S(1)} %collective-permute-done.5) | copy-start | bytes 3076
  52.0 10.8 %copy-start.15 = (s32[256]{0:T(256)}, s32[256]{0:T(256)S(1)}, u32[]{:S(2)}) copy-start(s32[256]{0:T(256)S(1)} %collective-permute-done.4) | copy-start | bytes 3076
  52.0 10.8 %copy-start.17 = (s32[256]{0:T(256)}, s32[256]{0:T(256)S(1)}, u32[]{:S(2)}) copy-start(s32[256]{0:T(256)S(1)} %collective-permute-done.3) | copy-start | bytes 3076
  62.8 7.0 %collective-permute-start.6 = (bf16[4,384,768]{2,1,0:T(8,128)(2,1)}, bf16[4,384,768]{2,1,0:T(8,128)(2,1)}, u32[]{:S(2)}, u32[]{:S(2)}) collective-permute-start(bf16[4,384,768]{2,1,0:T(8,128)(2,1)} %bitcast.66), channel_id=1, source_target_pairs={{0,1},{1,0},{2,3},{3,2},{4,5},{5,4},{6,7},{7,6},{8,9},{9,8},{10,11... | collective-permute-start | bytes 7077896 | tf_op jit(solution)/shard_map/ppermute | solution.py:76
  65.3 3.3 %copy-start.14 = (s32[256]{0:T(256)S(1)}, s32[256]{0:T(256)}, u32[]{:S(2)}) copy-start(s32[256]{0:T(256)} %copy-done.13) | copy-start | bytes 3076
  65.3 3.3 %copy-start.16 = (s32[256]{0:T(256)S(1)}, s32[256]{0:T(256)}, u32[]{:S(2)}) copy-start(s32[256]{0:T(256)} %copy-done.15) | copy-start | bytes 3076
  65.4 3.3 %copy-start.18 = (s32[256]{0:T(256)S(1)}, s32[256]{0:T(256)}, u32[]{:S(2)}) copy-start(s32[256]{0:T(256)} %copy-done.17) | copy-start | bytes 3076
  65.4 3.4 %copy-start.6 = (bf16[256,768]{1,0:T(8,128)(2,1)S(1)}, bf16[256,768]{1,0:T(8,128)(2,1)}, u32[]{:S(2)}) copy-start(bf16[256,768]{1,0:T(8,128)(2,1)} %get-tuple-element.26) | copy-start | bytes 1179652
  68.7 1.0 copy-start.5
  68.7 1.1 copy-start.4
  69.8 1.2 copy-start.11
  71.0 2.6 %copy-start.3 = (bf16[1536,768]{1,0:T(8,128)(2,1)S(1)}, bf16[1536,768]{1,0:T(8,128)(2,1)}, u32[]{:S(2)}) copy-start(bf16[1536,768]{1,0:T(8,128)(2,1)} %all-gather.3.cloned.1.call-done) | copy-start | bytes 7077892
  78.5 21.2 %copy-start.7 = (bf16[256,768]{1,0:T(8,128)(2,1)S(1)}, bf16[256,768]{1,0:T(8,128)(2,1)}, u32[]{:S(2)}) copy-start(bf16[256,768]{1,0:T(8,128)(2,1)} %get-tuple-element.20) | copy-start | bytes 1179652
  78.5 21.2 %copy-start.8 = (bf16[256,768]{1,0:T(8,128)(2,1)S(1)}, bf16[256,768]{1,0:T(8,128)(2,1)}, u32[]{:S(2)}) copy-start(bf16[256,768]{1,0:T(8,128)(2,1)} %get-tuple-element.19) | copy-start | bytes 1179652
  78.5 21.2 %copy-start.9 = (bf16[256,768]{1,0:T(8,128)(2,1)S(1)}, bf16[256,768]{1,0:T(8,128)(2,1)}, u32[]{:S(2)}) copy-start(bf16[256,768]{1,0:T(8,128)(2,1)} %get-tuple-element.18) | copy-start | bytes 1179652
  78.5 21.2 %copy-start.10 = (bf16[256,768]{1,0:T(8,128)(2,1)S(1)}, bf16[256,768]{1,0:T(8,128)(2,1)}, u32[]{:S(2)}) copy-start(bf16[256,768]{1,0:T(8,128)(2,1)} %get-tuple-element.17) | copy-start | bytes 1179652
  78.7 12.9 %collective-permute-start.12 = (bf16[256,768]{1,0:T(8,128)(2,1)S(1)}, bf16[256,768]{1,0:T(8,128)(2,1)S(1)}, u32[]{:S(2)}, u32[]{:S(2)}) collective-permute-start(bf16[256,768]{1,0:T(8,128)(2,1)S(1)} %multiply_convert_fusion), channel_id=1, source_target_pairs={{0,24},{8,16},{16,8},{24,0},{1,25},{9,17},{17,9},{25,1},{2,26},{10... | collective-permute-start | bytes 1179656 | tf_op jit(solution)/shard_map/ppermute | solution.py:41
  81.2 18.5 %collective-permute-start.11 = (bf16[256,768]{1,0:T(8,128)(2,1)S(1)}, bf16[256,768]{1,0:T(8,128)(2,1)S(1)}, u32[]{:S(2)}, u32[]{:S(2)}) collective-permute-start(bf16[256,768]{1,0:T(8,128)(2,1)S(1)} %multiply_convert_fusion), channel_id=1, source_target_pairs={{0,16},{8,24},{16,0},{24,8},{1,17},{9,25},{17,1},{25,9},{2,18},{10... | collective-permute-start | bytes 1179656 | tf_op jit(solution)/shard_map/ppermute | solution.py:41
  81.7 18.0 %collective-permute-start.10 = (bf16[256,768]{1,0:T(8,128)(2,1)S(1)}, bf16[256,768]{1,0:T(8,128)(2,1)S(1)}, u32[]{:S(2)}, u32[]{:S(2)}) collective-permute-start(bf16[256,768]{1,0:T(8,128)(2,1)S(1)} %multiply_convert_fusion), channel_id=1, source_target_pairs={{0,8},{8,0},{16,24},{24,16},{1,9},{9,1},{17,25},{25,17},{2,10},{10... | collective-permute-start | bytes 1179656 | tf_op jit(solution)/shard_map/ppermute | solution.py:41
  102.6 13.0 %collective-permute-start.9 = (bf16[256,768]{1,0:T(8,128)(2,1)S(1)}, bf16[256,768]{1,0:T(8,128)(2,1)S(1)}, u32[]{:S(2)}, u32[]{:S(2)}) collective-permute-start(bf16[256,768]{1,0:T(8,128)(2,1)S(1)} %multiply_convert_fusion.1), channel_id=1, source_target_pairs={{0,24},{8,16},{16,8},{24,0},{1,25},{9,17},{17,9},{25,1},{2,26},{10... | collective-permute-start | bytes 1179656 | tf_op jit(solution)/shard_map/ppermute | solution.py:41
  104.4 18.6 %collective-permute-start.8 = (bf16[256,768]{1,0:T(8,128)(2,1)S(1)}, bf16[256,768]{1,0:T(8,128)(2,1)S(1)}, u32[]{:S(2)}, u32[]{:S(2)}) collective-permute-start(bf16[256,768]{1,0:T(8,128)(2,1)S(1)} %multiply_convert_fusion.1), channel_id=1, source_target_pairs={{0,16},{8,24},{16,0},{24,8},{1,17},{9,25},{17,1},{25,9},{2,18},{10... | collective-permute-start | bytes 1179656 | tf_op jit(solution)/shard_map/ppermute | solution.py:41
  105.6 17.7 %collective-permute-start.7 = (bf16[256,768]{1,0:T(8,128)(2,1)S(1)}, bf16[256,768]{1,0:T(8,128)(2,1)S(1)}, u32[]{:S(2)}, u32[]{:S(2)}) collective-permute-start(bf16[256,768]{1,0:T(8,128)(2,1)S(1)} %multiply_convert_fusion.1), channel_id=1, source_target_pairs={{0,8},{8,0},{16,24},{24,16},{1,9},{9,1},{17,25},{25,17},{2,10},{10... | collective-permute-start | bytes 1179656 | tf_op jit(solution)/shard_map/ppermute | solution.py:41
  125.3 1.0 copy-start.2
Sparse Core Ops, SparseCore 0:
  9.6 53.1 all-gather.2
  102.7 34.3 reduce-scatter.1

commit v10 on v4

--- a/solution.py
+++ b/solution.py
@@ -77,7 +77,7 @@
 
     image_group = jnp.concatenate(image_from, axis=0)
     label_group = jnp.concatenate(label_from, axis=0)
-    hidden_group = jnp.concatenate(hidden_from, axis=0)
+    hidden_rest = jnp.concatenate(hidden_from[1:], axis=0)
     own_columns = my_index * row_count + local
     scores_t = lax.dot_general(
         image_group, text_unit, (((1,), (1,)), ((), ())), preferred_element_type=jnp.float32
@@ -99,10 +99,11 @@
     grad_from = [projection_output_gradient] + [
         exchange(projection_output_gradient, k) for k in range(1, blocks)
     ]
+    contract_rows = (((0,), (0,)), ((), ()))
     partial = lax.dot_general(
-        hidden_group,
-        jnp.concatenate(grad_from, axis=0),
-        (((0,), (0,)), ((), ())),
+        hidden_from[0], grad_from[0], contract_rows, preferred_element_type=jnp.float32
+    ) + lax.dot_general(
+        hidden_rest, jnp.concatenate(grad_from[1:], axis=0), contract_rows,
         preferred_element_type=jnp.float32,
     )
     projection_grad = lax.psum_scatter(partial, "group", scatter_dimension=0, tiled=True)

time: 139 us -> 141 us (1.014)
  matrix products: 14.6 us -> 17.7 us
    dot_general x1 -> x2, matrix products: 2.87 us -> 5.2 us  [the longest x1 3.59 us: body(): lax.dot_general(hidden_rest, jnp.concatenate(grad_from[1:], axis=0), cont...]
  transfers between devices with their start and end apart: 14 -> 14, of which waited for: 8 -> 9; matrix products, arithmetic and copies ran while one was open for 11% -> 11% of each run, Pallas kernels for 0% -> 0%
where the time goes in v10:
time: 141 us
  waiting for transfers between devices  79 us (56%)
  matrix products  17.7 us (13%)
  starting transfers between devices  16.4 us (12%)
  between operations  15.5 us (11%)
  other arithmetic  7 us (5%)
  local copies, waits for them, and re-layouts  5.42 us (4%)
    ppermute x12, waiting for transfers between devices, exchange(): return lax.ppermute(value, 'blk', partner_pairs(blocks, step))  62.7 us
    ppermute x12, starting transfers between devices, exchange(): return lax.ppermute(value, 'blk', partner_pairs(blocks, step))  16.3 us
    reduce_scatter x1, waiting for transfers between devices, body(): lax.psum_scatter(partial, 'group', scatter_dimension=0, tiled=True)  9.83 us
    all_gather x1, waiting for transfers between devices, body(): w_full = lax.all_gather(linear_map_matrix, 'group', axis=0, tiled=True)  5.71 us
    dot_general x1, matrix products, body(): lax.dot_general(weights_of(logits_t, pair_sign_t), image_group, (((0,), (...  5.04 us
    slice x3, local copies, waits for them, and re-layouts, body(): hidden_from.append(incoming[:, :chunk])  4.07 us
    dot_general x1, matrix products, body(): projected = jnp.dot(hidden_rows, w_full, preferred_element_type=jnp.float32)  3.79 us
    dot_general x1, matrix products, body(): lax.dot_general(hidden_rest, jnp.concatenate(grad_from[1:], axis=0), cont...  3.59 us
  transfers between devices with their start and end apart: 14, of which 9 were waited for; matrix products, arithmetic and copies ran while one was open for 11% of the time, Pallas kernels for 0%

profile of v10, /device:TPU:0, one launch (start us, length us, event | category | flops | bytes accessed | tf_op | source)
XLA Modules:
  0.0 141.0 jit_solution(16845841177889521014)
XLA Ops:
  7.2 0.0 copy-start
  7.2 0.0 all-gather.2.cloned.1.call-start
  7.2 0.7 all-gather.2.cloned.1.call-update
  7.9 0.0 reduce-scatter.2.cloned.1.call-start
  8.0 1.2 fusion.37
  9.1 1.3 dynamic-slice_bitcast_fusion.2
  10.5 0.0 copy-done
  10.5 0.1 fusion.32
  10.6 0.0 copy-start.5
  10.6 1.4 pad_maximum_fusion.5
  12.0 2.9 %collective-permute-start.6 = (bf16[256,1536]{1,0:T(8,128)(2,1)S(1)}, bf16[256,1536]{1,0:T(8,128)(2,1)S(1)}, u32[]{:S(2)}, u32[]{:S(2)}) collective-permute-start(bf16[256,1536]{1,0:T(8,128)(2,1)S(1)} %get-tuple-element.16), channel_id=1, source_target_pairs={{0,8},{8,0},{16,24},{24,16},{1,9},{9,1},{17,25},{25,17},{2,10},{10... | collective-permute-start | bytes 2359304 | tf_op jit(solution)/shard_map/ppermute | solution.py:41
  15.0 1.5 %collective-permute-start.7 = (bf16[256,1536]{1,0:T(8,128)(2,1)}, bf16[256,1536]{1,0:T(8,128)(2,1)}, u32[]{:S(2)}, u32[]{:S(2)}) collective-permute-start(bf16[256,1536]{1,0:T(8,128)(2,1)} %get-tuple-element.17), channel_id=1, source_target_pairs={{0,16},{8,24},{16,0},{24,8},{1,17},{9,25},{17,1},{25,9},{2,18},{10... | collective-permute-start | bytes 2359304 | tf_op jit(solution)/shard_map/ppermute | solution.py:41
  16.5 0.0 collective-permute-start.8
  16.5 0.0 copy-done.5
  16.5 2.9 %collective-permute-start.5 = (s32[256]{0:T(256)S(1)}, s32[256]{0:T(256)S(1)}, u32[]{:S(2)}, u32[]{:S(2)}) collective-permute-start(s32[256]{0:T(256)S(1)} %bitcast.55), channel_id=1, source_target_pairs={{0,24},{8,16},{16,8},{24,0},{1,25},{9,17},{17,9},{25,1},{2,26},{10... | collective-permute-start | bytes 3080 | tf_op jit(solution)/shard_map/ppermute | solution.py:41
  19.4 0.5 collective-permute-start.4
  19.9 30.8 %collective-permute-done.5 = s32[256]{0:T(256)S(1)} collective-permute-done((s32[256]{0:T(256)S(1)}, s32[256]{0:T(256)S(1)}, u32[]{:S(2)}, u32[]{:S(2)}) %collective-permute-start.5) | collective-permute-done | bytes 1056 | tf_op jit(solution)/shard_map/ppermute | solution.py:41
  50.7 1.4 collective-permute-start.3
  52.1 0.6 iota_add_fusion.3
  54.0 0.0 collective-permute-done.4
  54.0 0.3 collective-permute-done.3
  54.3 0.0 collective-permute-done.6
  54.3 0.9 fusion.128
  55.2 0.0 copy-start.1
  55.2 0.0 collective-permute-done.7
  55.2 2.2 %fusion.129 = (bf16[256,768]{1,0:T(8,128)(2,1)}, bf16[256,768]{1,0:T(8,128)(2,1)}) fusion(bf16[256,1536]{1,0:T(8,128)(2,1)} %collective-permute-done.7), kind=kLoop, calls=%fused_computation.165 | loop fusion | bytes 1572864 | tf_op jit(solution)/shard_map/slice | solution.py:61
  57.4 0.0 collective-permute-done.8
  57.4 1.0 fusion.130
  58.4 5.7 %all-gather.2.cloned.1.call-done = bf16[3072,768]{1,0:T(8,128)(2,1)} async-done(((bf16[384,768]{1,0:T(8,128)(2,1)}), bf16[3072,768]{1,0:T(8,128)(2,1)}) %all-gather.2.cloned.1.call-update) | async-done | bytes 4718608 | tf_op jit(solution)/shard_map/all_gather | solution.py:43
  64.1 0.0 copy-done.1
  64.1 3.8 %multiply_reduce_fusion.1 = (f32[256]{0:T(256)S(1)}, f32[256,768]{1,0:T(8,128)S(1)}) fusion(bf16[3072,768]{1,0:T(8,128)(2,1)} %all-gather.2.cloned.1.call-done, bf16[1,256,3072]{2,1,0:T(8,128)(2,1)S(1)} %copy-done.1), kind=kOutput, calls=%fused_computation.54 | convolution fusion | flops 1208352512 | bytes 7078912 | tf_op jit(solution)/shard_map/dot_general | solution.py:65
  67.9 0.1 multiply_convert_fusion.1
  68.0 5.0 %multiply_reduce_fusion = (f32[256]{0:T(256)}, f32[256,768]{1,0:T(8,128)}) fusion(f32[256,768]{1,0:T(8,128)S(1)} %get-tuple-element.20, f32[256]{0:T(256)S(1)} %add_rsqrt_fusion, bf16[256,768]{1,0:T(8,128)(2,1)} %get-tuple-element.15, bf16[256,768]{1,0:T(8,128)(2,1)} %get-tuple-element.13, bf16[256,768]{1,0:T(8,128)(2,1)} %get-tuple-element.11, ...), kind=kOutput, calls=%fused_computation.53 | convolution fusion | flops 821624576 | bytes 3546120 | tf_op jit(solution)/shard_map/dot_general | solution.py:89
  73.1 2.1 %multiply_convert_fusion = bf16[256,768]{1,0:T(8,128)(2,1)} fusion(f32[256,768]{1,0:T(8,128)} %get-tuple-element.25, f32[256,768]{1,0:T(8,128)S(1)} %get-tuple-element.20, f32[256]{0:T(256)} %get-tuple-element.24, f32[256]{0:T(256)S(1)} %add_rsqrt_fusion), kind=kLoop, calls=%fused_computation.52 | loop fusion | flops 983040 | bytes 1968128 | tf_op jit(solution)/shard_map/convert_element_type | solution.py:98
  75.1 2.4 %collective-permute-start.11 = (bf16[256,768]{1,0:T(8,128)(2,1)}, bf16[256,768]{1,0:T(8,128)(2,1)S(1)}, u32[]{:S(2)}, u32[]{:S(2)}) collective-permute-start(bf16[256,768]{1,0:T(8,128)(2,1)} %multiply_convert_fusion), channel_id=1, source_target_pairs={{0,24},{8,16},{16,8},{24,0},{1,25},{9,17},{17,9},{25,1},{2,26},{10... | collective-permute-start | bytes 1179656 | tf_op jit(solution)/shard_map/ppermute | solution.py:41
  77.5 0.5 collective-permute-start.10
  78.1 0.6 collective-permute-start.9
  78.6 1.6 %fusion.45 = f32[768,768]{1,0:T(8,128)S(1)} fusion(bf16[256,768]{1,0:T(8,128)(2,1)} %multiply_convert_fusion, bf16[1,256,3072]{2,1,0:T(8,128)(2,1)S(1)} %copy-done.1, s32[]{:T(128)S(6)} %select_n.51), kind=kOutput, calls=%fused_computation.67 | convolution fusion | flops 301989888 | bytes 3145732 | tf_op jit(solution)/shard_map/dot_general | solution.py:103
  80.3 8.0 %collective-permute-done.11 = bf16[256,768]{1,0:T(8,128)(2,1)S(1)} collective-permute-done((bf16[256,768]{1,0:T(8,128)(2,1)}, bf16[256,768]{1,0:T(8,128)(2,1)S(1)}, u32[]{:S(2)}, u32[]{:S(2)}) %collective-permute-start.11) | collective-permute-done | bytes 393248 | tf_op jit(solution)/shard_map/ppermute | solution.py:41
  88.3 7.7 %collective-permute-done.10 = bf16[256,768]{1,0:T(8,128)(2,1)S(1)} collective-permute-done((bf16[256,768]{1,0:T(8,128)(2,1)}, bf16[256,768]{1,0:T(8,128)(2,1)S(1)}, u32[]{:S(2)}, u32[]{:S(2)}) %collective-permute-start.10) | collective-permute-done | bytes 393248 | tf_op jit(solution)/shard_map/ppermute | solution.py:41
  95.9 0.2 collective-permute-done.9
  96.1 0.0 copy-done.2
  96.1 0.0 copy-done.3
  96.1 0.0 copy-done.4
  96.1 3.6 %convolution_add_fusion = f32[768,768]{1,0:T(8,128)} fusion(f32[768,768]{1,0:T(8,128)S(1)} %fusion.45, bf16[256,768]{1,0:T(8,128)(2,1)S(1)} %copy-done.4, bf16[256,768]{1,0:T(8,128)(2,1)S(1)} %copy-done.3, bf16[256,768]{1,0:T(8,128)(2,1)S(1)} %copy-done.2, bf16[256,768]{1,0:T(8,128)(2,1)S(1)} %collective-permute-done.11, ...), kind=kOutput, calls=%fused_computation | convolution fusion | flops 913637376 | bytes 7077888 | tf_op jit(solution)/shard_map/dot_general | solution.py:105
  99.7 0.0 reduce-scatter.2.cloned.1.call-update
  99.8 1.7 %collective-permute-start.2 = (bf16[256,768]{1,0:T(8,128)(2,1)S(1)}, bf16[256,768]{1,0:T(8,128)(2,1)S(1)}, u32[]{:S(2)}, u32[]{:S(2)}) collective-permute-start(bf16[256,768]{1,0:T(8,128)(2,1)S(1)} %multiply_convert_fusion.1), channel_id=1, source_target_pairs={{0,24},{8,16},{16,8},{24,0},{1,25},{9,17},{17,9},{25,1},{2,26},{10... | collective-permute-start | bytes 1179656 | tf_op jit(solution)/shard_map/ppermute | solution.py:41
  101.4 1.3 collective-permute-start.1
  102.8 0.6 collective-permute-start
  103.3 0.3 fusion.22
  103.6 0.0 copy-done.6
  103.6 0.4 fusion.88
  104.1 8.7 %collective-permute-done.2 = bf16[256,768]{1,0:T(8,128)(2,1)S(1)} collective-permute-done((bf16[256,768]{1,0:T(8,128)(2,1)S(1)}, bf16[256,768]{1,0:T(8,128)(2,1)S(1)}, u32[]{:S(2)}, u32[]{:S(2)}) %collective-permute-start.2) | collective-permute-done | bytes 393248 | tf_op jit(solution)/shard_map/ppermute | solution.py:41
  112.8 0.3 fusion.25
  113.1 7.1 %collective-permute-done.1 = bf16[256,768]{1,0:T(8,128)(2,1)S(1)} collective-permute-done((bf16[256,768]{1,0:T(8,128)(2,1)S(1)}, bf16[256,768]{1,0:T(8,128)(2,1)S(1)}, u32[]{:S(2)}, u32[]{:S(2)}) %collective-permute-start.1) | collective-permute-done | bytes 393248 | tf_op jit(solution)/shard_map/ppermute | solution.py:41
  120.2 0.3 fusion.24
  120.5 0.0 collective-permute-done
  120.5 0.9 fusion.81
  121.4 0.6 add_add_fusion
  121.9 0.4 fusion.92
  122.4 0.4 convolution_add_fusion.2
  122.8 0.5 fusion.33
  123.4 1.0 fusion.44
  124.3 9.8 %reduce-scatter.2.cloned.1.call-done = f32[96,768]{1,0:T(8,128)} async-done(((f32[768,768]{1,0:T(8,128)}), f32[96,768]{1,0:T(8,128)}) %reduce-scatter.2.cloned.1.call-update) | async-done | bytes 294928 | tf_op jit(solution)/shard_map/reduce_scatter | solution.py:109
  (9 shorter events, 0.0 us)
Async XLA Ops:
  7.2 3.3 %copy-start = (bf16[1,256,768]{2,1,0:T(8,128)(2,1)S(1)}, bf16[1,256,768]{2,1,0:T(8,128)(2,1)}, u32[]{:S(2)}) copy-start(bf16[1,256,768]{2,1,0:T(8,128)(2,1)} %param.6) | copy-start | bytes 1179652
  7.2 56.9 %all-gather.2.cloned.1.call-start = ((), (), s32[]{:S(2)}) async-start(), calls=%async_computation.1 | async-start | bytes 5308416 | tf_op jit(solution)/shard_map/all_gather | solution.py:43
  7.9 126.3 %reduce-scatter.2.cloned.1.call-start = ((), (), s32[]{:S(2)}) async-start(), calls=%async_computation.2 | async-start | bytes 2654208 | tf_op jit(solution)/shard_map/reduce_scatter | solution.py:109
  10.6 5.9 %copy-start.5 = (s32[1,256]{1,0:T(1,128)S(1)}, s32[1,256]{1,0:T(1,128)}, u32[]{:S(2)}) copy-start(s32[1,256]{1,0:T(1,128)} %param.9) | copy-start | bytes 3076
  12.0 42.3 %collective-permute-start.6 = (bf16[256,1536]{1,0:T(8,128)(2,1)S(1)}, bf16[256,1536]{1,0:T(8,128)(2,1)S(1)}, u32[]{:S(2)}, u32[]{:S(2)}) collective-permute-start(bf16[256,1536]{1,0:T(8,128)(2,1)S(1)} %get-tuple-element.16), channel_id=1, source_target_pairs={{0,8},{8,0},{16,24},{24,16},{1,9},{9,1},{17,25},{25,17},{2,10},{10... | collective-permute-start | bytes 2359304 | tf_op jit(solution)/shard_map/ppermute | solution.py:41
  15.0 40.3 %collective-permute-start.7 = (bf16[256,1536]{1,0:T(8,128)(2,1)}, bf16[256,1536]{1,0:T(8,128)(2,1)}, u32[]{:S(2)}, u32[]{:S(2)}) collective-permute-start(bf16[256,1536]{1,0:T(8,128)(2,1)} %get-tuple-element.17), channel_id=1, source_target_pairs={{0,16},{8,24},{16,0},{24,8},{1,17},{9,25},{17,1},{25,9},{2,18},{10... | collective-permute-start | bytes 2359304 | tf_op jit(solution)/shard_map/ppermute | solution.py:41
  16.5 40.9 %collective-permute-start.8 = (bf16[256,1536]{1,0:T(8,128)(2,1)}, bf16[256,1536]{1,0:T(8,128)(2,1)S(1)}, u32[]{:S(2)}, u32[]{:S(2)}) collective-permute-start(bf16[256,1536]{1,0:T(8,128)(2,1)} %get-tuple-element.18), channel_id=1, source_target_pairs={{0,24},{8,16},{16,8},{24,0},{1,25},{9,17},{17,9},{25,1},{2,26},{10... | collective-permute-start | bytes 2359304 | tf_op jit(solution)/shard_map/ppermute | solution.py:41
  16.5 34.2 %collective-permute-start.5 = (s32[256]{0:T(256)S(1)}, s32[256]{0:T(256)S(1)}, u32[]{:S(2)}, u32[]{:S(2)}) collective-permute-start(s32[256]{0:T(256)S(1)} %bitcast.55), channel_id=1, source_target_pairs={{0,24},{8,16},{16,8},{24,0},{1,25},{9,17},{17,9},{25,1},{2,26},{10... | collective-permute-start | bytes 3080 | tf_op jit(solution)/shard_map/ppermute | solution.py:41
  19.4 34.6 %collective-permute-start.4 = (s32[256]{0:T(256)S(1)}, s32[256]{0:T(256)S(1)}, u32[]{:S(2)}, u32[]{:S(2)}) collective-permute-start(s32[256]{0:T(256)S(1)} %bitcast.56), channel_id=1, source_target_pairs={{0,16},{8,24},{16,0},{24,8},{1,17},{9,25},{17,1},{25,9},{2,18},{10... | collective-permute-start | bytes 3080 | tf_op jit(solution)/shard_map/ppermute | solution.py:41
  50.7 3.6 %collective-permute-start.3 = (s32[256]{0:T(256)S(1)}, s32[256]{0:T(256)S(1)}, u32[]{:S(2)}, u32[]{:S(2)}) collective-permute-start(s32[256]{0:T(256)S(1)} %bitcast.57), channel_id=1, source_target_pairs={{0,8},{8,0},{16,24},{24,16},{1,9},{9,1},{17,25},{25,17},{2,10},{10... | collective-permute-start | bytes 3080 | tf_op jit(solution)/shard_map/ppermute | solution.py:41
  55.2 8.9 %copy-start.1 = (bf16[1,256,3072]{2,1,0:T(8,128)(2,1)S(1)}, bf16[1,256,3072]{2,1,0:T(8,128)(2,1)}, u32[]{:S(2)}) copy-start(bf16[1,256,3072]{2,1,0:T(8,128)(2,1)} %param.7) | copy-start | bytes 4718596
  75.1 13.1 %collective-permute-start.11 = (bf16[256,768]{1,0:T(8,128)(2,1)}, bf16[256,768]{1,0:T(8,128)(2,1)S(1)}, u32[]{:S(2)}, u32[]{:S(2)}) collective-permute-start(bf16[256,768]{1,0:T(8,128)(2,1)} %multiply_convert_fusion), channel_id=1, source_target_pairs={{0,24},{8,16},{16,8},{24,0},{1,25},{9,17},{17,9},{25,1},{2,26},{10... | collective-permute-start | bytes 1179656 | tf_op jit(solution)/shard_map/ppermute | solution.py:41
  77.5 18.4 %collective-permute-start.10 = (bf16[256,768]{1,0:T(8,128)(2,1)}, bf16[256,768]{1,0:T(8,128)(2,1)S(1)}, u32[]{:S(2)}, u32[]{:S(2)}) collective-permute-start(bf16[256,768]{1,0:T(8,128)(2,1)} %multiply_convert_fusion), channel_id=1, source_target_pairs={{0,16},{8,24},{16,0},{24,8},{1,17},{9,25},{17,1},{25,9},{2,18},{10... | collective-permute-start | bytes 1179656 | tf_op jit(solution)/shard_map/ppermute | solution.py:41
  78.1 18.0 %collective-permute-start.9 = (bf16[256,768]{1,0:T(8,128)(2,1)}, bf16[256,768]{1,0:T(8,128)(2,1)}, u32[]{:S(2)}, u32[]{:S(2)}) collective-permute-start(bf16[256,768]{1,0:T(8,128)(2,1)} %multiply_convert_fusion), channel_id=1, source_target_pairs={{0,8},{8,0},{16,24},{24,16},{1,9},{9,1},{17,25},{25,17},{2,10},{10... | collective-permute-start | bytes 1179656 | tf_op jit(solution)/shard_map/ppermute | solution.py:41
  78.6 17.5 %copy-start.2 = (bf16[256,768]{1,0:T(8,128)(2,1)S(1)}, bf16[256,768]{1,0:T(8,128)(2,1)}, u32[]{:S(2)}) copy-start(bf16[256,768]{1,0:T(8,128)(2,1)} %get-tuple-element.10) | copy-start | bytes 1179652
  78.6 17.5 %copy-start.3 = (bf16[256,768]{1,0:T(8,128)(2,1)S(1)}, bf16[256,768]{1,0:T(8,128)(2,1)}, u32[]{:S(2)}) copy-start(bf16[256,768]{1,0:T(8,128)(2,1)} %get-tuple-element.12) | copy-start | bytes 1179652
  78.6 17.5 %copy-start.4 = (bf16[256,768]{1,0:T(8,128)(2,1)S(1)}, bf16[256,768]{1,0:T(8,128)(2,1)}, u32[]{:S(2)}) copy-start(bf16[256,768]{1,0:T(8,128)(2,1)} %get-tuple-element.14) | copy-start | bytes 1179652
  99.7 3.9 %copy-start.6 = (s32[256]{0:T(256)S(1)}, s32[256]{0:T(256)}, u32[]{:S(2)}) copy-start(s32[256]{0:T(256)} %iota_add_fusion.3) | copy-start | bytes 3076
  99.8 13.0 %collective-permute-start.2 = (bf16[256,768]{1,0:T(8,128)(2,1)S(1)}, bf16[256,768]{1,0:T(8,128)(2,1)S(1)}, u32[]{:S(2)}, u32[]{:S(2)}) collective-permute-start(bf16[256,768]{1,0:T(8,128)(2,1)S(1)} %multiply_convert_fusion.1), channel_id=1, source_target_pairs={{0,24},{8,16},{16,8},{24,0},{1,25},{9,17},{17,9},{25,1},{2,26},{10... | collective-permute-start | bytes 1179656 | tf_op jit(solution)/shard_map/ppermute | solution.py:41
  101.4 18.7 %collective-permute-start.1 = (bf16[256,768]{1,0:T(8,128)(2,1)S(1)}, bf16[256,768]{1,0:T(8,128)(2,1)S(1)}, u32[]{:S(2)}, u32[]{:S(2)}) collective-permute-start(bf16[256,768]{1,0:T(8,128)(2,1)S(1)} %multiply_convert_fusion.1), channel_id=1, source_target_pairs={{0,16},{8,24},{16,0},{24,8},{1,17},{9,25},{17,1},{25,9},{2,18},{10... | collective-permute-start | bytes 1179656 | tf_op jit(solution)/shard_map/ppermute | solution.py:41
  102.8 17.7 %collective-permute-start = (bf16[256,768]{1,0:T(8,128)(2,1)S(1)}, bf16[256,768]{1,0:T(8,128)(2,1)S(1)}, u32[]{:S(2)}, u32[]{:S(2)}) collective-permute-start(bf16[256,768]{1,0:T(8,128)(2,1)S(1)} %multiply_convert_fusion.1), channel_id=1, source_target_pairs={{0,8},{8,0},{16,24},{24,16},{1,9},{9,1},{17,25},{25,17},{2,10},{10... | collective-permute-start | bytes 1179656 | tf_op jit(solution)/shard_map/ppermute | solution.py:41
Sparse Core Ops, SparseCore 0:
  9.6 54.3 all-gather.1
  99.9 34.2 reduce-scatter.1

commit v11 on v4

--- a/solution.py
+++ b/solution.py
@@ -77,7 +77,12 @@
 
     image_group = jnp.concatenate(image_from, axis=0)
     label_group = jnp.concatenate(label_from, axis=0)
-    hidden_group = jnp.concatenate(hidden_from, axis=0)
+    hidden_natural = jnp.zeros((blocks,) + own_hidden_chunk.shape, own_hidden_chunk.dtype)
+    for k in range(blocks):
+        hidden_natural = lax.dynamic_update_slice_in_dim(
+            hidden_natural, hidden_from[k][None], source[k], 0
+        )
+    hidden_group = hidden_natural.reshape(blocks * row_count, chunk)
     own_columns = my_index * row_count + local
     scores_t = lax.dot_general(
         image_group, text_unit, (((1,), (1,)), ((), ())), preferred_element_type=jnp.float32
@@ -96,12 +101,9 @@
         text_scale
         * (text_unit_grad - text_dir * jnp.sum(text_dir * text_unit_grad, axis=1, keepdims=True))
     ).astype(jnp.bfloat16)
-    grad_from = [projection_output_gradient] + [
-        exchange(projection_output_gradient, k) for k in range(1, blocks)
-    ]
     partial = lax.dot_general(
         hidden_group,
-        jnp.concatenate(grad_from, axis=0),
+        lax.all_gather(projection_output_gradient, "blk", axis=0, tiled=True),
         (((0,), (0,)), ((), ())),
         preferred_element_type=jnp.float32,
     )

time: 139 us -> 153 us (1.10)
  waiting for transfers between devices: 79.3 us -> 92.3 us
  starting transfers between devices: 16.8 us -> 13.2 us
  matrix products: 14.6 us -> 16.5 us
    all_gather x0 -> x1, waiting for transfers between devices: none -> 27.7 us  [body(): lax.all_gather(projection_output_gradient, 'blk', axis=0, tiled=True)]
    ppermute x12 -> x9, waiting for transfers between devices: 63.4 us -> 46.3 us  [exchange(): return lax.ppermute(value, 'blk', partner_pairs(blocks, step))]
    ppermute x12 -> x9, starting transfers between devices: 16.7 us -> 13.1 us  [exchange(): return lax.ppermute(value, 'blk', partner_pairs(blocks, step))]
    dynamic_update_slice x0 -> x3, local copies, waits for them, and re-layouts: none -> 2.15 us  [body(): lax.dynamic_update_slice_in_dim(hidden_natural, hidden_from[k][None], sou...]
    dynamic_slice x1, local copies, waits for them, and re-layouts: 2.26 us -> 0.16 us  [body(): lax.dynamic_slice_in_dim(hidden_rows, target * chunk, chunk, 1)]
    reduce_scatter x1, waiting for transfers between devices: 9.96 us -> 11.9 us  [body(): lax.psum_scatter(partial, 'group', scatter_dimension=0, tiled=True)]
    slice x3 -> x4, local copies, waits for them, and re-layouts: 3.97 us -> 3.85 us  [body(): image_from.append(incoming[:, chunk:])]
  transfers between devices with their start and end apart: 14 -> 12, of which waited for: 8 -> 6; matrix products, arithmetic and copies ran while one was open for 11% -> 10% of each run, Pallas kernels for 0% -> 0%
where the time goes in v11:
time: 153 us; the launch traced here: 152 us
  waiting for transfers between devices  92.3 us (60%)
  matrix products  16.5 us (11%)
  between operations  15.3 us (10%)
  starting transfers between devices  13.2 us (9%)
  local copies, waits for them, and re-layouts  7.46 us (5%)
  other arithmetic  7.33 us (5%)
    ppermute x9, waiting for transfers between devices, exchange(): return lax.ppermute(value, 'blk', partner_pairs(blocks, step))  46.3 us
    all_gather x1, waiting for transfers between devices, body(): lax.all_gather(projection_output_gradient, 'blk', axis=0, tiled=True)  27.7 us
    ppermute x9, starting transfers between devices, exchange(): return lax.ppermute(value, 'blk', partner_pairs(blocks, step))  13.1 us
    reduce_scatter x1, waiting for transfers between devices, body(): lax.psum_scatter(partial, 'group', scatter_dimension=0, tiled=True)  11.9 us
    all_gather x1, waiting for transfers between devices, body(): w_full = lax.all_gather(linear_map_matrix, 'group', axis=0, tiled=True)  5.69 us
    dot_general x1, matrix products, body(): lax.dot_general(weights_of(logits_t, pair_sign_t), image_group, (((0,), (...  4.73 us
    dot_general x1, matrix products, body(): lax.dot_general(hidden_group, lax.all_gather(projection_output_gradient,...  4.26 us
    slice x4, local copies, waits for them, and re-layouts, body(): image_from.append(incoming[:, chunk:])  3.85 us
  transfers between devices with their start and end apart: 12, of which 6 were waited for; matrix products, arithmetic and copies ran while one was open for 10% of the time, Pallas kernels for 0%

profile of v11, /device:TPU:0, one launch (start us, length us, event | category | flops | bytes accessed | tf_op | source)
XLA Modules:
  0.0 152.2 jit_solution(5768427372059956108)
XLA Ops:
  7.2 0.0 copy-start.1
  7.2 0.0 all-gather.3.cloned.1.call-start
  7.2 0.7 all-gather.3.cloned.1.call-update
  7.9 0.0 all-gather.5.cloned.1.call-start
  8.0 1.2 fusion.27
  9.1 0.1 broadcast_in_dim.52
  9.2 0.0 copy-done.1
  9.3 0.0 copy-start
  9.3 0.2 dynamic-slice_bitcast_fusion
  9.4 0.0 copy-start.2
  9.4 1.2 copy-done.2
  10.6 0.0 copy-done
  10.6 0.1 fusion.22
  10.8 0.0 copy-start.6
  10.8 1.6 %pad_maximum_fusion.3 = (bf16[256,1536]{1,0:T(8,128)(2,1)}, bf16[256,1536]{1,0:T(8,128)(2,1)}, bf16[256,1536]{1,0:T(8,128)(2,1)}) fusion(bf16[256,768]{1,0:T(8,128)(2,1)S(1)} %fusion.22, bf16[256,768]{1,0:T(8,128)(2,1)S(1)} %get-tuple-element.7, bf16[256,768]{1,0:T(8,128)(2,1)S(1)} %get-tuple-element.10, bf16[256,768]{1,0:T(8,128)(2,1)S(1)} %get-tuple-element.8), kind=kLoop, calls=%fused_computation.28 | loop fusion | flops 3932160 | bytes 3932160 | tf_op jit(solution)/shard_map/concatenate | solution.py:57
  12.4 3.9 %collective-permute-start.5 = (bf16[256,1536]{1,0:T(8,128)(2,1)}, bf16[256,1536]{1,0:T(8,128)(2,1)S(1)}, u32[]{:S(2)}, u32[]{:S(2)}) collective-permute-start(bf16[256,1536]{1,0:T(8,128)(2,1)} %get-tuple-element.11), channel_id=1, source_target_pairs={{0,24},{8,16},{16,8},{24,0},{1,25},{9,17},{17,9},{25,1},{2,26},{10... | collective-permute-start | bytes 2359304 | tf_op jit(solution)/shard_map/ppermute | solution.py:41
  16.3 0.5 collective-permute-start.4
  16.8 0.1 collective-permute-start.3
  16.8 0.0 copy-done.6
  16.8 2.9 %collective-permute-start.8 = (s32[256]{0:T(256)S(1)}, s32[256]{0:T(256)S(1)}, u32[]{:S(2)}, u32[]{:S(2)}) collective-permute-start(s32[256]{0:T(256)S(1)} %bitcast.67), channel_id=1, source_target_pairs={{0,24},{8,16},{16,8},{24,0},{1,25},{9,17},{17,9},{25,1},{2,26},{10... | collective-permute-start | bytes 3080 | tf_op jit(solution)/shard_map/ppermute | solution.py:41
  19.8 0.5 collective-permute-start.7
  20.3 30.7 %collective-permute-done.8 = s32[256]{0:T(256)S(1)} collective-permute-done((s32[256]{0:T(256)S(1)}, s32[256]{0:T(256)S(1)}, u32[]{:S(2)}, u32[]{:S(2)}) %collective-permute-start.8) | collective-permute-done | bytes 1056 | tf_op jit(solution)/shard_map/ppermute | solution.py:41
  50.9 1.7 %collective-permute-start.6 = (s32[256]{0:T(256)S(1)}, s32[256]{0:T(256)S(1)}, u32[]{:S(2)}, u32[]{:S(2)}) collective-permute-start(s32[256]{0:T(256)S(1)} %bitcast.69), channel_id=1, source_target_pairs={{0,8},{8,0},{16,24},{24,16},{1,9},{9,1},{17,25},{25,17},{2,10},{10... | collective-permute-start | bytes 3080 | tf_op jit(solution)/shard_map/ppermute | solution.py:41
  52.6 0.6 iota_add_fusion.3
  54.5 0.0 collective-permute-done.7
  54.5 0.0 collective-permute-done.6
  54.5 0.0 collective-permute-done.5
  54.5 0.0 copy-start.4
  54.5 0.0 collective-permute-done.4
  54.5 2.0 %slice.28 = bf16[256,768]{1,0:T(8,128)(2,1)} slice(bf16[256,1536]{1,0:T(8,128)(2,1)} %collective-permute-done.4), slice={[0:256], [768:1536]} | slice | bytes 786432 | tf_op jit(solution)/shard_map/slice | solution.py:62
  56.6 0.0 collective-permute-done.3
  56.6 1.8 %slice.27 = bf16[256,768]{1,0:T(8,128)(2,1)} slice(bf16[256,1536]{1,0:T(8,128)(2,1)} %collective-permute-done.3), slice={[0:256], [768:1536]} | slice | bytes 786432 | tf_op jit(solution)/shard_map/slice | solution.py:62
  58.4 0.0 copy-done.4
  58.4 5.7 %all-gather.3.cloned.1.call-done = bf16[3072,768]{1,0:T(8,128)(2,1)} async-done(((bf16[384,768]{1,0:T(8,128)(2,1)}), bf16[3072,768]{1,0:T(8,128)(2,1)}) %all-gather.3.cloned.1.call-update) | async-done | bytes 4718608 | tf_op jit(solution)/shard_map/all_gather | solution.py:43
  64.1 3.8 %multiply_reduce_fusion.1 = (f32[256]{0:T(256)S(1)}, f32[256,768]{1,0:T(8,128)S(1)}) fusion(bf16[3072,768]{1,0:T(8,128)(2,1)} %all-gather.3.cloned.1.call-done, bf16[1,256,3072]{2,1,0:T(8,128)(2,1)S(1)} %copy-done.1), kind=kOutput, calls=%fused_computation.43 | convolution fusion | flops 1208352512 | bytes 7078912 | tf_op jit(solution)/shard_map/dot_general | solution.py:65
  68.0 0.1 multiply_convert_fusion.1
  68.1 4.7 %multiply_reduce_fusion = (f32[256]{0:T(256)}, f32[256,768]{1,0:T(8,128)}) fusion(f32[256,768]{1,0:T(8,128)S(1)} %get-tuple-element.15, f32[256]{0:T(256)S(1)} %add_rsqrt_fusion, bf16[256,768]{1,0:T(8,128)(2,1)S(1)} %slice-done, bf16[256,768]{1,0:T(8,128)(2,1)} %slice.28, bf16[256,768]{1,0:T(8,128)(2,1)} %slice.27, bf16[256,768]{1,0:T(8,128)(2,1)S(1)} %fusion.22, ...), kind=kOutput, calls=%fused_computation.42 | convolution fusion | flops 821624576 | bytes 3546120 | tf_op jit(solution)/shard_map/dot_general | solution.py:94
  72.8 2.2 %multiply_convert_fusion = bf16[256,768]{1,0:T(8,128)(2,1)} fusion(f32[256,768]{1,0:T(8,128)} %get-tuple-element.20, f32[256,768]{1,0:T(8,128)S(1)} %get-tuple-element.15, f32[256]{0:T(256)} %get-tuple-element.19, f32[256]{0:T(256)S(1)} %add_rsqrt_fusion), kind=kLoop, calls=%fused_computation.41 | loop fusion | flops 983040 | bytes 1968128 | tf_op jit(solution)/shard_map/convert_element_type | solution.py:103
  75.0 0.0 all-gather.5.cloned.1.call-update
  75.0 0.0 reduce-scatter.2.cloned.1.call-start
  75.1 0.0 copy-done.3
  75.1 1.1 fusion.37
  76.2 1.0 fusion.36
  77.3 27.7 %all-gather.5.cloned.1.call-done = bf16[1024,768]{1,0:T(8,128)(2,1)} async-done(((bf16[256,768]{1,0:T(8,128)(2,1)}), bf16[1024,768]{1,0:T(8,128)(2,1)}) %all-gather.5.cloned.1.call-update) | async-done | bytes 1572880 | tf_op jit(solution)/shard_map/all_gather | solution.py:106
  105.0 4.3 %fusion.116 = f32[768,768]{1,0:T(8,128)} fusion(bf16[1024,768]{1,0:T(8,128)(2,1)S(1)} %bitcast.66, bf16[1024,768]{1,0:T(8,128)(2,1)} %all-gather.5.cloned.1.call-done), kind=kOutput, calls=%fused_computation.155 | convolution fusion | flops 1207959552 | bytes 5505024 | tf_op jit(solution)/shard_map/dot_general | solution.py:104
  109.2 0.0 reduce-scatter.2.cloned.1.call-update
  109.3 1.5 collective-permute-start.1
  110.8 1.5 collective-permute-start.2
  112.3 0.6 collective-permute-start
  112.8 0.3 fusion.12
  113.2 0.0 copy-done.7
  113.2 0.4 fusion.78
  113.6 15.0 %collective-permute-done.1 = bf16[256,768]{1,0:T(8,128)(2,1)S(1)} collective-permute-done((bf16[256,768]{1,0:T(8,128)(2,1)S(1)}, bf16[256,768]{1,0:T(8,128)(2,1)S(1)}, u32[]{:S(2)}, u32[]{:S(2)}) %collective-permute-start.1) | collective-permute-done | bytes 393248 | tf_op jit(solution)/shard_map/ppermute | solution.py:41
  128.6 0.3 fusion.14
  128.9 0.0 collective-permute-done.2
  129.0 0.3 fusion.15
  129.3 0.6 collective-permute-done
  129.9 0.9 fusion.71
  130.8 0.6 add_add_fusion
  131.3 0.4 fusion.82
  131.8 0.4 convolution_add_fusion.1
  132.2 0.5 fusion.23
  132.8 1.0 fusion.34
  133.7 11.9 %reduce-scatter.2.cloned.1.call-done = f32[96,768]{1,0:T(8,128)} async-done(((f32[768,768]{1,0:T(8,128)}), f32[96,768]{1,0:T(8,128)}) %reduce-scatter.2.cloned.1.call-update) | async-done | bytes 294928 | tf_op jit(solution)/shard_map/reduce_scatter | solution.py:110
  (12 shorter events, 0.1 us)
Async XLA Ops:
  7.2 2.1 %copy-start.1 = (bf16[1,256,3072]{2,1,0:T(8,128)(2,1)S(1)}, bf16[1,256,3072]{2,1,0:T(8,128)(2,1)}, u32[]{:S(2)}) copy-start(bf16[1,256,3072]{2,1,0:T(8,128)(2,1)} %param.7) | copy-start | bytes 4718596
  7.2 56.9 %all-gather.3.cloned.1.call-start = ((), (), s32[]{:S(2)}) async-start(), calls=%async_computation.1 | async-start | bytes 5308416 | tf_op jit(solution)/shard_map/all_gather | solution.py:43
  7.9 97.1 %all-gather.5.cloned.1.call-start = ((), (), s32[]{:S(2)}) async-start(), calls=%async_computation.2 | async-start | bytes 1966080 | tf_op jit(solution)/shard_map/all_gather | solution.py:106
  9.3 1.4 copy-start
  9.4 1.2 copy-start.2
  10.8 6.1 %copy-start.6 = (s32[1,256]{1,0:T(1,128)S(1)}, s32[1,256]{1,0:T(1,128)}, u32[]{:S(2)}) copy-start(s32[1,256]{1,0:T(1,128)} %param.9) | copy-start | bytes 3076
  12.4 42.1 %collective-permute-start.5 = (bf16[256,1536]{1,0:T(8,128)(2,1)}, bf16[256,1536]{1,0:T(8,128)(2,1)S(1)}, u32[]{:S(2)}, u32[]{:S(2)}) collective-permute-start(bf16[256,1536]{1,0:T(8,128)(2,1)} %get-tuple-element.11), channel_id=1, source_target_pairs={{0,24},{8,16},{16,8},{24,0},{1,25},{9,17},{17,9},{25,1},{2,26},{10... | collective-permute-start | bytes 2359304 | tf_op jit(solution)/shard_map/ppermute | solution.py:41
  16.3 38.3 %collective-permute-start.4 = (bf16[256,1536]{1,0:T(8,128)(2,1)}, bf16[256,1536]{1,0:T(8,128)(2,1)}, u32[]{:S(2)}, u32[]{:S(2)}) collective-permute-start(bf16[256,1536]{1,0:T(8,128)(2,1)} %get-tuple-element.12), channel_id=1, source_target_pairs={{0,16},{8,24},{16,0},{24,8},{1,17},{9,25},{17,1},{25,9},{2,18},{10... | collective-permute-start | bytes 2359304 | tf_op jit(solution)/shard_map/ppermute | solution.py:41
  16.8 39.8 %collective-permute-start.3 = (bf16[256,1536]{1,0:T(8,128)(2,1)}, bf16[256,1536]{1,0:T(8,128)(2,1)}, u32[]{:S(2)}, u32[]{:S(2)}) collective-permute-start(bf16[256,1536]{1,0:T(8,128)(2,1)} %get-tuple-element.13), channel_id=1, source_target_pairs={{0,8},{8,0},{16,24},{24,16},{1,9},{9,1},{17,25},{25,17},{2,10},{10... | collective-permute-start | bytes 2359304 | tf_op jit(solution)/shard_map/ppermute | solution.py:41
  16.8 34.1 %collective-permute-start.8 = (s32[256]{0:T(256)S(1)}, s32[256]{0:T(256)S(1)}, u32[]{:S(2)}, u32[]{:S(2)}) collective-permute-start(s32[256]{0:T(256)S(1)} %bitcast.67), channel_id=1, source_target_pairs={{0,24},{8,16},{16,8},{24,0},{1,25},{9,17},{17,9},{25,1},{2,26},{10... | collective-permute-start | bytes 3080 | tf_op jit(solution)/shard_map/ppermute | solution.py:41
  19.8 34.7 %collective-permute-start.7 = (s32[256]{0:T(256)S(1)}, s32[256]{0:T(256)S(1)}, u32[]{:S(2)}, u32[]{:S(2)}) collective-permute-start(s32[256]{0:T(256)S(1)} %bitcast.68), channel_id=1, source_target_pairs={{0,16},{8,24},{16,0},{24,8},{1,17},{9,25},{17,1},{25,9},{2,18},{10... | collective-permute-start | bytes 3080 | tf_op jit(solution)/shard_map/ppermute | solution.py:41
  50.9 3.6 %collective-permute-start.6 = (s32[256]{0:T(256)S(1)}, s32[256]{0:T(256)S(1)}, u32[]{:S(2)}, u32[]{:S(2)}) collective-permute-start(s32[256]{0:T(256)S(1)} %bitcast.69), channel_id=1, source_target_pairs={{0,8},{8,0},{16,24},{24,16},{1,9},{9,1},{17,25},{25,17},{2,10},{10... | collective-permute-start | bytes 3080 | tf_op jit(solution)/shard_map/ppermute | solution.py:41
  54.5 3.9 %copy-start.4 = (bf16[256,1536]{1,0:T(8,128)(2,1)}, bf16[256,1536]{1,0:T(8,128)(2,1)S(1)}, u32[]{:S(2)}) copy-start(bf16[256,1536]{1,0:T(8,128)(2,1)S(1)} %collective-permute-done.5) | copy-start | bytes 2359300
  64.1 4.0 %slice-start = ((bf16[256,1536]{1,0:T(8,128)(2,1)}), bf16[256,768]{1,0:T(8,128)(2,1)S(1)}, s32[]{:S(2)}) async-start(bf16[256,1536]{1,0:T(8,128)(2,1)} %copy-done.4), calls=%async_computation.4 | async-start | bytes 786432 | tf_op jit(solution)/shard_map/slice | solution.py:62
  72.8 2.3 %copy-start.3 = (bf16[4,256,768]{2,1,0:T(8,128)(2,1)S(1)}, bf16[4,256,768]{2,1,0:T(8,128)(2,1)}, u32[]{:S(2)}) copy-start(bf16[4,256,768]{2,1,0:T(8,128)(2,1)} %copy-done.2) | copy-start | bytes 4718596
  75.0 2.2 %copy-start.5 = (bf16[256,1536]{1,0:T(8,128)(2,1)S(1)}, bf16[256,1536]{1,0:T(8,128)(2,1)}, u32[]{:S(2)}) copy-start(bf16[256,1536]{1,0:T(8,128)(2,1)} %copy-done.4) | copy-start | bytes 2359300
  75.0 70.6 %reduce-scatter.2.cloned.1.call-start = ((), (), s32[]{:S(2)}) async-start(), calls=%async_computation.3 | async-start | bytes 2654208 | tf_op jit(solution)/shard_map/reduce_scatter | solution.py:110
  109.2 3.9 %copy-start.7 = (s32[256]{0:T(256)S(1)}, s32[256]{0:T(256)}, u32[]{:S(2)}) copy-start(s32[256]{0:T(256)} %iota_add_fusion.3) | copy-start | bytes 3076
  109.3 19.3 %collective-permute-start.1 = (bf16[256,768]{1,0:T(8,128)(2,1)S(1)}, bf16[256,768]{1,0:T(8,128)(2,1)S(1)}, u32[]{:S(2)}, u32[]{:S(2)}) collective-permute-start(bf16[256,768]{1,0:T(8,128)(2,1)S(1)} %multiply_convert_fusion.1), channel_id=1, source_target_pairs={{0,16},{8,24},{16,0},{24,8},{1,17},{9,25},{17,1},{25,9},{2,18},{10... | collective-permute-start | bytes 1179656 | tf_op jit(solution)/shard_map/ppermute | solution.py:41
  110.8 18.1 %collective-permute-start.2 = (bf16[256,768]{1,0:T(8,128)(2,1)S(1)}, bf16[256,768]{1,0:T(8,128)(2,1)S(1)}, u32[]{:S(2)}, u32[]{:S(2)}) collective-permute-start(bf16[256,768]{1,0:T(8,128)(2,1)S(1)} %multiply_convert_fusion.1), channel_id=1, source_target_pairs={{0,24},{8,16},{16,8},{24,0},{1,25},{9,17},{17,9},{25,1},{2,26},{10... | collective-permute-start | bytes 1179656 | tf_op jit(solution)/shard_map/ppermute | solution.py:41
  112.3 17.6 %collective-permute-start = (bf16[256,768]{1,0:T(8,128)(2,1)S(1)}, bf16[256,768]{1,0:T(8,128)(2,1)S(1)}, u32[]{:S(2)}, u32[]{:S(2)}) collective-permute-start(bf16[256,768]{1,0:T(8,128)(2,1)S(1)} %multiply_convert_fusion.1), channel_id=1, source_target_pairs={{0,8},{8,0},{16,24},{24,16},{1,9},{9,1},{17,25},{25,17},{2,10},{10... | collective-permute-start | bytes 1179656 | tf_op jit(solution)/shard_map/ppermute | solution.py:41
Sparse Core Ops, SparseCore 0:
  9.6 54.3 all-gather.2
  75.1 29.7 all-gather.4
  109.4 36.2 reduce-scatter.1

commit v12 on v8

--- a/solution.py
+++ b/solution.py
@@ -81,6 +81,7 @@
     groups = lax.axis_size("group")
     parity = lax.axis_index("group") % 2
     owner_rows = chunk // groups
+    mate_pairs = [(g, g ^ 1) for g in range(groups)]
     by_owner = hidden_group.reshape(hidden_group.shape[0], groups // 2, 2, owner_rows)
     hidden_keep = lax.dynamic_index_in_dim(by_owner, parity, 2, keepdims=False).reshape(
         hidden_group.shape[0], chunk // 2
@@ -88,6 +89,7 @@
     hidden_give = lax.dynamic_index_in_dim(by_owner, 1 - parity, 2, keepdims=False).reshape(
         hidden_group.shape[0], chunk // 2
     )
+    hidden_mate = lax.ppermute(hidden_give, "group", mate_pairs)
     own_columns = my_index * row_count + local
     scores_t = lax.dot_general(
         image_group, text_unit, (((1,), (1,)), ((), ())), preferred_element_type=jnp.float32
@@ -106,21 +108,23 @@
         text_scale
         * (text_unit_grad - text_dir * jnp.sum(text_dir * text_unit_grad, axis=1, keepdims=True))
     ).astype(jnp.bfloat16)
-    grad_from = [projection_output_gradient] + [
-        exchange(projection_output_gradient, k) for k in range(1, blocks)
-    ]
+    grad_send, hidden_keep, hidden_mate = lax.optimization_barrier(
+        (projection_output_gradient, hidden_keep, hidden_mate)
+    )
+    grad_from = [projection_output_gradient] + [exchange(grad_send, k) for k in range(1, blocks)]
     grad_group = jnp.concatenate(grad_from, axis=0)
-
-    def rows_for(hidden_part):
-        return lax.dot_general(
-            hidden_part, grad_group, (((0,), (0,)), ((), ())), preferred_element_type=jnp.float32
-        ).reshape(groups // 2, owner_rows, grad_group.shape[1])
-    mate_pairs = [(g, g ^ 1) for g in range(groups)]
-    incoming = lax.ppermute(rows_for(hidden_give), "group", mate_pairs)
-    chip_sum = rows_for(hidden_keep) + incoming
+    grad_mate = lax.ppermute(grad_group, "group", mate_pairs)
+    contract_rows = (((0,), (0,)), ((), ()))
+    chip_sum = lax.dot_general(
+        hidden_keep, grad_group, contract_rows, preferred_element_type=jnp.float32
+    ) + lax.dot_general(hidden_mate, grad_mate, contract_rows, preferred_element_type=jnp.float32)
     same_core = [list(range(p, groups, 2)) for p in range(2)]
     projection_grad = lax.psum_scatter(
-        chip_sum, "group", scatter_dimension=0, axis_index_groups=same_core, tiled=True
+        chip_sum.reshape(groups // 2, owner_rows, grad_group.shape[1]),
+        "group",
+        scatter_dimension=0,
+        axis_index_groups=same_core,
+        tiled=True,
     ).reshape(owner_rows, grad_group.shape[1])
 
     loss_local = jnp.zeros((row_count,), jnp.float32)

time: 143 us -> 139 us (0.972)
  matrix products: 22.9 us -> 20.5 us
  other arithmetic: 8 us -> 5.84 us
  local copies, waits for them, and re-layouts: 6.12 us -> 7.81 us
    slice x3 -> x0, local copies, waits for them, and re-layouts: 3.13 us -> none  [body(): image_from.append(incoming[:, chunk:])]
    slice x3 -> x6, local copies, waits for them, and re-layouts: 1.25 us -> 4.01 us  [body(): hidden_from.append(incoming[:, :chunk])]
    all_gather x1, waiting for transfers between devices: 7.07 us -> 4.59 us  [body(): w_full = lax.all_gather(linear_map_matrix, 'group', axis=0, tiled=True)]
    dot_general x2, matrix products: 6.72 us -> 4.39 us  [the longest x1 2.55 us: body(): lax.dot_general(hidden_mate, grad_mate, contract_rows, preferred_element_...]
  transfers between devices with their start and end apart: 15 -> 16, of which waited for: 9 -> 9; matrix products, arithmetic and copies ran while one was open for 16% -> 24% of each run, Pallas kernels for 0% -> 0%
where the time goes in v12:
time: 139 us
  waiting for transfers between devices  72.3 us (52%)
  matrix products  20.5 us (15%)
  starting transfers between devices  16.4 us (12%)
  between operations  15.7 us (11%)
  local copies, waits for them, and re-layouts  7.81 us (6%)
  other arithmetic  5.84 us (4%)
    ppermute x12, waiting for transfers between devices, exchange(): return lax.ppermute(value, 'blk', partner_pairs(blocks, step))  58.2 us
    ppermute x12, starting transfers between devices, exchange(): return lax.ppermute(value, 'blk', partner_pairs(blocks, step))  16.3 us
    reduce_scatter x1, waiting for transfers between devices, body(): lax.psum_scatter(chip_sum.reshape(groups // 2, owner_rows, grad_group.sha...  8.81 us
    all_gather x1, waiting for transfers between devices, body(): w_full = lax.all_gather(linear_map_matrix, 'group', axis=0, tiled=True)  4.59 us
    dot_general x4, matrix products, body(): lax.dot_general(image_unit, text_from[k], (((1,), (1,)), ((), ())), prefe...  4.56 us
    slice x6, local copies, waits for them, and re-layouts, body(): hidden_from.append(incoming[:, :chunk])  4.01 us
    dot_general x4, matrix products, body(): jnp.dot(weights_of(logits, pair_sign), text_from[k], preferred_element_ty...  3.87 us
    dot_general x1, matrix products, body(): lax.dot_general(weights_of(logits_t, pair_sign_t), image_group, (((0,), (...  3.86 us
  transfers between devices with their start and end apart: 16, of which 9 were waited for; matrix products, arithmetic and copies ran while one was open for 24% of the time, Pallas kernels for 0%

profile of v12, /device:TPU:0, one launch (start us, length us, event | category | flops | bytes accessed | tf_op | source)
XLA Modules:
  0.0 138.6 jit_solution(15652032161196442577)
XLA Ops:
  7.2 0.0 all-gather.2.cloned.1.call-start
  7.2 0.7 all-gather.2.cloned.1.call-update
  7.9 0.0 reduce-scatter.2.cloned.1.call-start
  8.0 1.5 %constant_dynamic-slice_fusion.2 = (bf16[1,256,768]{2,1,0:T(8,128)(2,1)S(1)}, bf16[256,768]{1,0:T(8,128)(2,1)S(1)}, bf16[256,768]{1,0:T(8,128)(2,1)S(1)}, bf16[256,768]{1,0:T(8,128)(2,1)S(1)}) fusion(bf16[1,256,3072]{2,1,0:T(8,128)(2,1)} %param.7, s32[]{:T(128)S(6)} %select_n.69, s32[]{:T(128)S(6)} %select_n.67, s32[]{:T(128)S(6)} %select_n.66, s32[]{:T(128)S(6)} %select_n.68), kind=kLoop, calls=%fused_computation.135 | loop fusion | bytes 3145744 | tf_op jit(solution)/shard_map/dynamic_slice | solution.py:51
  9.5 0.2 fusion.27
  9.7 0.1 fusion.22
  9.8 0.0 copy-start.11
  9.8 1.5 %pad_maximum_fusion.7 = (bf16[256,1536]{1,0:T(8,128)(2,1)}, bf16[256,1536]{1,0:T(8,128)(2,1)}, bf16[256,1536]{1,0:T(8,128)(2,1)}) fusion(bf16[256,768]{1,0:T(8,128)(2,1)S(1)} %fusion.22, bf16[256,768]{1,0:T(8,128)(2,1)S(1)} %get-tuple-element.17, bf16[256,768]{1,0:T(8,128)(2,1)S(1)} %get-tuple-element.16, bf16[256,768]{1,0:T(8,128)(2,1)S(1)} %get-tuple-element.18), kind=kLoop, calls=%fused_computation.33 | loop fusion | flops 3932160 | bytes 3932160 | tf_op jit(solution)/shard_map/concatenate | solution.py:57
  11.4 2.9 %collective-permute-start.6 = (bf16[256,1536]{1,0:T(8,128)(2,1)}, bf16[256,1536]{1,0:T(8,128)(2,1)S(1)}, u32[]{:S(2)}, u32[]{:S(2)}) collective-permute-start(bf16[256,1536]{1,0:T(8,128)(2,1)} %get-tuple-element.25), channel_id=1, source_target_pairs={{0,8},{8,0},{16,24},{24,16},{1,9},{9,1},{17,25},{25,17},{2,10},{10... | collective-permute-start | bytes 2359304 | tf_op jit(solution)/shard_map/ppermute | solution.py:41
  14.3 1.5 %collective-permute-start.7 = (bf16[256,1536]{1,0:T(8,128)(2,1)}, bf16[256,1536]{1,0:T(8,128)(2,1)}, u32[]{:S(2)}, u32[]{:S(2)}) collective-permute-start(bf16[256,1536]{1,0:T(8,128)(2,1)} %get-tuple-element.26), channel_id=1, source_target_pairs={{0,16},{8,24},{16,0},{24,8},{1,17},{9,25},{17,1},{25,9},{2,18},{10... | collective-permute-start | bytes 2359304 | tf_op jit(solution)/shard_map/ppermute | solution.py:41
  15.8 0.0 collective-permute-start.8
  15.8 2.9 %collective-permute-start.5 = (s32[256]{0:T(256)S(1)}, s32[256]{0:T(256)S(1)}, u32[]{:S(2)}, u32[]{:S(2)}) collective-permute-start(s32[256]{0:T(256)S(1)} %bitcast.68), channel_id=1, source_target_pairs={{0,24},{8,16},{16,8},{24,0},{1,25},{9,17},{17,9},{25,1},{2,26},{10... | collective-permute-start | bytes 3080 | tf_op jit(solution)/shard_map/ppermute | solution.py:41
  18.8 0.5 collective-permute-start.4
  19.3 0.6 iota_add_fusion.3
  19.9 30.4 %collective-permute-done.5 = s32[256]{0:T(256)S(1)} collective-permute-done((s32[256]{0:T(256)S(1)}, s32[256]{0:T(256)S(1)}, u32[]{:S(2)}, u32[]{:S(2)}) %collective-permute-start.5) | collective-permute-done | bytes 1056 | tf_op jit(solution)/shard_map/ppermute | solution.py:41
  50.3 1.4 %collective-permute-start.3 = (s32[256]{0:T(256)S(1)}, s32[256]{0:T(256)S(1)}, u32[]{:S(2)}, u32[]{:S(2)}) collective-permute-start(s32[256]{0:T(256)S(1)} %bitcast.70), channel_id=1, source_target_pairs={{0,8},{8,0},{16,24},{24,16},{1,9},{9,1},{17,25},{25,17},{2,10},{10... | collective-permute-start | bytes 3080 | tf_op jit(solution)/shard_map/ppermute | solution.py:41
  53.0 0.2 copy.13
  53.2 0.0 collective-permute-done.4
  53.2 0.7 collective-permute-done.3
  53.9 0.8 fusion.113
  54.7 0.2 copy.10
  54.9 1.9 %fusion.114 = (bf16[256,768]{1,0:T(8,128)(2,1)S(1)}, bf16[256,768]{1,0:T(8,128)(2,1)}) fusion(bf16[256,1536]{1,0:T(8,128)(2,1)} %collective-permute-done.7), kind=kLoop, calls=%fused_computation.155 | loop fusion | bytes 1572864 | tf_op jit(solution)/shard_map/slice | solution.py:61
  56.8 0.2 copy.11
  57.0 0.8 fusion.115
  57.8 0.2 copy.12
  57.9 0.2 pad_maximum_fusion.1
  58.1 0.0 copy-start.1
  58.1 1.3 constant_dynamic-slice_fusion
  59.5 4.6 %all-gather.2.cloned.1.call-done = bf16[3072,768]{1,0:T(8,128)(2,1)} async-done(((bf16[384,768]{1,0:T(8,128)(2,1)}), bf16[3072,768]{1,0:T(8,128)(2,1)}) %all-gather.2.cloned.1.call-update) | async-done | bytes 4718608 | tf_op jit(solution)/shard_map/all_gather | solution.py:43
  64.1 3.8 %multiply_reduce_fusion.1 = (f32[256]{0:T(256)S(1)}, f32[256,768]{1,0:T(8,128)S(1)}) fusion(bf16[3072,768]{1,0:T(8,128)(2,1)} %all-gather.2.cloned.1.call-done, bf16[1,256,3072]{2,1,0:T(8,128)(2,1)S(1)} %copy-done.1), kind=kOutput, calls=%fused_computation.46 | convolution fusion | flops 1208352512 | bytes 7078912 | tf_op jit(solution)/shard_map/dot_general | solution.py:65
  67.9 0.1 multiply_convert_fusion.1
  68.0 3.9 %multiply_reduce_fusion = (f32[256]{0:T(256)}, f32[256,768]{1,0:T(8,128)S(1)}) fusion(f32[256,768]{1,0:T(8,128)S(1)} %get-tuple-element.29, f32[256]{0:T(256)S(1)} %add_rsqrt_fusion, bf16[256,768]{1,0:T(8,128)(2,1)} %get-tuple-element.24, bf16[256,768]{1,0:T(8,128)(2,1)} %get-tuple-element.22, bf16[256,768]{1,0:T(8,128)(2,1)S(1)} %copy-done.9, ...), kind=kOutput, calls=%fused_computation.45 | convolution fusion | flops 821624576 | bytes 3546120 | tf_op jit(solution)/shard_map/dot_general | solution.py:101
  71.9 0.9 multiply_convert_fusion
  72.8 2.4 %collective-permute-start.12 = (bf16[256,768]{1,0:T(8,128)(2,1)S(1)}, bf16[256,768]{1,0:T(8,128)(2,1)S(1)}, u32[]{:S(2)}, u32[]{:S(2)}) collective-permute-start(bf16[256,768]{1,0:T(8,128)(2,1)S(1)} %multiply_convert_fusion), channel_id=1, source_target_pairs={{0,24},{8,16},{16,8},{24,0},{1,25},{9,17},{17,9},{25,1},{2,26},{10... | collective-permute-start | bytes 1179656 | tf_op jit(solution)/shard_map/ppermute | solution.py:41
  75.2 0.6 collective-permute-start.11
  75.8 0.6 collective-permute-start.10
  76.3 9.4 %collective-permute-done.12 = bf16[256,768]{1,0:T(8,128)(2,1)S(1)} collective-permute-done((bf16[256,768]{1,0:T(8,128)(2,1)S(1)}, bf16[256,768]{1,0:T(8,128)(2,1)S(1)}, u32[]{:S(2)}, u32[]{:S(2)}) %collective-permute-start.12) | collective-permute-done | bytes 393248 | tf_op jit(solution)/shard_map/ppermute | solution.py:41
  85.7 7.7 %collective-permute-done.11 = bf16[256,768]{1,0:T(8,128)(2,1)S(1)} collective-permute-done((bf16[256,768]{1,0:T(8,128)(2,1)S(1)}, bf16[256,768]{1,0:T(8,128)(2,1)S(1)}, u32[]{:S(2)}, u32[]{:S(2)}) %collective-permute-start.11) | collective-permute-done | bytes 393248 | tf_op jit(solution)/shard_map/ppermute | solution.py:41
  93.4 0.1 collective-permute-done.10
  93.5 0.1 pad_maximum_fusion.2
  93.6 0.6 copy-done.5
  94.2 0.1 copy-done.7
  94.3 0.0 collective-permute-start.13
  94.3 0.6 iota_add_fusion
  94.9 1.7 %collective-permute-start.2 = (bf16[256,768]{1,0:T(8,128)(2,1)S(1)}, bf16[256,768]{1,0:T(8,128)(2,1)}, u32[]{:S(2)}, u32[]{:S(2)}) collective-permute-start(bf16[256,768]{1,0:T(8,128)(2,1)S(1)} %multiply_convert_fusion.1), channel_id=1, source_target_pairs={{0,24},{8,16},{16,8},{24,0},{1,25},{9,17},{17,9},{25,1},{2,26},{10... | collective-permute-start | bytes 1179656 | tf_op jit(solution)/shard_map/ppermute | solution.py:41
  96.6 1.2 collective-permute-start.1
  97.8 0.6 collective-permute-start
  98.4 1.0 fusion.12
  99.4 2.6 %fusion.116 = f32[384,768]{1,0:T(8,128)S(1)} fusion(bf16[1024,384]{0,1:T(8,128)(2,1)} %collective-permute-done.9, bf16[1024,768]{1,0:T(8,128)(2,1)} %collective-permute-done.13), kind=kOutput, calls=%fused_computation.157 | convolution fusion | flops 603979776 | bytes 3538944 | tf_op jit(solution)/shard_map/dot_general | solution.py:120
  102.0 1.8 %convolution_add_fusion = f32[384,768]{1,0:T(8,128)} fusion(f32[384,768]{1,0:T(8,128)S(1)} %fusion.116, bf16[1024,384]{0,1:T(8,128)(2,1)S(1)} %bitcast.67, bf16[256,768]{1,0:T(8,128)(2,1)S(1)} %copy-done.4, bf16[256,768]{1,0:T(8,128)(2,1)S(1)} %copy-done.6, bf16[256,768]{1,0:T(8,128)(2,1)S(1)} %copy-done.8, bf16[256,768]{1,0:T(8,128)(2,1)S(1)} %multiply_convert_fusion), kind=kOutput, calls=%fused_computation.5 | convolution fusion | flops 610566144 | bytes 4718592 | tf_op jit(solution)/shard_map/dot_general | solution.py:118
  103.9 0.0 reduce-scatter.2.cloned.1.call-update
  103.9 0.0 copy-start.12
  103.9 0.4 fusion.75
  104.4 3.5 %collective-permute-done.2 = bf16[256,768]{1,0:T(8,128)(2,1)} collective-permute-done((bf16[256,768]{1,0:T(8,128)(2,1)S(1)}, bf16[256,768]{1,0:T(8,128)(2,1)}, u32[]{:S(2)}, u32[]{:S(2)}) %collective-permute-start.2) | collective-permute-done | bytes 393248 | tf_op jit(solution)/shard_map/ppermute | solution.py:41
  107.8 1.4 fusion.15
  109.2 6.5 %collective-permute-done.1 = bf16[256,768]{1,0:T(8,128)(2,1)S(1)} collective-permute-done((bf16[256,768]{1,0:T(8,128)(2,1)S(1)}, bf16[256,768]{1,0:T(8,128)(2,1)S(1)}, u32[]{:S(2)}, u32[]{:S(2)}) %collective-permute-start.1) | collective-permute-done | bytes 393248 | tf_op jit(solution)/shard_map/ppermute | solution.py:41
  115.7 0.3 fusion.14
  116.0 1.9 %fusion.68 = (f32[256]{0:T(256)S(1)}, f32[256]{0:T(256)S(1)}, f32[256]{0:T(256)S(1)}, f32[256]{0:T(256)S(1)}, f32[256,256]{0,1:T(8,128)S(1)}) fusion(s32[256]{0:T(256)S(1)} %bitcast.73, s32[256]{0:T(256)S(1)} %iota_add_fusion.2, f32[256,256]{0,1:T(8,128)S(1)} %fusion.14, s32[256]{0:T(256)S(1)} %get-tuple-element.36, f32[256,256]{0,1:T(8,128)S(1)} %fusion.15, ...), kind=kOutput, calls=%fused_computation.103 | convolution fusion | flops 103676928 | bytes 1844232 | tf_op jit(solution)/shard_map/dot_general | solution.py:133
  117.9 0.6 add_add_fusion
  118.5 1.4 %fusion.79 = f32[256,768]{1,0:T(8,128)S(1)} fusion(bf16[256,768]{1,0:T(8,128)(2,1)} %collective-permute-done.2, f32[256,256]{0,1:T(8,128)S(1)} %fusion.15, f32[]{:T(128)} %bitcast.50, s32[256]{0:T(256)S(1)} %bitcast.74, s32[256]{0:T(256)S(1)} %copy-done.12), kind=kOutput, calls=%fused_computation.111 | convolution fusion | flops 101318656 | bytes 1443844 | tf_op jit(solution)/shard_map/dot_general | solution.py:142
  119.9 1.4 %convolution_add_fusion.2 = f32[256,768]{1,0:T(8,128)S(1)} fusion(f32[256,768]{1,0:T(8,128)S(1)} %fusion.75, bf16[256,768]{1,0:T(8,128)(2,1)} %collective-permute-done, f32[256,256]{0,1:T(8,128)S(1)} %get-tuple-element.30, f32[]{:T(128)} %bitcast.52, s32[256]{0:T(256)S(1)} %bitcast.75, s32[256]{0:T(256)S(1)} %iota_add_fusion.2), kind=kOutput, calls=%fused_computation.18 | convolution fusion | flops 101515264 | bytes 2230276 | tf_op jit(solution)/shard_map/dot_general | solution.py:142
  121.4 0.5 fusion.23
  121.9 1.0 fusion.34
  122.9 8.8 %reduce-scatter.2.cloned.1.call-done = f32[1,96,768]{2,1,0:T(8,128)} async-done(((f32[4,96,768]{2,1,0:T(8,128)}), f32[1,96,768]{2,1,0:T(8,128)}) %reduce-scatter.2.cloned.1.call-update) | async-done | bytes 294928 | tf_op jit(solution)/shard_map/reduce_scatter | solution.py:122
  (34 shorter events, 0.1 us)
Async XLA Ops:
  7.2 56.9 %all-gather.2.cloned.1.call-start = ((), (), s32[]{:S(2)}) async-start(), calls=%async_computation.1 | async-start | bytes 5308416 | tf_op jit(solution)/shard_map/all_gather | solution.py:43
  7.9 123.8 %reduce-scatter.2.cloned.1.call-start = ((), (), s32[]{:S(2)}) async-start(), calls=%async_computation.2 | async-start | bytes 1474560 | tf_op jit(solution)/shard_map/reduce_scatter | solution.py:122
  8.0 1.5 %copy-start = (bf16[1,256,768]{2,1,0:T(8,128)(2,1)S(1)}, bf16[1,256,768]{2,1,0:T(8,128)(2,1)}, u32[]{:S(2)}) copy-start(bf16[1,256,768]{2,1,0:T(8,128)(2,1)} %param.6) | copy-start | bytes 1179652
  9.8 6.0 %copy-start.11 = (s32[1,256]{1,0:T(1,128)S(1)}, s32[1,256]{1,0:T(1,128)}, u32[]{:S(2)}) copy-start(s32[1,256]{1,0:T(1,128)} %param.9) | copy-start | bytes 3076
  11.4 42.5 %collective-permute-start.6 = (bf16[256,1536]{1,0:T(8,128)(2,1)}, bf16[256,1536]{1,0:T(8,128)(2,1)S(1)}, u32[]{:S(2)}, u32[]{:S(2)}) collective-permute-start(bf16[256,1536]{1,0:T(8,128)(2,1)} %get-tuple-element.25), channel_id=1, source_target_pairs={{0,8},{8,0},{16,24},{24,16},{1,9},{9,1},{17,25},{25,17},{2,10},{10... | collective-permute-start | bytes 2359304 | tf_op jit(solution)/shard_map/ppermute | solution.py:41
  14.3 40.5 %collective-permute-start.7 = (bf16[256,1536]{1,0:T(8,128)(2,1)}, bf16[256,1536]{1,0:T(8,128)(2,1)}, u32[]{:S(2)}, u32[]{:S(2)}) collective-permute-start(bf16[256,1536]{1,0:T(8,128)(2,1)} %get-tuple-element.26), channel_id=1, source_target_pairs={{0,16},{8,24},{16,0},{24,8},{1,17},{9,25},{17,1},{25,9},{2,18},{10... | collective-permute-start | bytes 2359304 | tf_op jit(solution)/shard_map/ppermute | solution.py:41
  15.8 41.1 %collective-permute-start.8 = (bf16[256,1536]{1,0:T(8,128)(2,1)}, bf16[256,1536]{1,0:T(8,128)(2,1)S(1)}, u32[]{:S(2)}, u32[]{:S(2)}) collective-permute-start(bf16[256,1536]{1,0:T(8,128)(2,1)} %get-tuple-element.27), channel_id=1, source_target_pairs={{0,24},{8,16},{16,8},{24,0},{1,25},{9,17},{17,9},{25,1},{2,26},{10... | collective-permute-start | bytes 2359304 | tf_op jit(solution)/shard_map/ppermute | solution.py:41
  15.8 34.4 %collective-permute-start.5 = (s32[256]{0:T(256)S(1)}, s32[256]{0:T(256)S(1)}, u32[]{:S(2)}, u32[]{:S(2)}) collective-permute-start(s32[256]{0:T(256)S(1)} %bitcast.68), channel_id=1, source_target_pairs={{0,24},{8,16},{16,8},{24,0},{1,25},{9,17},{17,9},{25,1},{2,26},{10... | collective-permute-start | bytes 3080 | tf_op jit(solution)/shard_map/ppermute | solution.py:41
  18.8 34.4 %collective-permute-start.4 = (s32[256]{0:T(256)S(1)}, s32[256]{0:T(256)S(1)}, u32[]{:S(2)}, u32[]{:S(2)}) collective-permute-start(s32[256]{0:T(256)S(1)} %bitcast.69), channel_id=1, source_target_pairs={{0,16},{8,24},{16,0},{24,8},{1,17},{9,25},{17,1},{25,9},{2,18},{10... | collective-permute-start | bytes 3080 | tf_op jit(solution)/shard_map/ppermute | solution.py:41
  50.3 3.6 %collective-permute-start.3 = (s32[256]{0:T(256)S(1)}, s32[256]{0:T(256)S(1)}, u32[]{:S(2)}, u32[]{:S(2)}) collective-permute-start(s32[256]{0:T(256)S(1)} %bitcast.70), channel_id=1, source_target_pairs={{0,8},{8,0},{16,24},{24,16},{1,9},{9,1},{17,25},{25,17},{2,10},{10... | collective-permute-start | bytes 3080 | tf_op jit(solution)/shard_map/ppermute | solution.py:41
  58.1 6.0 %copy-start.1 = (bf16[1,256,3072]{2,1,0:T(8,128)(2,1)S(1)}, bf16[1,256,3072]{2,1,0:T(8,128)(2,1)}, u32[]{:S(2)}) copy-start(bf16[1,256,3072]{2,1,0:T(8,128)(2,1)} %param.7) | copy-start | bytes 4718596
  59.5 8.5 %copy-start.9 = (bf16[256,768]{1,0:T(8,128)(2,1)S(1)}, bf16[256,768]{1,0:T(8,128)(2,1)}, u32[]{:S(2)}) copy-start(bf16[256,768]{1,0:T(8,128)(2,1)} %get-tuple-element.20) | copy-start | bytes 1179652
  59.5 13.3 %collective-permute-start.9 = (bf16[1024,384]{0,1:T(8,128)(2,1)}, bf16[1024,384]{0,1:T(8,128)(2,1)}, u32[]{:S(2)}, u32[]{:S(2)}) collective-permute-start(bf16[1024,384]{0,1:T(8,128)(2,1)} %bitcast.16), channel_id=1, source_target_pairs={{0,1},{1,0},{2,3},{3,2},{4,5},{5,4},{6,7},{7,6},{8,9},{9,8},{10,11... | collective-permute-start | bytes 2359304 | tf_op jit(solution)/shard_map/ppermute | solution.py:92
  72.8 13.0 %collective-permute-start.12 = (bf16[256,768]{1,0:T(8,128)(2,1)S(1)}, bf16[256,768]{1,0:T(8,128)(2,1)S(1)}, u32[]{:S(2)}, u32[]{:S(2)}) collective-permute-start(bf16[256,768]{1,0:T(8,128)(2,1)S(1)} %multiply_convert_fusion), channel_id=1, source_target_pairs={{0,24},{8,16},{16,8},{24,0},{1,25},{9,17},{17,9},{25,1},{2,26},{10... | collective-permute-start | bytes 1179656 | tf_op jit(solution)/shard_map/ppermute | solution.py:41
  75.2 18.2 %collective-permute-start.11 = (bf16[256,768]{1,0:T(8,128)(2,1)S(1)}, bf16[256,768]{1,0:T(8,128)(2,1)S(1)}, u32[]{:S(2)}, u32[]{:S(2)}) collective-permute-start(bf16[256,768]{1,0:T(8,128)(2,1)S(1)} %multiply_convert_fusion), channel_id=1, source_target_pairs={{0,16},{8,24},{16,0},{24,8},{1,17},{9,25},{17,1},{25,9},{2,18},{10... | collective-permute-start | bytes 1179656 | tf_op jit(solution)/shard_map/ppermute | solution.py:41
  75.8 17.7 %collective-permute-start.10 = (bf16[256,768]{1,0:T(8,128)(2,1)S(1)}, bf16[256,768]{1,0:T(8,128)(2,1)S(1)}, u32[]{:S(2)}, u32[]{:S(2)}) collective-permute-start(bf16[256,768]{1,0:T(8,128)(2,1)S(1)} %multiply_convert_fusion), channel_id=1, source_target_pairs={{0,8},{8,0},{16,24},{24,16},{1,9},{9,1},{17,25},{25,17},{2,10},{10... | collective-permute-start | bytes 1179656 | tf_op jit(solution)/shard_map/ppermute | solution.py:41
  85.7 7.8 %copy-start.3 = (bf16[256,768]{1,0:T(8,128)(2,1)}, bf16[256,768]{1,0:T(8,128)(2,1)S(1)}, u32[]{:S(2)}) copy-start(bf16[256,768]{1,0:T(8,128)(2,1)S(1)} %collective-permute-done.12) | copy-start | bytes 1179652
  93.4 0.8 copy-start.5
  93.5 0.8 copy-start.7
  94.3 5.1 %collective-permute-start.13 = (bf16[1024,768]{1,0:T(8,128)(2,1)S(1)}, bf16[1024,768]{1,0:T(8,128)(2,1)}, u32[]{:S(2)}, u32[]{:S(2)}) collective-permute-start(bf16[1024,768]{1,0:T(8,128)(2,1)S(1)} %pad_maximum_fusion.2), channel_id=1, source_target_pairs={{0,1},{1,0},{2,3},{3,2},{4,5},{5,4},{6,7},{7,6},{8,9},{9,8},{10,11... | collective-permute-start | bytes 4718600 | tf_op jit(solution)/shard_map/ppermute | solution.py:116
  94.9 13.0 %collective-permute-start.2 = (bf16[256,768]{1,0:T(8,128)(2,1)S(1)}, bf16[256,768]{1,0:T(8,128)(2,1)}, u32[]{:S(2)}, u32[]{:S(2)}) collective-permute-start(bf16[256,768]{1,0:T(8,128)(2,1)S(1)} %multiply_convert_fusion.1), channel_id=1, source_target_pairs={{0,24},{8,16},{16,8},{24,0},{1,25},{9,17},{17,9},{25,1},{2,26},{10... | collective-permute-start | bytes 1179656 | tf_op jit(solution)/shard_map/ppermute | solution.py:41
  96.6 19.1 %collective-permute-start.1 = (bf16[256,768]{1,0:T(8,128)(2,1)S(1)}, bf16[256,768]{1,0:T(8,128)(2,1)S(1)}, u32[]{:S(2)}, u32[]{:S(2)}) collective-permute-start(bf16[256,768]{1,0:T(8,128)(2,1)S(1)} %multiply_convert_fusion.1), channel_id=1, source_target_pairs={{0,16},{8,24},{16,0},{24,8},{1,17},{9,25},{17,1},{25,9},{2,18},{10... | collective-permute-start | bytes 1179656 | tf_op jit(solution)/shard_map/ppermute | solution.py:41
  97.8 18.2 %collective-permute-start = (bf16[256,768]{1,0:T(8,128)(2,1)S(1)}, bf16[256,768]{1,0:T(8,128)(2,1)}, u32[]{:S(2)}, u32[]{:S(2)}) collective-permute-start(bf16[256,768]{1,0:T(8,128)(2,1)S(1)} %multiply_convert_fusion.1), channel_id=1, source_target_pairs={{0,8},{8,0},{16,24},{24,16},{1,9},{9,1},{17,25},{25,17},{2,10},{10... | collective-permute-start | bytes 1179656 | tf_op jit(solution)/shard_map/ppermute | solution.py:41
  99.4 2.6 %copy-start.2 = (bf16[1024,4,1,96]{0,3,2,1:T(8,128)(2,1)S(1)}, bf16[1024,4,1,96]{0,3,2,1:T(8,128)(2,1)}, u32[]{:S(2)}) copy-start(bf16[1024,4,1,96]{0,3,2,1:T(8,128)(2,1)} %get-tuple-element.14) | copy-start | bytes 2359300
  99.4 2.6 %copy-start.4 = (bf16[256,768]{1,0:T(8,128)(2,1)S(1)}, bf16[256,768]{1,0:T(8,128)(2,1)}, u32[]{:S(2)}) copy-start(bf16[256,768]{1,0:T(8,128)(2,1)} %copy-done.3) | copy-start | bytes 1179652
  99.4 2.6 %copy-start.6 = (bf16[256,768]{1,0:T(8,128)(2,1)S(1)}, bf16[256,768]{1,0:T(8,128)(2,1)}, u32[]{:S(2)}) copy-start(bf16[256,768]{1,0:T(8,128)(2,1)} %copy-done.5) | copy-start | bytes 1179652
  99.4 2.6 %copy-start.8 = (bf16[256,768]{1,0:T(8,128)(2,1)S(1)}, bf16[256,768]{1,0:T(8,128)(2,1)}, u32[]{:S(2)}) copy-start(bf16[256,768]{1,0:T(8,128)(2,1)} %copy-done.7) | copy-start | bytes 1179652
  102.0 1.9 %copy-start.10 = (f32[256,256]{0,1:T(8,128)S(1)}, f32[256,256]{0,1:T(8,128)}, u32[]{:S(2)}) copy-start(f32[256,256]{0,1:T(8,128)} %fusion.12) | copy-start | bytes 786436
  102.0 1.9 %copy-start.13 = (s32[256]{0:T(256)S(1)}, s32[256]{0:T(256)}, u32[]{:S(2)}) copy-start(s32[256]{0:T(256)} %iota_add_fusion.3) | copy-start | bytes 3076
  103.9 12.1 %copy-start.12 = (s32[256]{0:T(256)S(1)}, s32[256]{0:T(256)}, u32[]{:S(2)}) copy-start(s32[256]{0:T(256)} %get-tuple-element.35) | copy-start | bytes 3076
Sparse Core Ops, SparseCore 0:
  9.6 54.3 all-gather.1
  104.0 27.6 reduce-scatter.1
